TPU v7x, 256 devices: a whole 4x4x8 slice. The times are simulated.
256 devices in a mesh: space: 32 (over z_hi, x, core), scen: 8 (over y, z_lo).
Axes of the slice: x: 4, y: 4, z: 8 (z_hi: 4, z_lo: 2; z = z_hi * 2 + z_lo), core: 2. Of those that a mesh axis runs over, the one named last changes fastest.
Arguments:
- concentration: float32 [8, 8, 6, 384, 384], P('scen', None, None, 'space'), may hold values from -6 to 6
- emissions: float32 [8, 6, 384, 384], P('scen', None, 'space'), may hold values from -3 to 3
- courant: float32 [2, 8, 6, 384, 384], P(None, None, None, 'space'), may hold values from -0.9 to 0.9
- tile_source: int32 [8640], P('space'), may hold values from 0 to 215, as said below
- tile_target: int32 [8640], P('space'), may hold values from 0 to 1023, as said below
- intersection: bfloat16 [8640, 128, 128], P('space'), may hold values from 0 to 0.0625
Outputs:
- transported: float32 [8, 8, 6, 384, 384], P('scen', None, None, 'space')
- regridded: float32 [8, 8, 1024, 128], P('scen', None, 'space')
- ensemble_moments: float32 [2, 8, 1024, 128], P(None, None, 'space')
Inputs may be any that keep to these rules, and one draw needn't show every extreme that they name: `tile_source`: every source block of a row band is named by at least one of the band's tiles. `tile_target`: latitude band b holds target blocks b * 32 to (b+1) * 32 - 1. The 270 tiles of one row band name at most 16 blocks of any one latitude band and at least 8 of every latitude band but one, which receives exactly 16 tiles from every row band. Every target block is named by some tile.
All inputs are finite; a program needn't handle non-finite values.
Results may differ from a plain program's by a relative error of at most 0.0027.
Values sent between devices are 32-bit elements; how exact they have to be, the bound alone decides.
No kernel may reach another device: no remote copies, remote signals or barrier semaphores. Data moves between devices by JAX's collectives and lax.ppermute only.
A program may use at most 128 MiB of HBM per device.

v0:
```python
import jax
import jax.numpy as jnp
from jax import lax
from jax.sharding import PartitionSpec as P

TGT_DEV = 32
SLOTS = 16


def from_behind(block, axis, distance):
    devices = range(lax.axis_size(axis))
    route = [((i - distance) % len(devices), i) for i in devices]
    return lax.ppermute(block, axis, route)


def parabola_sweep(padded, courant_faces, sweep_axis):
    cells_along = padded.shape[sweep_axis] - 6

    def window(values_in, first_cell, length):
        return lax.slice_in_dim(values_in, first_cell, first_cell + length, axis=sweep_axis)

    edge_values = 7.0 / 12.0 * (
        window(padded, 1, cells_along + 3) + window(padded, 2, cells_along + 3)
    ) - 1.0 / 12.0 * (window(padded, 0, cells_along + 3) + window(padded, 3, cells_along + 3))
    left_edge = window(edge_values, 0, cells_along + 2)
    right_edge = window(edge_values, 1, cells_along + 2)
    centre = window(padded, 2, cells_along + 2)
    slopes = right_edge - left_edge
    curvature = 6.0 * centre - 3.0 * (left_edge + right_edge)
    backward = -courant_faces
    upwind_left = courant_faces * (
        window(right_edge, 0, cells_along + 1)
        - 0.5
        * courant_faces
        * (
            window(slopes, 0, cells_along + 1)
            - (1.0 - 2.0 * courant_faces / 3.0) * window(curvature, 0, cells_along + 1)
        )
    )
    upwind_right = courant_faces * (
        window(left_edge, 1, cells_along + 1)
        + 0.5
        * backward
        * (
            window(slopes, 1, cells_along + 1)
            + (1.0 - 2.0 * backward / 3.0) * window(curvature, 1, cells_along + 1)
        )
    )
    fluxes = jnp.where(courant_faces >= 0.0, upwind_left, upwind_right)
    return window(padded, 3, cells_along) - (
        window(fluxes, 1, cells_along) - window(fluxes, 0, cells_along)
    )


def pack_rows(tracer, north_wind, lowest):
    row_count = tracer.shape[3]
    width_cells = tracer.shape[4]
    if lowest:
        layers = tracer[:, :, :, 0:3, :]
    else:
        layers = tracer[:, :, :, row_count - 3 :, :]
    parts = [layers.reshape(-1, width_cells)]
    if north_wind is not None:
        wind_row = north_wind[:, :, 0:1, :] if lowest else north_wind[:, :, row_count - 1 :, :]
        parts.append(wind_row.reshape(-1, width_cells))
    return jnp.concatenate(parts, 0)


def edge_rows(tracer, north_wind, position, band_count, with_wind):
    row_count = tracer.shape[3]
    width_cells = tracer.shape[4]
    top = [tracer[:, :, 0::2, row_count - 3 :, :].reshape(-1, width_cells)]
    low = [tracer[:, :, 1::2, 0:3, :].reshape(-1, width_cells)]
    if with_wind:
        top.append(north_wind[:, 0::2, row_count - 1, :].reshape(-1, width_cells))
        low.append(north_wind[:, 1::2, 0, :].reshape(-1, width_cells))
    top = jnp.concatenate(top, 0)
    low = jnp.concatenate(low, 0)
    send = jnp.where(position == band_count - 1, top, jnp.where(position == 0, low, 0.0))
    send = jnp.flip(send.T, 0).reshape(band_count, -1)
    got = lax.all_to_all(send, "space", 0, 0, tiled=True)
    count = top.shape[0]
    return got[band_count - 1].reshape(-1, count), got[0].reshape(-1, count)


def column_halos(tracer, east_wind, north_wind, position, band_count, edge_wind, faces_known):
    scenarios, levels, _, row_count, width_cells = tracer.shape
    top, low = edge_rows(tracer, north_wind, position, band_count, edge_wind is None)
    cells = scenarios * levels * 3 * 3
    top_layers = top[:, :cells].reshape(row_count, scenarios, levels, 3, 3)
    low_layers = low[:, :cells].reshape(row_count, scenarios, levels, 3, 3)
    if edge_wind is None:
        edge_wind = (
            top[:, cells:].reshape(row_count, levels, 3),
            low[:, cells:].reshape(row_count, levels, 3),
        )
    top_wind, low_wind = edge_wind
    west_faces, east_faces, west_speeds, east_speeds = [], [], [], []
    for face_number in range(6):
        half = face_number // 2
        if face_number % 2 == 0:
            west_cells = jnp.moveaxis(top_layers[:, :, :, (half - 1) % 3], 0, 2)
            west_speed = top_wind[:, :, (half - 1) % 3].T
            east_cells = tracer[:, :, (face_number + 1) % 6, :, 0:3]
            east_speed = east_wind[:, (face_number + 1) % 6, :, 0]
        else:
            west_cells = tracer[:, :, (face_number - 1) % 6, :, width_cells - 3 :]
            west_speed = east_wind[:, (face_number - 1) % 6, :, width_cells - 1]
            east_cells = jnp.moveaxis(low_layers[:, :, :, (half + 1) % 3], 0, 2)
            east_speed = low_wind[:, :, (half + 1) % 3].T
        west_faces.append(west_cells)
        east_faces.append(east_cells)
        west_speeds.append(west_speed)
        east_speeds.append(east_speed)
    padded = jnp.concatenate(
        [jnp.stack(west_faces, 2), tracer, jnp.stack(east_faces, 2)], -1
    )
    if faces_known is None:
        speeds = jnp.concatenate(
            [
                jnp.stack(west_speeds, 1)[..., None],
                east_wind,
                jnp.stack(east_speeds, 1)[..., None],
            ],
            -1,
        )
        faces_known = 0.5 * (speeds[..., :-1] + speeds[..., 1:])
    return (padded, faces_known, edge_wind)


def edge_columns(tracer, east_wind, position, band_count, with_wind):
    scenarios, levels, _, row_count, width_cells = tracer.shape
    to_top = [jnp.moveaxis(tracer[:, :, 0::2, :, 0:3], 3, 0).reshape(row_count, -1)]
    to_low = [jnp.moveaxis(tracer[:, :, 1::2, :, width_cells - 3 :], 3, 0).reshape(row_count, -1)]
    if with_wind:
        to_top.append(jnp.moveaxis(east_wind[:, 0::2, :, 0], 2, 0).reshape(row_count, -1))
        to_low.append(
            jnp.moveaxis(east_wind[:, 1::2, :, width_cells - 1], 2, 0).reshape(row_count, -1)
        )
    to_top = jnp.concatenate(to_top, 1)
    to_low = jnp.concatenate(to_low, 1)
    count = to_top.shape[1]
    send = jnp.zeros((band_count, row_count, count), to_top.dtype)
    send = send.at[band_count - 1].set(to_top).at[0].set(to_low)
    got = lax.all_to_all(send, "space", 0, 0, tiled=True)
    flipped = jnp.flip(got.reshape(-1, count), 0).T
    cells = scenarios * levels * 3 * 3
    layers = flipped[:cells].reshape(scenarios, levels, 3, 3, band_count * row_count)
    wind = None
    if with_wind:
        wind = flipped[cells:].reshape(levels, 3, band_count * row_count)
    return layers, wind


def row_halos(tracer, east_wind, north_wind, position, band_count, row_wind, faces_known):
    first_step = row_wind is None
    shifted = []
    for step_by, lowest in ((-1, True), (1, False)):
        packed = pack_rows(tracer, north_wind if first_step else None, lowest)
        shifted.append(from_behind(packed, "space", step_by))
    edge_layers, edge_speed = edge_columns(tracer, east_wind, position, band_count, first_step)
    layer_rows = tracer.shape[0] * tracer.shape[1] * 18
    width_cells = tracer.shape[4]
    if first_step:
        levels = tracer.shape[1]
        row_wind = tuple(
            packed[layer_rows:].reshape(levels, 6, width_cells) for packed in shifted
        ) + (edge_speed,)
    above_wind, below_wind, edge_speed = row_wind
    above_layers, below_layers = (
        packed[:layer_rows].reshape(tracer.shape[0], tracer.shape[1], 6, 3, width_cells)
        for packed in shifted
    )
    at_top = position == band_count - 1
    at_bottom = position == 0
    south_faces, north_faces, south_speeds, north_speeds = [], [], [], []
    for face_number in range(6):
        half = face_number // 2
        if face_number % 2 == 0:
            north_cells = jnp.where(
                at_top,
                edge_layers[:, :, (half + 1) % 3],
                above_layers[:, :, face_number],
            )
            north_speed = jnp.where(
                at_top,
                edge_speed[:, (half + 1) % 3],
                above_wind[:, face_number],
            )
            south_cells = jnp.where(
                at_bottom,
                below_layers[:, :, (face_number - 1) % 6],
                below_layers[:, :, face_number],
            )
            south_speed = jnp.where(
                at_bottom, below_wind[:, (face_number - 1) % 6], below_wind[:, face_number]
            )
        else:
            north_cells = jnp.where(
                at_top, above_layers[:, :, (face_number + 1) % 6], above_layers[:, :, face_number]
            )
            north_speed = jnp.where(
                at_top, above_wind[:, (face_number + 1) % 6], above_wind[:, face_number]
            )
            south_cells = jnp.where(
                at_bottom,
                edge_layers[:, :, (half - 1) % 3],
                below_layers[:, :, face_number],
            )
            south_speed = jnp.where(
                at_bottom,
                edge_speed[:, (half - 1) % 3],
                below_wind[:, face_number],
            )
        south_faces.append(south_cells)
        north_faces.append(north_cells)
        south_speeds.append(south_speed)
        north_speeds.append(north_speed)
    padded = jnp.concatenate(
        [jnp.stack(south_faces, 2), tracer, jnp.stack(north_faces, 2)], -2
    )
    if faces_known is None:
        speeds = jnp.concatenate(
            [
                jnp.stack(south_speeds, 1)[:, :, None, :],
                north_wind,
                jnp.stack(north_speeds, 1)[:, :, None, :],
            ],
            -2,
        )
        faces_known = 0.5 * (speeds[:, :, :-1, :] + speeds[:, :, 1:, :])
    return (padded, faces_known, row_wind)


def regrid(tracer, tile_source, tile_target, intersection, band_count):
    scenarios = tracer.shape[0]
    levels = tracer.shape[1]
    batch_rows = scenarios * levels
    block_cells = intersection.shape[1]
    blocks = tracer.astype(jnp.bfloat16).reshape(batch_rows, -1, block_cells)
    chosen = jnp.take(blocks, tile_source, axis=1)
    partial_value = jnp.einsum(
        "btk,tkc->tbc", chosen, intersection, preferred_element_type=jnp.float32
    )
    target_band = tile_target // TGT_DEV
    target_block = tile_target % TGT_DEV
    band_hot = (target_band[:, None] == jnp.arange(band_count)[None, :]).astype(jnp.int32)
    rank = jnp.sum((jnp.cumsum(band_hot, 0) - band_hot) * band_hot, 1)
    slot = jnp.where(rank < SLOTS, target_band * SLOTS + rank, -1)
    slot_hot = (slot[None, :] == jnp.arange(band_count * SLOTS)[:, None]).astype(jnp.float32)
    slotted = jnp.einsum(
        "st,tbc->sbc", slot_hot, partial_value, precision=lax.Precision.HIGHEST
    )
    slot_block = jnp.sum(slot_hot * target_block[None, :].astype(jnp.float32), 1)
    index_rows = jnp.zeros((band_count, 8, block_cells), jnp.float32)
    index_rows = index_rows.at[:, 0, :SLOTS].set(slot_block.reshape(band_count, SLOTS))
    send = jnp.concatenate(
        [slotted.reshape(band_count, SLOTS * batch_rows, block_cells), index_rows], 1
    )
    got = lax.all_to_all(send, "space", 0, 0, tiled=True)
    values = got[:, : SLOTS * batch_rows].reshape(band_count * SLOTS, batch_rows, block_cells)
    got_block = got[:, SLOTS * batch_rows, :SLOTS].reshape(-1)
    block_hot = (got_block[None, :] == jnp.arange(TGT_DEV)[:, None].astype(jnp.float32)).astype(
        jnp.float32
    )
    summed = jnp.einsum("ks,sbc->bkc", block_hot, values, precision=lax.Precision.HIGHEST)
    return summed.reshape(scenarios, levels, TGT_DEV, block_cells)


def moments_of(regridded):
    scenarios = regridded.shape[0]
    scen_count = lax.axis_size("scen")
    copies = jnp.broadcast_to(regridded, (scen_count,) + regridded.shape[1:])
    everyone = lax.all_to_all(copies, "scen", 0, 0, tiled=True)
    moment_sums = jnp.stack([jnp.sum(everyone, 0), jnp.sum(everyone * everyone, 0)])
    return moment_sums / (scenarios * scen_count)


def local(concentration, emissions, courant, tile_source, tile_target, intersection):
    band_count = lax.axis_size("space")
    position = lax.axis_index("space")
    tracer = concentration.at[:, 0].add(emissions)
    east_wind = courant[0]
    north_wind = courant[1]
    edge_wind = None
    row_wind = None
    cx = None
    cy = None
    for step_number in range(2):
        padded, cx, edge_wind = column_halos(
            tracer, east_wind, north_wind, position, band_count, edge_wind, cx
        )
        tracer = parabola_sweep(padded, cx, 4)
        padded, cy, row_wind = row_halos(
            tracer, east_wind, north_wind, position, band_count, row_wind, cy
        )
        tracer = parabola_sweep(padded, cy, 3)
    regridded = regrid(tracer, tile_source, tile_target, intersection, band_count)
    ensemble_moments = moments_of(regridded)
    return (tracer, regridded, ensemble_moments)


def solution(mesh):
    return jax.shard_map(
        local,
        mesh=mesh,
        in_specs=(
            P("scen", None, None, "space", None),
            P("scen", None, "space", None),
            P(None, None, None, "space", None),
            P("space"),
            P("space"),
            P("space", None, None),
        ),
        out_specs=(
            P("scen", None, None, "space", None),
            P("scen", None, "space", None),
            P(None, None, "space", None),
        ),
        check_vma=False,
    )
```

profile of v0, /device:TPU:2, one launch (start us, length us, event | category | flops | bytes accessed | tf_op | source)
XLA Modules:
  0.0 243.2 jit_solution(8800865998904568574)
XLA Ops:
  0.6 1.2 copy.1170
  2.0 1.1 scatter-add.4
  4.6 1.8 fusion.82
  8.5 1.4 reshape_squeeze.13
  10.0 1.4 copy.892
  11.4 1.4 reshape_squeeze.12
  12.8 1.7 fusion.68
  14.5 2.4 rev.14
  16.9 1.7 copy.895
  18.6 1.8 all_to_all.32
  20.4 11.7 %all-to-all-start = ((f32[32,1,1152]{2,1,0:T(1,128)}), f32[32,1,1152]{2,1,0:T(1,128)}, u32[]{:S(2)}, u32[]{:S(2)}) async-start(f32[32,1,1152]{2,1,0:T(1,128)} %all_to_all.32), calls=%async_computation | async-start | bytes 294912 | tf_op jit(solution)/shard_map/all_to_all | solution.py:81
  32.1 1.6 fusion.85
  50.2 1.1 copy.901
  57.1 1.4 fusion.18
  61.2 9.8 %all-to-all-start.1 = ((f32[32,12,96]{2,1,0:T(8,128)}), f32[32,12,96]{2,1,0:T(8,128)S(1)}, u32[]{:S(2)}, u32[]{:S(2)}) async-start(f32[32,12,96]{2,1,0:T(8,128)} %fusion.75), calls=%async_computation.1 | async-start | bytes 524288 | tf_op jit(solution)/shard_map/all_to_all | solution.py:145
  72.8 1.7 pad_maximum_fusion.5
  75.7 6.8 %all-to-all-done.1 = f32[32,12,96]{2,1,0:T(8,128)S(1)} async-done(((f32[32,12,96]{2,1,0:T(8,128)}), f32[32,12,96]{2,1,0:T(8,128)S(1)}, u32[]{:S(2)}, u32[]{:S(2)}) %all-to-all-start.1) | async-done | bytes 147488 | tf_op jit(solution)/shard_map/all_to_all | solution.py:145
  93.5 12.6 %all-to-all-start.2 = ((f32[32,1,864]{2,1,0:T(1,128)}), f32[32,1,864]{2,1,0:T(1,128)S(1)}, u32[]{:S(2)}, u32[]{:S(2)}) async-start(f32[32,1,864]{2,1,0:T(1,128)} %all_to_all.33), calls=%async_computation.2 | async-start | bytes 229376 | tf_op jit(solution)/shard_map/all_to_all | solution.py:81
  106.1 9.1 %all-to-all-done.2 = f32[32,1,864]{2,1,0:T(1,128)S(1)} async-done(((f32[32,1,864]{2,1,0:T(1,128)}), f32[32,1,864]{2,1,0:T(1,128)S(1)}, u32[]{:S(2)}, u32[]{:S(2)}) %all-to-all-start.2) | async-done | bytes 110624 | tf_op jit(solution)/shard_map/all_to_all | solution.py:81
  118.8 1.4 fusion.6
  121.3 2.2 scatter.21
  125.1 5.0 %all-to-all-start.3 = ((f32[32,1,864]{2,1,0:T(1,128)}), f32[32,1,864]{2,1,0:T(1,128)S(1)}, u32[]{:S(2)}, u32[]{:S(2)}) async-start(f32[32,1,864]{2,1,0:T(1,128)} %reshape.1058), calls=%async_computation.3 | async-start | bytes 229376 | tf_op jit(solution)/shard_map/all_to_all | solution.py:145
  130.8 1.9 collective-permute-start.3
  132.7 7.1 %all-to-all-done.3 = f32[32,1,864]{2,1,0:T(1,128)S(1)} async-done(((f32[32,1,864]{2,1,0:T(1,128)}), f32[32,1,864]{2,1,0:T(1,128)S(1)}, u32[]{:S(2)}, u32[]{:S(2)}) %all-to-all-start.3) | async-done | bytes 110624 | tf_op jit(solution)/shard_map/all_to_all | solution.py:145
  145.5 1.8 gather_fusion
  147.3 4.9 %fusion.62 = f32[270,8,128]{2,1,0:T(8,128)S(1)} fusion(bf16[270,128,128]{2,1,0:T(8,128)(2,1)} %param.23, bf16[270,8,128]{2,1,0:T(8,128)(2,1)S(1)} %gather_fusion, pred[270]{0:T(512)(128)(4,1)S(1)} %compare_and_fusion), kind=kOutput, calls=%fused_computation.107 | convolution fusion | flops 71055360 | bytes 10506510 | tf_op jit(solution)/shard_map/btk,tkc->tbc/dot_general | solution.py:242
  152.2 2.0 fusion.28
  154.3 1.2 copy.983
  155.5 1.6 select_maximum_fusion
  157.1 10.8 %all-to-all-start.4 = ((f32[32,136,128]{2,1,0:T(8,128)}), f32[32,136,128]{2,1,0:T(8,128)S(1)}, u32[]{:S(2)}, u32[]{:S(2)}) async-start(f32[32,136,128]{2,1,0:T(8,128)} %select_maximum_fusion), calls=%async_computation.4 | async-start | bytes 4456448 | tf_op jit(solution)/shard_map/all_to_all | solution.py:260
  167.9 52.0 %all-to-all-done.4 = f32[32,136,128]{2,1,0:T(8,128)S(1)} async-done(((f32[32,136,128]{2,1,0:T(8,128)}), f32[32,136,128]{2,1,0:T(8,128)S(1)}, u32[]{:S(2)}, u32[]{:S(2)}) %all-to-all-start.4) | async-done | bytes 2228256 | tf_op jit(solution)/shard_map/all_to_all | solution.py:260
  221.5 20.8 %all_to_all.40 = f32[8,8,32,128]{3,2,1,0:T(8,128)S(1)} all-to-all(f32[8,8,32,128]{3,2,1,0:T(8,128)S(1)} %broadcast_in_dim.31), channel_id=1, replica_groups=mesh['space'=32,'scen'=8] {'scen'}, dimensions={0} | all-to-all | bytes 2097152 | tf_op jit(solution)/shard_map/all_to_all | solution.py:274
  (293 shorter events, 56.7 us)
Async XLA Ops:
  0.6 1.2 copy-start.24
  6.4 84.9 %copy-start = (f32[1,8,6,12,384]{4,1,3,2,0:T(8,128)}, f32[1,8,6,12,384]{4,1,3,2,0:T(8,128)S(1)}, u32[]{:S(2)}) copy-start(f32[1,8,6,12,384]{4,1,3,2,0:T(8,128)S(1)} %get-tuple-element.101) | copy-start | bytes 2654212
  16.9 18.3 %copy-start.31 = (s32[270]{0:T(512)S(1)}, s32[270]{0:T(512)}, u32[]{:S(2)}) copy-start(s32[270]{0:T(512)} %param.21) | copy-start | bytes 3244
  16.9 18.4 %copy-start.33 = (s32[270]{0:T(512)S(1)}, s32[270]{0:T(512)}, u32[]{:S(2)}) copy-start(s32[270]{0:T(512)} %param.22) | copy-start | bytes 3244
  20.4 23.1 %all-to-all-start = ((f32[32,1,1152]{2,1,0:T(1,128)}), f32[32,1,1152]{2,1,0:T(1,128)}, u32[]{:S(2)}, u32[]{:S(2)}) async-start(f32[32,1,1152]{2,1,0:T(1,128)} %all_to_all.32), calls=%async_computation | async-start | bytes 294912 | tf_op jit(solution)/shard_map/all_to_all | solution.py:81
  35.2 5.1 %copy-start.9 = (f32[8,3,12,1]{3,0,2,1:T(8,128)S(1)}, f32[8,3,12,1]{3,0,2,1:T(8,128)}, u32[]{:S(2)}) copy-start(f32[8,3,12,1]{3,0,2,1:T(8,128)} %get-tuple-element.129) | copy-start | bytes 3460
  35.2 5.3 %copy-start.23 = (f32[8,1,12,1]{3,0,2,1:T(8,128)S(1)}, f32[8,1,12,1]{3,0,2,1:T(8,128)}, u32[]{:S(2)}) copy-start(f32[8,1,12,1]{3,0,2,1:T(8,128)} %get-tuple-element.131) | copy-start | bytes 1156
  35.2 5.4 %copy-start.22 = (f32[8,1,12,1]{3,0,2,1:T(8,128)S(1)}, f32[8,1,12,1]{3,0,2,1:T(8,128)}, u32[]{:S(2)}) copy-start(f32[8,1,12,1]{3,0,2,1:T(8,128)} %get-tuple-element.132) | copy-start | bytes 1156
  35.2 5.6 %copy-start.21 = (f32[8,1,12,1]{3,0,2,1:T(8,128)S(1)}, f32[8,1,12,1]{3,0,2,1:T(8,128)}, u32[]{:S(2)}) copy-start(f32[8,1,12,1]{3,0,2,1:T(8,128)} %get-tuple-element.133) | copy-start | bytes 1156
  35.2 5.7 %copy-start.20 = (f32[8,1,12,1]{3,0,2,1:T(8,128)S(1)}, f32[8,1,12,1]{3,0,2,1:T(8,128)}, u32[]{:S(2)}) copy-start(f32[8,1,12,1]{3,0,2,1:T(8,128)} %get-tuple-element.134) | copy-start | bytes 1156
  35.3 5.8 %copy-start.19 = (f32[8,1,12,1]{3,0,2,1:T(8,128)S(1)}, f32[8,1,12,1]{3,0,2,1:T(8,128)}, u32[]{:S(2)}) copy-start(f32[8,1,12,1]{3,0,2,1:T(8,128)} %get-tuple-element.135) | copy-start | bytes 1156
  35.3 5.9 %copy-start.18 = (f32[8,1,12,1]{3,0,2,1:T(8,128)S(1)}, f32[8,1,12,1]{3,0,2,1:T(8,128)}, u32[]{:S(2)}) copy-start(f32[8,1,12,1]{3,0,2,1:T(8,128)} %get-tuple-element.136) | copy-start | bytes 1156
  35.3 6.8 %copy-start.8 = (f32[8,3,12,1]{3,0,2,1:T(8,128)S(1)}, f32[8,3,12,1]{3,0,2,1:T(8,128)}, u32[]{:S(2)}) copy-start(f32[8,3,12,1]{3,0,2,1:T(8,128)} %get-tuple-element.130) | copy-start | bytes 3460
  49.5 7.6 %copy-start.2 = (f32[1,8,6,12,1]{4,1,3,2,0:T(8,128)}, f32[1,8,6,12,1]{4,1,3,2,0:T(8,128)S(1)}, u32[]{:S(2)}) copy-start(f32[1,8,6,12,1]{4,1,3,2,0:T(8,128)S(1)} %copy.906) | copy-start | bytes 6916
  51.3 5.8 %copy-start.4 = (f32[1,8,6,12,1]{4,1,3,2,0:T(8,128)}, f32[1,8,6,12,1]{4,1,3,2,0:T(8,128)S(1)}, u32[]{:S(2)}) copy-start(f32[1,8,6,12,1]{4,1,3,2,0:T(8,128)S(1)} %copy.901) | copy-start | bytes 6916
  58.8 1.7 copy-start.26
  61.2 21.4 %all-to-all-start.1 = ((f32[32,12,96]{2,1,0:T(8,128)}), f32[32,12,96]{2,1,0:T(8,128)S(1)}, u32[]{:S(2)}, u32[]{:S(2)}) async-start(f32[32,12,96]{2,1,0:T(8,128)} %fusion.75), calls=%async_computation.1 | async-start | bytes 524288 | tf_op jit(solution)/shard_map/all_to_all | solution.py:145
  71.1 3.5 %copy-start.13 = (f32[48,384]{1,0:T(8,128)S(1)}, f32[48,384]{1,0:T(8,128)}, u32[]{:S(2)}) copy-start(f32[48,384]{1,0:T(8,128)} %reshape.1003) | copy-start | bytes 221188
  72.0 2.6 %copy-start.7 = (f32[144,384]{1,0:T(8,128)S(1)}, f32[144,384]{1,0:T(8,128)}, u32[]{:S(2)}) copy-start(f32[144,384]{1,0:T(8,128)} %reshape.1002) | copy-start | bytes 663556
  74.5 9.3 %collective-permute-start.1 = (f32[192,384]{1,0:T(8,128)}, f32[192,384]{1,0:T(8,128)}, u32[]{:S(2)}, u32[]{:S(2)}) collective-permute-start(f32[192,384]{1,0:T(8,128)} %pad_maximum_fusion.5), channel_id=1, source_target_pairs={{8,0},{16,8},{24,16},{32,24},{40,32},{48,40},{56,48},{64,56},{72,6... | collective-permute-start | bytes 884744 | tf_op jit(solution)/shard_map/ppermute | solution.py:13
  75.4 11.4 %collective-permute-start = (f32[192,384]{1,0:T(8,128)}, f32[192,384]{1,0:T(8,128)}, u32[]{:S(2)}, u32[]{:S(2)}) collective-permute-start(f32[192,384]{1,0:T(8,128)} %pad_maximum_fusion.4), channel_id=1, source_target_pairs={{248,0},{0,8},{8,16},{16,24},{24,32},{32,40},{40,48},{48,56},{56,6... | collective-permute-start | bytes 884744 | tf_op jit(solution)/shard_map/ppermute | solution.py:13
  83.1 2.8 %copy-start.12 = (f32[8,3,384]{2,1,0:T(4,128)}, f32[8,3,384]{2,1,0:T(4,128)S(1)}, u32[]{:S(2)}) copy-start(f32[8,3,384]{2,1,0:T(4,128)S(1)} %reshape.1012) | copy-start | bytes 110596
  92.1 14.0 %copy-start.32 = (s32[270]{0:T(512)S(1)}, s32[270]{0:T(512)}, u32[]{:S(2)}) copy-start(s32[270]{0:T(512)} %param.21) | copy-start | bytes 3244
  93.5 21.7 %all-to-all-start.2 = ((f32[32,1,864]{2,1,0:T(1,128)}), f32[32,1,864]{2,1,0:T(1,128)S(1)}, u32[]{:S(2)}, u32[]{:S(2)}) async-start(f32[32,1,864]{2,1,0:T(1,128)} %all_to_all.33), calls=%async_computation.2 | async-start | bytes 229376 | tf_op jit(solution)/shard_map/all_to_all | solution.py:81
  125.1 14.7 %all-to-all-start.3 = ((f32[32,1,864]{2,1,0:T(1,128)}), f32[32,1,864]{2,1,0:T(1,128)S(1)}, u32[]{:S(2)}, u32[]{:S(2)}) async-start(f32[32,1,864]{2,1,0:T(1,128)} %reshape.1058), calls=%async_computation.3 | async-start | bytes 229376 | tf_op jit(solution)/shard_map/all_to_all | solution.py:145
  130.4 11.4 %collective-permute-start.2 = (f32[144,384]{1,0:T(8,128)S(1)}, f32[144,384]{1,0:T(8,128)S(1)}, u32[]{:S(2)}, u32[]{:S(2)}) collective-permute-start(f32[144,384]{1,0:T(8,128)S(1)} %reshape.1019), channel_id=1, source_target_pairs={{248,0},{0,8},{8,16},{16,24},{24,32},{32,40},{40,48},{48,56},{56,6... | collective-permute-start | bytes 663560 | tf_op jit(solution)/shard_map/ppermute | solution.py:13
  130.8 11.1 %collective-permute-start.3 = (f32[144,384]{1,0:T(8,128)S(1)}, f32[144,384]{1,0:T(8,128)S(1)}, u32[]{:S(2)}, u32[]{:S(2)}) collective-permute-start(f32[144,384]{1,0:T(8,128)S(1)} %reshape.1025), channel_id=1, source_target_pairs={{8,0},{16,8},{24,16},{32,24},{40,32},{48,40},{56,48},{64,56},{72,6... | collective-permute-start | bytes 663560 | tf_op jit(solution)/shard_map/ppermute | solution.py:13
  142.6 1.2 copy-start.1
  144.5 1.1 copy-start.30
  147.3 4.9 %copy-start.29 = (s32[270]{0:T(512)S(1)}, s32[270]{0:T(512)}, u32[]{:S(2)}) copy-start(s32[270]{0:T(512)} %copy-done.28) | copy-start | bytes 3244
  157.1 62.9 %all-to-all-start.4 = ((f32[32,136,128]{2,1,0:T(8,128)}), f32[32,136,128]{2,1,0:T(8,128)S(1)}, u32[]{:S(2)}, u32[]{:S(2)}) async-start(f32[32,136,128]{2,1,0:T(8,128)} %select_maximum_fusion), calls=%async_computation.4 | async-start | bytes 4456448 | tf_op jit(solution)/shard_map/all_to_all | solution.py:260
  221.4 21.0 %copy-start.10 = (f32[8,128,32]{1,2,0:T(8,128)}, f32[8,128,32]{1,2,0:T(8,128)S(1)}, u32[]{:S(2)}) copy-start(f32[8,128,32]{1,2,0:T(8,128)S(1)} %fusion) | copy-start | bytes 393220
  (11 other events, 9.2 us)
where the time goes:
time: 247 us; the launch traced here: 243 us
  waiting for transfers between devices  75.1 us (30%)
  local copies, waits for them, and re-layouts  62.1 us (25%)
  starting transfers between devices  52.5 us (21%)
  other arithmetic  22.7 us (9%)
  blocking collectives  20.8 us (8%)
  matrix products  7.99 us (3%)
    all_to_all x1, waiting for transfers between devices, regrid(): got = lax.all_to_all(send, 'space', 0, 0, tiled=True)  52 us
    all_to_all x2, starting transfers between devices, edge_rows(): got = lax.all_to_all(send, 'space', 0, 0, tiled=True)  24.2 us
    all_to_all x1, blocking collectives, moments_of(): everyone = lax.all_to_all(copies, 'scen', 0, 0, tiled=True)  20.8 us
    all_to_all x2, starting transfers between devices, edge_columns(): got = lax.all_to_all(send, 'space', 0, 0, tiled=True)  14.8 us
    all_to_all x2, waiting for transfers between devices, edge_columns(): got = lax.all_to_all(send, 'space', 0, 0, tiled=True)  13.9 us
    unnamed x104, local copies, waits for them, and re-layouts  13.3 us
    all_to_all x1, starting transfers between devices, regrid(): got = lax.all_to_all(send, 'space', 0, 0, tiled=True)  10.8 us
    all_to_all x2, waiting for transfers between devices, edge_rows(): got = lax.all_to_all(send, 'space', 0, 0, tiled=True)  9.14 us
  transfers between devices with their start and end apart: 9, of which 4 were waited for; matrix products, arithmetic and copies ran while one was open for 9% of the time, Pallas kernels for 0%

commit v1 on v0

--- a/solution.py
+++ b/solution.py
@@ -66,9 +66,14 @@
     return jnp.concatenate(parts, 0)
 
 
-def edge_rows(tracer, north_wind, position, band_count, with_wind):
+def edge_rows(tracer, north_wind, east_wind, position, band_count, with_wind):
+    levels = tracer.shape[1]
     row_count = tracer.shape[3]
     width_cells = tracer.shape[4]
+    column_wind = (
+        jnp.moveaxis(east_wind[:, 0::2, :, 0], 2, 0).reshape(row_count, -1),
+        jnp.moveaxis(east_wind[:, 1::2, :, width_cells - 1], 2, 0).reshape(row_count, -1),
+    )
     top = [tracer[:, :, 0::2, row_count - 3 :, :].reshape(-1, width_cells)]
     low = [tracer[:, :, 1::2, 0:3, :].reshape(-1, width_cells)]
     if with_wind:
@@ -77,15 +82,25 @@
     top = jnp.concatenate(top, 0)
     low = jnp.concatenate(low, 0)
     send = jnp.where(position == band_count - 1, top, jnp.where(position == 0, low, 0.0))
-    send = jnp.flip(send.T, 0).reshape(band_count, -1)
+    count = top.shape[0]
+    send = jnp.flip(send.T, 0).reshape(band_count, row_count, count)
+    if with_wind:
+        gathered = jnp.zeros((band_count,) + column_wind[0].shape, send.dtype)
+        gathered = gathered.at[band_count - 1].set(column_wind[0]).at[0].set(column_wind[1])
+        send = jnp.concatenate([send, gathered], 2)
     got = lax.all_to_all(send, "space", 0, 0, tiled=True)
-    count = top.shape[0]
-    return got[band_count - 1].reshape(-1, count), got[0].reshape(-1, count)
+    wind = None
+    if with_wind:
+        extra = got[:, :, count:].reshape(band_count * row_count, -1)
+        wind = jnp.flip(extra, 0).T.reshape(levels, 3, band_count * row_count)
+    return got[band_count - 1, :, :count], got[0, :, :count], wind
 
 
 def column_halos(tracer, east_wind, north_wind, position, band_count, edge_wind, faces_known):
     scenarios, levels, _, row_count, width_cells = tracer.shape
-    top, low = edge_rows(tracer, north_wind, position, band_count, edge_wind is None)
+    top, low, column_wind = edge_rows(
+        tracer, north_wind, east_wind, position, band_count, edge_wind is None
+    )
     cells = scenarios * levels * 3 * 3
     top_layers = top[:, :cells].reshape(row_count, scenarios, levels, 3, 3)
     low_layers = low[:, :cells].reshape(row_count, scenarios, levels, 3, 3)
@@ -93,8 +108,9 @@
         edge_wind = (
             top[:, cells:].reshape(row_count, levels, 3),
             low[:, cells:].reshape(row_count, levels, 3),
-        )
-    top_wind, low_wind = edge_wind
+            column_wind,
+        )
+    top_wind, low_wind, _ = edge_wind
     west_faces, east_faces, west_speeds, east_speeds = [], [], [], []
     for face_number in range(6):
         half = face_number // 2
@@ -153,19 +169,13 @@
 
 
 def row_halos(tracer, east_wind, north_wind, position, band_count, row_wind, faces_known):
-    first_step = row_wind is None
     shifted = []
     for step_by, lowest in ((-1, True), (1, False)):
-        packed = pack_rows(tracer, north_wind if first_step else None, lowest)
+        packed = pack_rows(tracer, None, lowest)
         shifted.append(from_behind(packed, "space", step_by))
-    edge_layers, edge_speed = edge_columns(tracer, east_wind, position, band_count, first_step)
+    edge_layers, _ = edge_columns(tracer, east_wind, position, band_count, False)
     layer_rows = tracer.shape[0] * tracer.shape[1] * 18
     width_cells = tracer.shape[4]
-    if first_step:
-        levels = tracer.shape[1]
-        row_wind = tuple(
-            packed[layer_rows:].reshape(levels, 6, width_cells) for packed in shifted
-        ) + (edge_speed,)
     above_wind, below_wind, edge_speed = row_wind
     above_layers, below_layers = (
         packed[:layer_rows].reshape(tracer.shape[0], tracer.shape[1], 6, 3, width_cells)
@@ -283,7 +293,12 @@
     east_wind = courant[0]
     north_wind = courant[1]
     edge_wind = None
+    row_count = tracer.shape[3]
     row_wind = None
+    neighbour_wind = (
+        from_behind(north_wind[:, :, 0, :], "space", -1),
+        from_behind(north_wind[:, :, row_count - 1, :], "space", 1),
+    )
     cx = None
     cy = None
     for step_number in range(2):
@@ -291,6 +306,7 @@
             tracer, east_wind, north_wind, position, band_count, edge_wind, cx
         )
         tracer = parabola_sweep(padded, cx, 4)
+        row_wind = neighbour_wind + (edge_wind[2],)
         padded, cy, row_wind = row_halos(
             tracer, east_wind, north_wind, position, band_count, row_wind, cy
         )

time: 247 us -> 278 us (1.13)
  local copies, waits for them, and re-layouts: 62.1 us -> 84.1 us
  other arithmetic: 22.7 us -> 33.5 us
  waiting for transfers between devices: 75.1 us -> 71.9 us
    unnamed x18 -> x27, other arithmetic: 0.14 us -> 8.85 us
    scatter x4 -> x6, local copies, waits for them, and re-layouts: 3.8 us -> 8.93 us  [edge_columns(): send = send.at[band_count - 1].set(to_top).at[0].set(to_low)]
    all_to_all x2, waiting for transfers between devices: 13.9 us -> 9.3 us  [edge_columns(): got = lax.all_to_all(send, 'space', 0, 0, tiled=True)]
    another operation x10 -> x6, local copies, waits for them, and re-layouts: 1.24 us -> 4.31 us
    slice x15 -> x10, local copies, waits for them, and re-layouts: 9.4 us -> 6.35 us  [the longest x2 2.51 us: edge_rows(): east_wind[:, 1::2, :, width_cells - 1]]
    all_to_all x2, starting transfers between devices: 24.2 us -> 21.3 us  [edge_rows(): got = lax.all_to_all(send, 'space', 0, 0, tiled=True)]
    ppermute x4 -> x6, starting transfers between devices: 2.63 us -> 5.52 us  [from_behind(): return lax.ppermute(block, axis, route)]
    unnamed x104 -> x90, local copies, waits for them, and re-layouts: 13.3 us -> 14.5 us
  transfers between devices with their start and end apart: 9 -> 11, of which waited for: 4 -> 5; matrix products, arithmetic and copies ran while one was open for 9% -> 32% of each run, Pallas kernels for 0% -> 0%
where the time goes in v1:
time: 278 us; the launch traced here: 273 us
  local copies, waits for them, and re-layouts  84.1 us (30%)
  waiting for transfers between devices  71.9 us (26%)
  starting transfers between devices  53.6 us (19%)
  other arithmetic  33.5 us (12%)
  blocking collectives  20.3 us (7%)
  matrix products  8 us (3%)
    all_to_all x1, waiting for transfers between devices, regrid(): got = lax.all_to_all(send, 'space', 0, 0, tiled=True)  52.1 us
    all_to_all x2, starting transfers between devices, edge_rows(): got = lax.all_to_all(send, 'space', 0, 0, tiled=True)  21.3 us
    all_to_all x1, blocking collectives, moments_of(): everyone = lax.all_to_all(copies, 'scen', 0, 0, tiled=True)  20.3 us
    all_to_all x2, starting transfers between devices, edge_columns(): got = lax.all_to_all(send, 'space', 0, 0, tiled=True)  15.6 us
    unnamed x90, local copies, waits for them, and re-layouts  14.5 us
    all_to_all x1, starting transfers between devices, regrid(): got = lax.all_to_all(send, 'space', 0, 0, tiled=True)  11.2 us
    all_to_all x2, waiting for transfers between devices, edge_rows(): got = lax.all_to_all(send, 'space', 0, 0, tiled=True)  10.5 us
    all_to_all x2, waiting for transfers between devices, edge_columns(): got = lax.all_to_all(send, 'space', 0, 0, tiled=True)  9.3 us
  transfers between devices with their start and end apart: 11, of which 5 were waited for; matrix products, arithmetic and copies ran while one was open for 32% of the time, Pallas kernels for 0%

profile of v1, /device:TPU:2, one launch (start us, length us, event | category | flops | bytes accessed | tf_op | source)
XLA Modules:
  0.0 273.1 jit_solution(10277153299909368321)
XLA Ops:
  3.5 1.7 collective-permute-start.1
  5.8 1.6 bitcast_add_fusion
  7.5 2.2 scatter-add.4
  11.0 1.6 reshape.1033
  12.7 1.6 copy.419
  14.3 1.6 reshape.1032
  21.5 1.7 fusion.68
  23.2 2.4 rev.18
  25.6 1.7 copy.423
  27.3 1.6 reshape.1034
  29.8 1.7 copy.427
  34.2 1.7 copy.424
  38.8 1.8 pad_maximum_fusion.4
  40.6 13.4 %all-to-all-start = ((f32[32,12,120]{2,1,0:T(8,128)}), f32[32,12,120]{2,1,0:T(8,128)}, u32[]{:S(2)}, u32[]{:S(2)}) async-start(f32[32,12,120]{2,1,0:T(8,128)} %pad_maximum_fusion.4), calls=%async_computation | async-start | bytes 524288 | tf_op jit(solution)/shard_map/all_to_all | solution.py:91
  85.3 1.8 copy.457
  92.8 2.7 %scatter.29 = f32[32,12,72]{1,0,2:T(8,128)} dynamic-update-slice(f32[32,12,72]{1,0,2:T(8,128)} %scatter.26, f32[1,12,72]{1,0,2:T(1,128)S(1)} %bitcast.228, s32[]{:T(128)} %constant.265.clone.1, s32[]{:T(128)} %constant.265.clone.1, s32[]{:T(128)} %constant.265.clone.1) | dynamic-update-slice | bytes 6916 | tf_op jit(solution)/shard_map/scatter | solution.py:160
  95.5 1.9 copy.458
  98.3 10.2 %all-to-all-start.1 = ((f32[32,1,864]{2,1,0:T(1,128)}), f32[32,1,864]{2,1,0:T(1,128)S(1)}, u32[]{:S(2)}, u32[]{:S(2)}) async-start(f32[32,1,864]{2,1,0:T(1,128)} %reshape.1088), calls=%async_computation.1 | async-start | bytes 229376 | tf_op jit(solution)/shard_map/all_to_all | solution.py:161
  115.8 2.0 all-to-all-done.1
  127.1 7.8 %all-to-all-start.2 = ((f32[32,1,864]{2,1,0:T(1,128)}), f32[32,1,864]{2,1,0:T(1,128)S(1)}, u32[]{:S(2)}, u32[]{:S(2)}) async-start(f32[32,1,864]{2,1,0:T(1,128)} %reshape.1090), calls=%async_computation.2 | async-start | bytes 229376 | tf_op jit(solution)/shard_map/all_to_all | solution.py:91
  134.9 9.2 %all-to-all-done.2 = f32[32,1,864]{2,1,0:T(1,128)S(1)} async-done(((f32[32,1,864]{2,1,0:T(1,128)}), f32[32,1,864]{2,1,0:T(1,128)S(1)}, u32[]{:S(2)}, u32[]{:S(2)}) %all-to-all-start.2) | async-done | bytes 110624 | tf_op jit(solution)/shard_map/all_to_all | solution.py:91
  151.6 2.2 scatter.31
  155.4 5.4 %all-to-all-start.3 = ((f32[32,1,864]{2,1,0:T(1,128)}), f32[32,1,864]{2,1,0:T(1,128)S(1)}, u32[]{:S(2)}, u32[]{:S(2)}) async-start(f32[32,1,864]{2,1,0:T(1,128)} %reshape.1092), calls=%async_computation.3 | async-start | bytes 229376 | tf_op jit(solution)/shard_map/all_to_all | solution.py:161
  161.4 1.7 collective-permute-start.5
  163.1 7.3 %all-to-all-done.3 = f32[32,1,864]{2,1,0:T(1,128)S(1)} async-done(((f32[32,1,864]{2,1,0:T(1,128)}), f32[32,1,864]{2,1,0:T(1,128)S(1)}, u32[]{:S(2)}, u32[]{:S(2)}) %all-to-all-start.3) | async-done | bytes 110624 | tf_op jit(solution)/shard_map/all_to_all | solution.py:161
  175.5 1.8 gather_fusion
  177.3 4.9 %fusion.62 = f32[270,8,128]{2,1,0:T(8,128)S(1)} fusion(bf16[270,128,128]{2,1,0:T(8,128)(2,1)} %param.27, bf16[270,8,128]{2,1,0:T(8,128)(2,1)S(1)} %gather_fusion, pred[270]{0:T(512)(128)(4,1)S(1)} %compare_and_fusion), kind=kOutput, calls=%fused_computation.107 | convolution fusion | flops 71055360 | bytes 10506510 | tf_op jit(solution)/shard_map/btk,tkc->tbc/dot_general | solution.py:252
  182.3 2.0 fusion.28
  185.5 1.6 select_maximum_fusion
  187.1 11.2 %all-to-all-start.4 = ((f32[32,136,128]{2,1,0:T(8,128)}), f32[32,136,128]{2,1,0:T(8,128)S(1)}, u32[]{:S(2)}, u32[]{:S(2)}) async-start(f32[32,136,128]{2,1,0:T(8,128)} %select_maximum_fusion), calls=%async_computation.4 | async-start | bytes 4456448 | tf_op jit(solution)/shard_map/all_to_all | solution.py:270
  198.3 52.1 %all-to-all-done.4 = f32[32,136,128]{2,1,0:T(8,128)S(1)} async-done(((f32[32,136,128]{2,1,0:T(8,128)}), f32[32,136,128]{2,1,0:T(8,128)S(1)}, u32[]{:S(2)}, u32[]{:S(2)}) %all-to-all-start.4) | async-done | bytes 2228256 | tf_op jit(solution)/shard_map/all_to_all | solution.py:270
  251.9 20.3 %all_to_all.30 = f32[8,8,32,128]{3,2,1,0:T(8,128)S(1)} all-to-all(f32[8,8,32,128]{3,2,1,0:T(8,128)S(1)} %broadcast_in_dim.31), channel_id=1, replica_groups=mesh['space'=32,'scen'=8] {'scen'}, dimensions={0} | all-to-all | bytes 2097152 | tf_op jit(solution)/shard_map/all_to_all | solution.py:284
  (282 shorter events, 88.6 us)
Async XLA Ops:
  0.6 1.7 copy-start.6
  2.7 122.0 %copy-start = (f32[1,8,6,12,384]{4,1,3,2,0:T(8,128)}, f32[1,8,6,12,384]{4,1,3,2,0:T(8,128)S(1)}, u32[]{:S(2)}) copy-start(f32[1,8,6,12,384]{4,1,3,2,0:T(8,128)S(1)} %get-tuple-element.109) | copy-start | bytes 2654212
  3.5 59.7 %collective-permute-start = (f32[8,6,384]{2,0,1:T(8,128)}, f32[8,6,384]{2,0,1:T(8,128)}, u32[]{:S(2)}, u32[]{:S(2)}) collective-permute-start(f32[8,6,384]{2,0,1:T(8,128)} %get-tuple-element.131), channel_id=1, source_target_pairs={{248,0},{0,8},{8,16},{16,24},{24,32},{32,40},{40,48},{48,56},{56,6... | collective-permute-start | bytes 221192 | tf_op jit(solution)/shard_map/ppermute | solution.py:13
  3.5 108.0 %collective-permute-start.1 = (f32[8,6,384]{2,0,1:T(8,128)}, f32[8,6,384]{2,0,1:T(8,128)}, u32[]{:S(2)}, u32[]{:S(2)}) collective-permute-start(f32[8,6,384]{2,0,1:T(8,128)} %get-tuple-element.132), channel_id=1, source_target_pairs={{8,0},{16,8},{24,16},{32,24},{40,32},{48,40},{56,48},{64,56},{72,6... | collective-permute-start | bytes 221192 | tf_op jit(solution)/shard_map/ppermute | solution.py:13
  37.3 17.5 %copy-start.21 = (s32[270]{0:T(512)S(1)}, s32[270]{0:T(512)}, u32[]{:S(2)}) copy-start(s32[270]{0:T(512)} %param.25) | copy-start | bytes 3244
  38.1 16.7 %copy-start.23 = (s32[270]{0:T(512)S(1)}, s32[270]{0:T(512)}, u32[]{:S(2)}) copy-start(s32[270]{0:T(512)} %param.26) | copy-start | bytes 3244
  40.6 25.1 %all-to-all-start = ((f32[32,12,120]{2,1,0:T(8,128)}), f32[32,12,120]{2,1,0:T(8,128)}, u32[]{:S(2)}, u32[]{:S(2)}) async-start(f32[32,12,120]{2,1,0:T(8,128)} %pad_maximum_fusion.4), calls=%async_computation | async-start | bytes 524288 | tf_op jit(solution)/shard_map/all_to_all | solution.py:91
  71.4 7.6 %copy-start.2 = (f32[1,8,6,12,1]{4,1,3,2,0:T(8,128)}, f32[1,8,6,12,1]{4,1,3,2,0:T(8,128)S(1)}, u32[]{:S(2)}) copy-start(f32[1,8,6,12,1]{4,1,3,2,0:T(8,128)S(1)} %copy.434) | copy-start | bytes 6916
  73.3 5.8 %copy-start.4 = (f32[1,8,6,12,1]{4,1,3,2,0:T(8,128)}, f32[1,8,6,12,1]{4,1,3,2,0:T(8,128)S(1)}, u32[]{:S(2)}) copy-start(f32[1,8,6,12,1]{4,1,3,2,0:T(8,128)S(1)} %copy.439) | copy-start | bytes 6916
  87.9 3.6 %copy-start.14 = (f32[12,1,8,3,3]{0,1,4,3,2:T(1,128)S(1)}, f32[12,1,8,3,3]{0,1,4,3,2:T(1,128)}, u32[]{:S(2)}) copy-start(f32[12,1,8,3,3]{0,1,4,3,2:T(1,128)} %copy.456) | copy-start | bytes 10372
  88.8 4.0 %copy-start.15 = (f32[12,1,8,3,3]{0,1,4,3,2:T(1,128)S(1)}, f32[12,1,8,3,3]{0,1,4,3,2:T(1,128)}, u32[]{:S(2)}) copy-start(f32[12,1,8,3,3]{0,1,4,3,2:T(1,128)} %copy.457) | copy-start | bytes 10372
  88.8 30.9 %collective-permute-start.2 = (f32[144,384]{1,0:T(8,128)}, f32[144,384]{1,0:T(8,128)}, u32[]{:S(2)}, u32[]{:S(2)}) collective-permute-start(f32[144,384]{1,0:T(8,128)} %reshape.1043), channel_id=1, source_target_pairs={{248,0},{0,8},{8,16},{16,24},{24,32},{32,40},{40,48},{48,56},{56,6... | collective-permute-start | bytes 663560 | tf_op jit(solution)/shard_map/ppermute | solution.py:13
  90.5 30.9 %collective-permute-start.3 = (f32[144,384]{1,0:T(8,128)}, f32[144,384]{1,0:T(8,128)}, u32[]{:S(2)}, u32[]{:S(2)}) collective-permute-start(f32[144,384]{1,0:T(8,128)} %reshape.1049), channel_id=1, source_target_pairs={{8,0},{16,8},{24,16},{32,24},{40,32},{48,40},{56,48},{64,56},{72,6... | collective-permute-start | bytes 663560 | tf_op jit(solution)/shard_map/ppermute | solution.py:13
  92.8 15.8 %copy-start.8 = (f32[8,6,384]{2,0,1:T(8,128)S(1)}, f32[8,6,384]{2,0,1:T(8,128)}, u32[]{:S(2)}) copy-start(f32[8,6,384]{2,0,1:T(8,128)} %constant_dynamic-update-slice_fusion.29) | copy-start | bytes 221188
  92.8 15.8 %copy-start.16 = (f32[8,1,384]{2,1,0:T(1,128)S(1)}, f32[8,1,384]{2,1,0:T(1,128)}, u32[]{:S(2)}) copy-start(f32[8,1,384]{2,1,0:T(1,128)} %get-tuple-element.192) | copy-start | bytes 36868
  92.8 18.7 %copy-start.18 = (f32[8,1,384]{2,1,0:T(1,128)S(1)}, f32[8,1,384]{2,1,0:T(1,128)}, u32[]{:S(2)}) copy-start(f32[8,1,384]{2,1,0:T(1,128)} %get-tuple-element.193) | copy-start | bytes 36868
  98.3 19.5 %all-to-all-start.1 = ((f32[32,1,864]{2,1,0:T(1,128)}), f32[32,1,864]{2,1,0:T(1,128)S(1)}, u32[]{:S(2)}, u32[]{:S(2)}) async-start(f32[32,1,864]{2,1,0:T(1,128)} %reshape.1088), calls=%async_computation.1 | async-start | bytes 229376 | tf_op jit(solution)/shard_map/all_to_all | solution.py:161
  112.2 12.6 %copy-start.9 = (f32[8,6,384]{2,0,1:T(8,128)}, f32[8,6,384]{2,0,1:T(8,128)S(1)}, u32[]{:S(2)}) copy-start(f32[8,6,384]{2,0,1:T(8,128)S(1)} %get-tuple-element.214) | copy-start | bytes 221188
  115.8 8.9 %copy-start.11 = (f32[8,6,384]{2,0,1:T(8,128)}, f32[8,6,384]{2,0,1:T(8,128)S(1)}, u32[]{:S(2)}) copy-start(f32[8,6,384]{2,0,1:T(8,128)S(1)} %constant_dynamic-update-slice_fusion.30) | copy-start | bytes 221188
  122.4 1.7 copy-start.13
  125.6 9.3 %copy-start.22 = (s32[270]{0:T(512)S(1)}, s32[270]{0:T(512)}, u32[]{:S(2)}) copy-start(s32[270]{0:T(512)} %param.25) | copy-start | bytes 3244
  127.1 17.1 %all-to-all-start.2 = ((f32[32,1,864]{2,1,0:T(1,128)}), f32[32,1,864]{2,1,0:T(1,128)S(1)}, u32[]{:S(2)}, u32[]{:S(2)}) async-start(f32[32,1,864]{2,1,0:T(1,128)} %reshape.1090), calls=%async_computation.2 | async-start | bytes 229376 | tf_op jit(solution)/shard_map/all_to_all | solution.py:91
  155.4 15.1 %all-to-all-start.3 = ((f32[32,1,864]{2,1,0:T(1,128)}), f32[32,1,864]{2,1,0:T(1,128)S(1)}, u32[]{:S(2)}, u32[]{:S(2)}) async-start(f32[32,1,864]{2,1,0:T(1,128)} %reshape.1092), calls=%async_computation.3 | async-start | bytes 229376 | tf_op jit(solution)/shard_map/all_to_all | solution.py:161
  161.0 10.8 %collective-permute-start.4 = (f32[144,384]{1,0:T(8,128)S(1)}, f32[144,384]{1,0:T(8,128)S(1)}, u32[]{:S(2)}, u32[]{:S(2)}) collective-permute-start(f32[144,384]{1,0:T(8,128)S(1)} %reshape.1052), channel_id=1, source_target_pairs={{248,0},{0,8},{8,16},{16,24},{24,32},{32,40},{40,48},{48,56},{56,6... | collective-permute-start | bytes 663560 | tf_op jit(solution)/shard_map/ppermute | solution.py:13
  161.4 10.5 %collective-permute-start.5 = (f32[144,384]{1,0:T(8,128)S(1)}, f32[144,384]{1,0:T(8,128)S(1)}, u32[]{:S(2)}, u32[]{:S(2)}) collective-permute-start(f32[144,384]{1,0:T(8,128)S(1)} %reshape.1058), channel_id=1, source_target_pairs={{8,0},{16,8},{24,16},{32,24},{40,32},{48,40},{56,48},{64,56},{72,6... | collective-permute-start | bytes 663560 | tf_op jit(solution)/shard_map/ppermute | solution.py:13
  172.6 1.2 copy-start.1
  172.6 1.2 copy-start.10
  172.6 1.2 copy-start.12
  174.5 1.1 copy-start.20
  184.3 1.2 copy-start.17
  187.1 63.3 %all-to-all-start.4 = ((f32[32,136,128]{2,1,0:T(8,128)}), f32[32,136,128]{2,1,0:T(8,128)S(1)}, u32[]{:S(2)}, u32[]{:S(2)}) async-start(f32[32,136,128]{2,1,0:T(8,128)} %select_maximum_fusion), calls=%async_computation.4 | async-start | bytes 4456448 | tf_op jit(solution)/shard_map/all_to_all | solution.py:270
  251.8 20.4 %copy-start.7 = (f32[8,128,32]{1,2,0:T(8,128)}, f32[8,128,32]{1,2,0:T(8,128)S(1)}, u32[]{:S(2)}) copy-start(f32[8,128,32]{1,2,0:T(8,128)S(1)} %fusion) | copy-start | bytes 393220
  (3 other events, 2.7 us)

commit v2 on v0

--- a/solution.py
+++ b/solution.py
@@ -66,48 +66,69 @@
     return jnp.concatenate(parts, 0)
 
 
-def edge_rows(tracer, north_wind, position, band_count, with_wind):
-    row_count = tracer.shape[3]
-    width_cells = tracer.shape[4]
-    top = [tracer[:, :, 0::2, row_count - 3 :, :].reshape(-1, width_cells)]
-    low = [tracer[:, :, 1::2, 0:3, :].reshape(-1, width_cells)]
-    if with_wind:
-        top.append(north_wind[:, 0::2, row_count - 1, :].reshape(-1, width_cells))
-        low.append(north_wind[:, 1::2, 0, :].reshape(-1, width_cells))
-    top = jnp.concatenate(top, 0)
-    low = jnp.concatenate(low, 0)
+def first_exchange(tracer, north_wind, position, band_count):
+    scenarios, levels, _, row_count, width_cells = tracer.shape
+    top = jnp.concatenate(
+        [
+            tracer[:, :, 0::2, row_count - 3 :, :].reshape(-1, width_cells),
+            north_wind[:, 0::2, row_count - 4 :, :].reshape(-1, width_cells),
+        ],
+        0,
+    )
+    low = jnp.concatenate(
+        [
+            tracer[:, :, 1::2, 0:3, :].reshape(-1, width_cells),
+            north_wind[:, 1::2, 0:4, :].reshape(-1, width_cells),
+        ],
+        0,
+    )
     send = jnp.where(position == band_count - 1, top, jnp.where(position == 0, low, 0.0))
     send = jnp.flip(send.T, 0).reshape(band_count, -1)
     got = lax.all_to_all(send, "space", 0, 0, tiled=True)
     count = top.shape[0]
-    return got[band_count - 1].reshape(-1, count), got[0].reshape(-1, count)
-
-
-def column_halos(tracer, east_wind, north_wind, position, band_count, edge_wind, faces_known):
-    scenarios, levels, _, row_count, width_cells = tracer.shape
-    top, low = edge_rows(tracer, north_wind, position, band_count, edge_wind is None)
     cells = scenarios * levels * 3 * 3
-    top_layers = top[:, :cells].reshape(row_count, scenarios, levels, 3, 3)
-    low_layers = low[:, :cells].reshape(row_count, scenarios, levels, 3, 3)
-    if edge_wind is None:
-        edge_wind = (
-            top[:, cells:].reshape(row_count, levels, 3),
-            low[:, cells:].reshape(row_count, levels, 3),
-        )
-    top_wind, low_wind = edge_wind
+
+    def cells_of(block):
+        return jnp.moveaxis(block[:, :cells].reshape(row_count, scenarios, levels, 3, 3), 0, 3)
+
+    def wind_of(block):
+        return jnp.moveaxis(block[:, cells:].reshape(row_count, levels, 3, 4), 0, 2)
+
+    top_got = got[band_count - 1].reshape(row_count, count)
+    low_got = got[0].reshape(row_count, count)
+    return cells_of(top_got), cells_of(low_got), wind_of(top_got), wind_of(low_got)
+
+
+def next_edge_cells(swept, east_wind, rows_top, rows_low, top_wind, low_wind):
+    width_cells = swept.shape[4]
+    halo_top = jnp.stack([swept[:, :, (2 * e + 2) % 6, :, 0:3] for e in range(3)], 2)
+    halo_low = jnp.stack([swept[:, :, (2 * o - 1) % 6, :, width_cells - 3 :] for o in range(3)], 2)
+    speed_top = jnp.stack([east_wind[:, (2 * e + 2) % 6, :, 0] for e in range(3)], 1)
+    speed_low = jnp.stack([east_wind[:, (2 * o - 1) % 6, :, width_cells - 1] for o in range(3)], 1)
+    speeds_top = jnp.concatenate([top_wind, speed_top[..., None]], -1)
+    speeds_low = jnp.concatenate([speed_low[..., None], low_wind], -1)
+    faces_top = 0.5 * (speeds_top[..., :-1] + speeds_top[..., 1:])
+    faces_low = 0.5 * (speeds_low[..., :-1] + speeds_low[..., 1:])
+    top_cells = parabola_sweep(jnp.concatenate([rows_top, halo_top], -1), faces_top, 4)
+    low_cells = parabola_sweep(jnp.concatenate([halo_low, rows_low], -1), faces_low, 4)
+    return top_cells, low_cells
+
+
+def column_halos(tracer, east_wind, top_cells, low_cells, top_wind, low_wind, faces_known):
+    width_cells = tracer.shape[4]
     west_faces, east_faces, west_speeds, east_speeds = [], [], [], []
     for face_number in range(6):
         half = face_number // 2
         if face_number % 2 == 0:
-            west_cells = jnp.moveaxis(top_layers[:, :, :, (half - 1) % 3], 0, 2)
-            west_speed = top_wind[:, :, (half - 1) % 3].T
+            west_cells = top_cells[:, :, (half - 1) % 3]
+            west_speed = top_wind[:, (half - 1) % 3, :, 3]
             east_cells = tracer[:, :, (face_number + 1) % 6, :, 0:3]
             east_speed = east_wind[:, (face_number + 1) % 6, :, 0]
         else:
             west_cells = tracer[:, :, (face_number - 1) % 6, :, width_cells - 3 :]
             west_speed = east_wind[:, (face_number - 1) % 6, :, width_cells - 1]
-            east_cells = jnp.moveaxis(low_layers[:, :, :, (half + 1) % 3], 0, 2)
-            east_speed = low_wind[:, :, (half + 1) % 3].T
+            east_cells = low_cells[:, :, (half + 1) % 3]
+            east_speed = low_wind[:, (half + 1) % 3, :, 0]
         west_faces.append(west_cells)
         east_faces.append(east_cells)
         west_speeds.append(west_speed)
@@ -125,10 +146,10 @@
             -1,
         )
         faces_known = 0.5 * (speeds[..., :-1] + speeds[..., 1:])
-    return (padded, faces_known, edge_wind)
-
-
-def edge_columns(tracer, east_wind, position, band_count, with_wind):
+    return padded, faces_known
+
+
+def edge_columns(tracer, east_wind, position, band_count, with_wind, scatter_rows):
     scenarios, levels, _, row_count, width_cells = tracer.shape
     to_top = [jnp.moveaxis(tracer[:, :, 0::2, :, 0:3], 3, 0).reshape(row_count, -1)]
     to_low = [jnp.moveaxis(tracer[:, :, 1::2, :, width_cells - 3 :], 3, 0).reshape(row_count, -1)]
@@ -142,23 +163,43 @@
     count = to_top.shape[1]
     send = jnp.zeros((band_count, row_count, count), to_top.dtype)
     send = send.at[band_count - 1].set(to_top).at[0].set(to_low)
+    if scatter_rows:
+        rows_top = tracer[:, :, 0::2, row_count - 6 :, :].reshape(-1, width_cells)
+        rows_low = tracer[:, :, 1::2, 0:6, :].reshape(-1, width_cells)
+        chosen = jnp.where(
+            position == band_count - 1, rows_top, jnp.where(position == 0, rows_low, 0.0)
+        )
+        scattered = jnp.flip(chosen.T, 0).reshape(band_count, row_count, rows_top.shape[0])
+        send = jnp.concatenate([send, scattered], 2)
     got = lax.all_to_all(send, "space", 0, 0, tiled=True)
+    extra = None
+    if scatter_rows:
+
+        def rows_of(block):
+            return jnp.moveaxis(block.reshape(row_count, scenarios, levels, 3, 6), 0, 3)
+
+        extra = (rows_of(got[band_count - 1, :, count:]), rows_of(got[0, :, count:]))
+        got = got[:, :, :count]
     flipped = jnp.flip(got.reshape(-1, count), 0).T
     cells = scenarios * levels * 3 * 3
     layers = flipped[:cells].reshape(scenarios, levels, 3, 3, band_count * row_count)
     wind = None
     if with_wind:
         wind = flipped[cells:].reshape(levels, 3, band_count * row_count)
-    return layers, wind
-
-
-def row_halos(tracer, east_wind, north_wind, position, band_count, row_wind, faces_known):
+    return layers, wind, extra
+
+
+def row_halos(
+    tracer, east_wind, north_wind, position, band_count, row_wind, faces_known, scatter_rows
+):
     first_step = row_wind is None
     shifted = []
     for step_by, lowest in ((-1, True), (1, False)):
         packed = pack_rows(tracer, north_wind if first_step else None, lowest)
         shifted.append(from_behind(packed, "space", step_by))
-    edge_layers, edge_speed = edge_columns(tracer, east_wind, position, band_count, first_step)
+    edge_layers, edge_speed, extra = edge_columns(
+        tracer, east_wind, position, band_count, first_step, scatter_rows
+    )
     layer_rows = tracer.shape[0] * tracer.shape[1] * 18
     width_cells = tracer.shape[4]
     if first_step:
@@ -229,7 +270,7 @@
             -2,
         )
         faces_known = 0.5 * (speeds[:, :, :-1, :] + speeds[:, :, 1:, :])
-    return (padded, faces_known, row_wind)
+    return (padded, faces_known, row_wind, extra)
 
 
 def regrid(tracer, tile_source, tile_target, intersection, band_count):
@@ -282,18 +323,24 @@
     tracer = concentration.at[:, 0].add(emissions)
     east_wind = courant[0]
     north_wind = courant[1]
-    edge_wind = None
+    top_cells, low_cells, top_wind, low_wind = first_exchange(
+        tracer, north_wind, position, band_count
+    )
     row_wind = None
     cx = None
     cy = None
     for step_number in range(2):
-        padded, cx, edge_wind = column_halos(
-            tracer, east_wind, north_wind, position, band_count, edge_wind, cx
+        padded, cx = column_halos(
+            tracer, east_wind, top_cells, low_cells, top_wind, low_wind, cx
         )
         tracer = parabola_sweep(padded, cx, 4)
-        padded, cy, row_wind = row_halos(
-            tracer, east_wind, north_wind, position, band_count, row_wind, cy
-        )
+        padded, cy, row_wind, extra = row_halos(
+            tracer, east_wind, north_wind, position, band_count, row_wind, cy, step_number == 0
+        )
+        if step_number == 0:
+            top_cells, low_cells = next_edge_cells(
+                tracer, east_wind, extra[0], extra[1], top_wind, low_wind
+            )
         tracer = parabola_sweep(padded, cy, 3)
     regridded = regrid(tracer, tile_source, tile_target, intersection, band_count)
     ensemble_moments = moments_of(regridded)

time: 247 us -> 292 us (1.18)
  local copies, waits for them, and re-layouts: 62.1 us -> 108 us
  other arithmetic: 22.7 us -> 40.8 us
  waiting for transfers between devices: 75.1 us -> 61.8 us
  starting transfers between devices: 52.5 us -> 45.8 us
    slice x16 -> x35, local copies, waits for them, and re-layouts: 3.9 us -> 17.5 us  [the longest x4 3.67 us: next_edge_cells(): east_wind[:, (2 * e + 2) % 6, :, 0]]
    all_to_all x2 -> x1, starting transfers between devices: 24.2 us -> 11.8 us  [first_exchange(): got = lax.all_to_all(send, 'space', 0, 0, tiled=True)]
    all_to_all x2 -> x1, waiting for transfers between devices: 9.14 us -> 0.01 us  [first_exchange(): got = lax.all_to_all(send, 'space', 0, 0, tiled=True)]
    unnamed x18, other arithmetic: 0.14 us -> 7.36 us
    all_to_all x2, starting transfers between devices: 14.8 us -> 20.4 us  [edge_columns(): got = lax.all_to_all(send, 'space', 0, 0, tiled=True)]
    reshape x6 -> x11, local copies, waits for them, and re-layouts: 1.48 us -> 6.73 us  [the longest x1 1.62 us: first_exchange(): north_wind[:, 0::2, row_count - 4:, :].reshape(-1, width_cells)]
    all_to_all x2, waiting for transfers between devices: 13.9 us -> 9.73 us  [edge_columns(): got = lax.all_to_all(send, 'space', 0, 0, tiled=True)]
    unnamed x104 -> x122, local copies, waits for them, and re-layouts: 13.3 us -> 16.1 us
  transfers between devices with their start and end apart: 9 -> 8, of which waited for: 4 -> 3; matrix products, arithmetic and copies ran while one was open for 9% -> 14% of each run, Pallas kernels for 0% -> 0%
where the time goes in v2:
time: 292 us; the launch traced here: 286 us
  local copies, waits for them, and re-layouts  108 us (37%)
  waiting for transfers between devices  61.8 us (21%)
  starting transfers between devices  45.8 us (16%)
  other arithmetic  40.8 us (14%)
  blocking collectives  20.3 us (7%)
  matrix products  8 us (3%)
    all_to_all x1, waiting for transfers between devices, regrid(): got = lax.all_to_all(send, 'space', 0, 0, tiled=True)  52.1 us
    all_to_all x2, starting transfers between devices, edge_columns(): got = lax.all_to_all(send, 'space', 0, 0, tiled=True)  20.4 us
    all_to_all x1, blocking collectives, moments_of(): everyone = lax.all_to_all(copies, 'scen', 0, 0, tiled=True)  20.3 us
    unnamed x122, local copies, waits for them, and re-layouts  16.1 us
    all_to_all x1, starting transfers between devices, first_exchange(): got = lax.all_to_all(send, 'space', 0, 0, tiled=True)  11.8 us
    all_to_all x1, starting transfers between devices, regrid(): got = lax.all_to_all(send, 'space', 0, 0, tiled=True)  10.9 us
    all_to_all x2, waiting for transfers between devices, edge_columns(): got = lax.all_to_all(send, 'space', 0, 0, tiled=True)  9.73 us
    unnamed x18, other arithmetic  7.36 us
  transfers between devices with their start and end apart: 8, of which 3 were waited for; matrix products, arithmetic and copies ran while one was open for 14% of the time, Pallas kernels for 0%

profile of v2, /device:TPU:2, one launch (start us, length us, event | category | flops | bytes accessed | tf_op | source)
XLA Modules:
  0.0 286.1 jit_solution(4412026020196126462)
XLA Ops:
  4.6 2.7 fusion.112
  7.3 1.7 fusion.120
  9.7 1.6 reshape.1000
  11.3 1.6 copy.892
  12.9 1.6 reshape.998
  14.5 1.8 fusion.68
  16.4 3.9 %rev.16 = f32[384,168]{0,1:T(8,128)} reverse(f32[384,168]{0,1:T(8,128)} %fusion.68), dimensions={0} | reverse | bytes 516096 | tf_op jit(solution)/shard_map/jit(_flip)/rev | solution.py:86
  20.3 1.9 copy.895
  22.2 2.5 all_to_all.24
  24.7 11.8 %all-to-all-start = ((f32[32,1,2016]{2,1,0:T(1,128)}), f32[32,1,2016]{2,1,0:T(1,128)}, u32[]{:S(2)}, u32[]{:S(2)}) async-start(f32[32,1,2016]{2,1,0:T(1,128)} %all_to_all.24), calls=%async_computation | async-start | bytes 524288 | tf_op jit(solution)/shard_map/all_to_all | solution.py:87
  36.5 1.6 fusion.117
  78.7 1.5 pad_maximum_fusion.2
  91.9 1.7 pad_maximum_fusion.6
  93.8 1.7 pad_maximum_fusion.5
  97.1 13.5 %all-to-all-start.1 = ((f32[32,12,240]{2,1,0:T(8,128)}), f32[32,12,240]{2,1,0:T(8,128)S(1)}, u32[]{:S(2)}, u32[]{:S(2)}) async-start(f32[32,12,240]{2,1,0:T(8,128)} %pad_maximum_fusion.4), calls=%async_computation.1 | async-start | bytes 1048576 | tf_op jit(solution)/shard_map/all_to_all | solution.py:174
  112.8 1.6 slice.1127
  118.6 1.6 slice.1116
  120.2 1.7 reshape.1020
  121.9 1.6 fusion.124
  125.0 2.8 all-to-all-done.1
  129.3 1.7 rev.18
  143.2 2.0 broadcast_select_fusion.6
  163.2 2.2 scatter.21
  167.0 7.0 %all-to-all-start.2 = ((f32[32,1,864]{2,1,0:T(1,128)}), f32[32,1,864]{2,1,0:T(1,128)S(1)}, u32[]{:S(2)}, u32[]{:S(2)}) async-start(f32[32,1,864]{2,1,0:T(1,128)} %reshape.1068), calls=%async_computation.2 | async-start | bytes 229376 | tf_op jit(solution)/shard_map/all_to_all | solution.py:174
  174.8 1.7 collective-permute-start.3
  176.5 6.9 %all-to-all-done.2 = f32[32,1,864]{2,1,0:T(1,128)S(1)} async-done(((f32[32,1,864]{2,1,0:T(1,128)}), f32[32,1,864]{2,1,0:T(1,128)S(1)}, u32[]{:S(2)}, u32[]{:S(2)}) %all-to-all-start.2) | async-done | bytes 110624 | tf_op jit(solution)/shard_map/all_to_all | solution.py:174
  188.9 1.8 gather_fusion
  190.7 4.9 %fusion.62 = f32[270,8,128]{2,1,0:T(8,128)S(1)} fusion(bf16[270,128,128]{2,1,0:T(8,128)(2,1)} %param.23, bf16[270,8,128]{2,1,0:T(8,128)(2,1)S(1)} %gather_fusion, pred[270]{0:T(512)(128)(4,1)S(1)} %copy-done.46), kind=kOutput, calls=%fused_computation.107 | convolution fusion | flops 71055360 | bytes 10506510 | tf_op jit(solution)/shard_map/btk,tkc->tbc/dot_general | solution.py:283
  195.6 2.0 fusion.28
  200.4 10.9 %all-to-all-start.3 = ((f32[32,136,128]{2,1,0:T(8,128)}), f32[32,136,128]{2,1,0:T(8,128)S(1)}, u32[]{:S(2)}, u32[]{:S(2)}) async-start(f32[32,136,128]{2,1,0:T(8,128)} %select_maximum_fusion), calls=%async_computation.3 | async-start | bytes 4456448 | tf_op jit(solution)/shard_map/all_to_all | solution.py:301
  211.3 52.1 %all-to-all-done.3 = f32[32,136,128]{2,1,0:T(8,128)S(1)} async-done(((f32[32,136,128]{2,1,0:T(8,128)}), f32[32,136,128]{2,1,0:T(8,128)S(1)}, u32[]{:S(2)}, u32[]{:S(2)}) %all-to-all-start.3) | async-done | bytes 2228256 | tf_op jit(solution)/shard_map/all_to_all | solution.py:301
  265.0 20.3 %all_to_all.30 = f32[8,8,32,128]{3,2,1,0:T(8,128)S(1)} all-to-all(f32[8,8,32,128]{3,2,1,0:T(8,128)S(1)} %broadcast_in_dim.134), channel_id=1, replica_groups=mesh['space'=32,'scen'=8] {'scen'}, dimensions={0} | all-to-all | bytes 2097152 | tf_op jit(solution)/shard_map/all_to_all | solution.py:315
  (344 shorter events, 110.0 us)
Async XLA Ops:
  24.7 15.1 %copy-start.44 = (s32[270]{0:T(512)S(1)}, s32[270]{0:T(512)}, u32[]{:S(2)}) copy-start(s32[270]{0:T(512)} %param.21) | copy-start | bytes 3244
  24.7 15.2 %copy-start.47 = (s32[270]{0:T(512)S(1)}, s32[270]{0:T(512)}, u32[]{:S(2)}) copy-start(s32[270]{0:T(512)} %param.22) | copy-start | bytes 3244
  24.7 33.7 %all-to-all-start = ((f32[32,1,2016]{2,1,0:T(1,128)}), f32[32,1,2016]{2,1,0:T(1,128)}, u32[]{:S(2)}, u32[]{:S(2)}) async-start(f32[32,1,2016]{2,1,0:T(1,128)} %all_to_all.24), calls=%async_computation | async-start | bytes 524288 | tf_op jit(solution)/shard_map/all_to_all | solution.py:87
  39.7 9.4 %copy-start.24 = (f32[8,6,1,384]{3,0,2,1:T(8,128)S(1)}, f32[8,6,1,384]{3,0,2,1:T(8,128)}, u32[]{:S(2)}) copy-start(f32[8,6,1,384]{3,0,2,1:T(8,128)} %get-tuple-element.145) | copy-start | bytes 221188
  39.7 10.1 %copy-start.20 = (f32[8,3,12,1]{3,0,2,1:T(8,128)S(1)}, f32[8,3,12,1]{3,0,2,1:T(8,128)}, u32[]{:S(2)}) copy-start(f32[8,3,12,1]{3,0,2,1:T(8,128)} %get-tuple-element.148) | copy-start | bytes 3460
  39.8 11.0 %copy-start.30 = (f32[8,1,12,1]{3,0,2,1:T(8,128)S(1)}, f32[8,1,12,1]{3,0,2,1:T(8,128)}, u32[]{:S(2)}) copy-start(f32[8,1,12,1]{3,0,2,1:T(8,128)} %get-tuple-element.130) | copy-start | bytes 1156
  39.8 11.7 %copy-start.29 = (f32[8,1,12,1]{3,0,2,1:T(8,128)S(1)}, f32[8,1,12,1]{3,0,2,1:T(8,128)}, u32[]{:S(2)}) copy-start(f32[8,1,12,1]{3,0,2,1:T(8,128)} %get-tuple-element.131) | copy-start | bytes 1156
  39.8 12.4 %copy-start.28 = (f32[8,1,12,1]{3,0,2,1:T(8,128)S(1)}, f32[8,1,12,1]{3,0,2,1:T(8,128)}, u32[]{:S(2)}) copy-start(f32[8,1,12,1]{3,0,2,1:T(8,128)} %get-tuple-element.132) | copy-start | bytes 1156
  39.8 12.6 %copy-start.27 = (f32[8,1,12,1]{3,0,2,1:T(8,128)S(1)}, f32[8,1,12,1]{3,0,2,1:T(8,128)}, u32[]{:S(2)}) copy-start(f32[8,1,12,1]{3,0,2,1:T(8,128)} %get-tuple-element.133) | copy-start | bytes 1156
  39.8 13.3 %copy-start.26 = (f32[8,1,12,1]{3,0,2,1:T(8,128)S(1)}, f32[8,1,12,1]{3,0,2,1:T(8,128)}, u32[]{:S(2)}) copy-start(f32[8,1,12,1]{3,0,2,1:T(8,128)} %get-tuple-element.134) | copy-start | bytes 1156
  39.8 14.0 %copy-start.25 = (f32[8,1,12,1]{3,0,2,1:T(8,128)S(1)}, f32[8,1,12,1]{3,0,2,1:T(8,128)}, u32[]{:S(2)}) copy-start(f32[8,1,12,1]{3,0,2,1:T(8,128)} %get-tuple-element.135) | copy-start | bytes 1156
  39.8 14.7 %copy-start.19 = (f32[8,3,12,1]{3,0,2,1:T(8,128)S(1)}, f32[8,3,12,1]{3,0,2,1:T(8,128)}, u32[]{:S(2)}) copy-start(f32[8,3,12,1]{3,0,2,1:T(8,128)} %get-tuple-element.149) | copy-start | bytes 3460
  41.1 16.2 %copy-start.45 = (s32[270]{0:T(512)S(1)}, s32[270]{0:T(512)}, u32[]{:S(2)}) copy-start(s32[270]{0:T(512)} %param.21) | copy-start | bytes 3244
  41.2 6.4 %copy-start.38 = (s32[270]{0:T(512)}, s32[270]{0:T(512)S(1)}, u32[]{:S(2)}) copy-start(s32[270]{0:T(512)S(1)} %add_select_fusion.2) | copy-start | bytes 3244
  60.2 5.2 %copy-start.8 = (f32[12,8,3,4]{3,1,0,2:T(8,128)}, f32[12,8,3,4]{3,1,0,2:T(8,128)S(1)}, u32[]{:S(2)}) copy-start(f32[12,8,3,4]{3,1,0,2:T(8,128)S(1)} %copy.898) | copy-start | bytes 13828
  60.5 5.0 %copy-start.6 = (f32[12,8,3,4]{3,1,0,2:T(8,128)}, f32[12,8,3,4]{3,1,0,2:T(8,128)S(1)}, u32[]{:S(2)}) copy-start(f32[12,8,3,4]{3,1,0,2:T(8,128)S(1)} %copy.908) | copy-start | bytes 13828
  71.2 10.8 %copy-start = (f32[1,8,6,12,1]{4,1,3,2,0:T(8,128)}, f32[1,8,6,12,1]{4,1,3,2,0:T(8,128)S(1)}, u32[]{:S(2)}) copy-start(f32[1,8,6,12,1]{4,1,3,2,0:T(8,128)S(1)} %copy.914) | copy-start | bytes 6916
  90.1 5.8 %copy-start.37 = (f32[12,24]{1,0:T(8,128)S(1)}, f32[12,24]{1,0:T(8,128)}, u32[]{:S(2)}) copy-start(f32[12,24]{1,0:T(8,128)} %copy.925) | copy-start | bytes 3460
  90.1 5.9 %copy-start.36 = (f32[12,24]{1,0:T(8,128)S(1)}, f32[12,24]{1,0:T(8,128)}, u32[]{:S(2)}) copy-start(f32[12,24]{1,0:T(8,128)} %copy.930) | copy-start | bytes 3460
  93.7 17.6 %collective-permute-start.1 = (f32[192,384]{1,0:T(8,128)}, f32[192,384]{1,0:T(8,128)}, u32[]{:S(2)}, u32[]{:S(2)}) collective-permute-start(f32[192,384]{1,0:T(8,128)} %pad_maximum_fusion.6), channel_id=1, source_target_pairs={{8,0},{16,8},{24,16},{32,24},{40,32},{48,40},{56,48},{64,56},{72,6... | collective-permute-start | bytes 884744 | tf_op jit(solution)/shard_map/ppermute | solution.py:13
  95.5 20.0 %collective-permute-start = (f32[192,384]{1,0:T(8,128)}, f32[192,384]{1,0:T(8,128)}, u32[]{:S(2)}, u32[]{:S(2)}) collective-permute-start(f32[192,384]{1,0:T(8,128)} %pad_maximum_fusion.5), channel_id=1, source_target_pairs={{248,0},{0,8},{8,16},{16,24},{24,32},{32,40},{40,48},{48,56},{56,6... | collective-permute-start | bytes 884744 | tf_op jit(solution)/shard_map/ppermute | solution.py:13
  97.1 30.7 %all-to-all-start.1 = ((f32[32,12,240]{2,1,0:T(8,128)}), f32[32,12,240]{2,1,0:T(8,128)S(1)}, u32[]{:S(2)}, u32[]{:S(2)}) async-start(f32[32,12,240]{2,1,0:T(8,128)} %pad_maximum_fusion.4), calls=%async_computation.1 | async-start | bytes 1048576 | tf_op jit(solution)/shard_map/all_to_all | solution.py:174
  123.6 8.6 %copy-start.23 = (f32[1,8,1,3,384]{4,3,2,1,0:T(4,128)}, f32[1,8,1,3,384]{4,3,2,1,0:T(4,128)S(1)}, u32[]{:S(2)}) copy-start(f32[1,8,1,3,384]{4,3,2,1,0:T(4,128)S(1)} %get-tuple-element.179) | copy-start | bytes 110596
  138.1 9.5 %copy-start.11 = (f32[1,8,6,3,384]{4,1,3,2,0:T(8,128)S(1)}, f32[1,8,6,3,384]{4,1,3,2,0:T(8,128)}, u32[]{:S(2)}) copy-start(f32[1,8,6,3,384]{4,1,3,2,0:T(8,128)} %constant_dynamic-update-slice_fusion.29) | copy-start | bytes 663556
  138.1 12.8 %copy-start.22 = (f32[1,8,1,3,384]{4,3,2,1,0:T(4,128)S(1)}, f32[1,8,1,3,384]{4,3,2,1,0:T(4,128)}, u32[]{:S(2)}) copy-start(f32[1,8,1,3,384]{4,3,2,1,0:T(4,128)} %get-tuple-element.185) | copy-start | bytes 110596
  143.2 13.2 %copy-start.12 = (f32[8,6,384]{2,0,1:T(8,128)}, f32[8,6,384]{2,0,1:T(8,128)S(1)}, u32[]{:S(2)}) copy-start(f32[8,6,384]{2,0,1:T(8,128)S(1)} %copy.1107) | copy-start | bytes 221188
  147.6 8.8 %copy-start.14 = (f32[8,6,384]{2,0,1:T(8,128)}, f32[8,6,384]{2,0,1:T(8,128)S(1)}, u32[]{:S(2)}) copy-start(f32[8,6,384]{2,0,1:T(8,128)S(1)} %copy.1108) | copy-start | bytes 221188
  167.0 16.5 %all-to-all-start.2 = ((f32[32,1,864]{2,1,0:T(1,128)}), f32[32,1,864]{2,1,0:T(1,128)S(1)}, u32[]{:S(2)}, u32[]{:S(2)}) async-start(f32[32,1,864]{2,1,0:T(1,128)} %reshape.1068), calls=%async_computation.2 | async-start | bytes 229376 | tf_op jit(solution)/shard_map/all_to_all | solution.py:174
  174.2 11.2 %collective-permute-start.2 = (f32[144,384]{1,0:T(8,128)S(1)}, f32[144,384]{1,0:T(8,128)S(1)}, u32[]{:S(2)}, u32[]{:S(2)}) collective-permute-start(f32[144,384]{1,0:T(8,128)S(1)} %reshape.1023), channel_id=1, source_target_pairs={{248,0},{0,8},{8,16},{16,24},{24,32},{32,40},{40,48},{48,56},{56,6... | collective-permute-start | bytes 663560 | tf_op jit(solution)/shard_map/ppermute | solution.py:13
  174.8 10.7 %collective-permute-start.3 = (f32[144,384]{1,0:T(8,128)S(1)}, f32[144,384]{1,0:T(8,128)S(1)}, u32[]{:S(2)}, u32[]{:S(2)}) collective-permute-start(f32[144,384]{1,0:T(8,128)S(1)} %reshape.1029), channel_id=1, source_target_pairs={{8,0},{16,8},{24,16},{32,24},{40,32},{48,40},{56,48},{64,56},{72,6... | collective-permute-start | bytes 663560 | tf_op jit(solution)/shard_map/ppermute | solution.py:13
  200.4 63.0 %all-to-all-start.3 = ((f32[32,136,128]{2,1,0:T(8,128)}), f32[32,136,128]{2,1,0:T(8,128)S(1)}, u32[]{:S(2)}, u32[]{:S(2)}) async-start(f32[32,136,128]{2,1,0:T(8,128)} %select_maximum_fusion), calls=%async_computation.3 | async-start | bytes 4456448 | tf_op jit(solution)/shard_map/all_to_all | solution.py:301
  264.8 20.4 %copy-start.21 = (f32[8,128,32]{1,2,0:T(8,128)}, f32[8,128,32]{1,2,0:T(8,128)S(1)}, u32[]{:S(2)}) copy-start(f32[8,128,32]{1,2,0:T(8,128)S(1)} %fusion) | copy-start | bytes 393220
  (24 other events, 54.0 us)

commit v3 on v2

--- a/solution.py
+++ b/solution.py
@@ -89,10 +89,10 @@
     cells = scenarios * levels * 3 * 3
 
     def cells_of(block):
-        return jnp.moveaxis(block[:, :cells].reshape(row_count, scenarios, levels, 3, 3), 0, 3)
+        return block[:, :cells].reshape(row_count, scenarios, levels, 3, 3)
 
     def wind_of(block):
-        return jnp.moveaxis(block[:, cells:].reshape(row_count, levels, 3, 4), 0, 2)
+        return block[:, cells:].reshape(row_count, levels, 3, 4)
 
     top_got = got[band_count - 1].reshape(row_count, count)
     low_got = got[0].reshape(row_count, count)
@@ -101,16 +101,25 @@
 
 def next_edge_cells(swept, east_wind, rows_top, rows_low, top_wind, low_wind):
     width_cells = swept.shape[4]
-    halo_top = jnp.stack([swept[:, :, (2 * e + 2) % 6, :, 0:3] for e in range(3)], 2)
-    halo_low = jnp.stack([swept[:, :, (2 * o - 1) % 6, :, width_cells - 3 :] for o in range(3)], 2)
-    speed_top = jnp.stack([east_wind[:, (2 * e + 2) % 6, :, 0] for e in range(3)], 1)
-    speed_low = jnp.stack([east_wind[:, (2 * o - 1) % 6, :, width_cells - 1] for o in range(3)], 1)
+    halo_top = jnp.stack(
+        [jnp.moveaxis(swept[:, :, (2 * e + 2) % 6, :, 0:3], 2, 0) for e in range(3)], 3
+    )
+    halo_low = jnp.stack(
+        [jnp.moveaxis(swept[:, :, (2 * o - 1) % 6, :, width_cells - 3 :], 2, 0) for o in range(3)],
+        3,
+    )
+    speed_top = jnp.stack([east_wind[:, (2 * e + 2) % 6, :, 0].T for e in range(3)], 2)
+    speed_low = jnp.stack([east_wind[:, (2 * o - 1) % 6, :, width_cells - 1].T for o in range(3)], 2)
     speeds_top = jnp.concatenate([top_wind, speed_top[..., None]], -1)
     speeds_low = jnp.concatenate([speed_low[..., None], low_wind], -1)
     faces_top = 0.5 * (speeds_top[..., :-1] + speeds_top[..., 1:])
     faces_low = 0.5 * (speeds_low[..., :-1] + speeds_low[..., 1:])
-    top_cells = parabola_sweep(jnp.concatenate([rows_top, halo_top], -1), faces_top, 4)
-    low_cells = parabola_sweep(jnp.concatenate([halo_low, rows_low], -1), faces_low, 4)
+    top_cells = parabola_sweep(
+        jnp.concatenate([rows_top, halo_top], -1), faces_top[:, None], 4
+    )
+    low_cells = parabola_sweep(
+        jnp.concatenate([halo_low, rows_low], -1), faces_low[:, None], 4
+    )
     return top_cells, low_cells
 
 
@@ -120,15 +129,15 @@
     for face_number in range(6):
         half = face_number // 2
         if face_number % 2 == 0:
-            west_cells = top_cells[:, :, (half - 1) % 3]
-            west_speed = top_wind[:, (half - 1) % 3, :, 3]
+            west_cells = jnp.moveaxis(top_cells[:, :, :, (half - 1) % 3], 0, 2)
+            west_speed = top_wind[:, :, (half - 1) % 3, 3].T
             east_cells = tracer[:, :, (face_number + 1) % 6, :, 0:3]
             east_speed = east_wind[:, (face_number + 1) % 6, :, 0]
         else:
             west_cells = tracer[:, :, (face_number - 1) % 6, :, width_cells - 3 :]
             west_speed = east_wind[:, (face_number - 1) % 6, :, width_cells - 1]
-            east_cells = low_cells[:, :, (half + 1) % 3]
-            east_speed = low_wind[:, (half + 1) % 3, :, 0]
+            east_cells = jnp.moveaxis(low_cells[:, :, :, (half + 1) % 3], 0, 2)
+            east_speed = low_wind[:, :, (half + 1) % 3, 0].T
         west_faces.append(west_cells)
         east_faces.append(east_cells)
         west_speeds.append(west_speed)
@@ -176,7 +185,7 @@
     if scatter_rows:
 
         def rows_of(block):
-            return jnp.moveaxis(block.reshape(row_count, scenarios, levels, 3, 6), 0, 3)
+            return block.reshape(row_count, scenarios, levels, 3, 6)
 
         extra = (rows_of(got[band_count - 1, :, count:]), rows_of(got[0, :, count:]))
         got = got[:, :, :count]

time: 292 us -> 283 us (0.969)
  local copies, waits for them, and re-layouts: 108 us -> 99.9 us
    slice x17 -> x12, local copies, waits for them, and re-layouts: 5.14 us -> 0.59 us  [the longest x4 0.35 us: wind_of(): return block[:, cells:].reshape(row_count, levels, 3, 4)]
    unnamed x122 -> x128, local copies, waits for them, and re-layouts: 16.1 us -> 15.6 us
where the time goes in v3:
time: 283 us; the launch traced here: 278 us
  local copies, waits for them, and re-layouts  99.9 us (35%)
  waiting for transfers between devices  60 us (21%)
  starting transfers between devices  47.8 us (17%)
  other arithmetic  39.9 us (14%)
  blocking collectives  20.3 us (7%)
  matrix products  8 us (3%)
    all_to_all x1, waiting for transfers between devices, regrid(): got = lax.all_to_all(send, 'space', 0, 0, tiled=True)  52.1 us
    all_to_all x2, starting transfers between devices, edge_columns(): got = lax.all_to_all(send, 'space', 0, 0, tiled=True)  22.4 us
    all_to_all x1, blocking collectives, moments_of(): everyone = lax.all_to_all(copies, 'scen', 0, 0, tiled=True)  20.3 us
    unnamed x128, local copies, waits for them, and re-layouts  15.6 us
    all_to_all x1, starting transfers between devices, first_exchange(): got = lax.all_to_all(send, 'space', 0, 0, tiled=True)  11.8 us
    all_to_all x1, starting transfers between devices, regrid(): got = lax.all_to_all(send, 'space', 0, 0, tiled=True)  10.9 us
    all_to_all x2, waiting for transfers between devices, edge_columns(): got = lax.all_to_all(send, 'space', 0, 0, tiled=True)  7.89 us
    unnamed x18, other arithmetic  7.36 us
  transfers between devices with their start and end apart: 8, of which 3 were waited for; matrix products, arithmetic and copies ran while one was open for 14% of the time, Pallas kernels for 0%

profile of v3, /device:TPU:2, one launch (start us, length us, event | category | flops | bytes accessed | tf_op | source)
XLA Modules:
  0.0 277.9 jit_solution(17681009371665083641)
XLA Ops:
  4.6 2.7 fusion.112
  7.3 1.7 fusion.119
  9.7 1.6 reshape.1020
  11.3 1.6 copy.1179
  12.9 1.6 reshape.1018
  14.5 1.8 fusion.68
  16.4 3.9 %rev.16 = f32[384,168]{0,1:T(8,128)} reverse(f32[384,168]{0,1:T(8,128)} %fusion.68), dimensions={0} | reverse | bytes 516096 | tf_op jit(solution)/shard_map/jit(_flip)/rev | solution.py:86
  20.3 1.9 copy.1182
  22.1 2.5 all_to_all.24
  24.7 11.8 %all-to-all-start = ((f32[32,1,2016]{2,1,0:T(1,128)}), f32[32,1,2016]{2,1,0:T(1,128)}, u32[]{:S(2)}, u32[]{:S(2)}) async-start(f32[32,1,2016]{2,1,0:T(1,128)} %all_to_all.24), calls=%async_computation | async-start | bytes 524288 | tf_op jit(solution)/shard_map/all_to_all | solution.py:87
  36.5 1.6 fusion.116
  63.5 1.5 constant_dynamic-update-slice_fusion.15
  82.6 1.7 pad_maximum_fusion.6
  84.4 1.7 pad_maximum_fusion.5
  87.8 13.6 %all-to-all-start.1 = ((f32[32,12,240]{2,1,0:T(8,128)}), f32[32,12,240]{2,1,0:T(8,128)S(1)}, u32[]{:S(2)}, u32[]{:S(2)}) async-start(f32[32,12,240]{2,1,0:T(8,128)} %pad_maximum_fusion.4), calls=%async_computation.1 | async-start | bytes 1048576 | tf_op jit(solution)/shard_map/all_to_all | solution.py:183
  105.5 1.6 slice.1127
  109.7 1.5 reshape.1027
  111.2 1.6 slice.1116
  112.9 1.7 reshape.1040
  114.6 1.6 fusion.123
  120.1 1.7 rev.18
  133.1 2.0 broadcast_select_fusion.6
  153.0 2.2 scatter.21
  156.9 8.8 %all-to-all-start.2 = ((f32[32,1,864]{2,1,0:T(1,128)}), f32[32,1,864]{2,1,0:T(1,128)S(1)}, u32[]{:S(2)}, u32[]{:S(2)}) async-start(f32[32,1,864]{2,1,0:T(1,128)} %reshape.1088), calls=%async_computation.2 | async-start | bytes 229376 | tf_op jit(solution)/shard_map/all_to_all | solution.py:183
  166.6 1.7 collective-permute-start.3
  168.3 6.9 %all-to-all-done.2 = f32[32,1,864]{2,1,0:T(1,128)S(1)} async-done(((f32[32,1,864]{2,1,0:T(1,128)}), f32[32,1,864]{2,1,0:T(1,128)S(1)}, u32[]{:S(2)}, u32[]{:S(2)}) %all-to-all-start.2) | async-done | bytes 110624 | tf_op jit(solution)/shard_map/all_to_all | solution.py:183
  180.6 1.8 gather_fusion
  182.4 4.9 %fusion.62 = f32[270,8,128]{2,1,0:T(8,128)S(1)} fusion(bf16[270,128,128]{2,1,0:T(8,128)(2,1)} %param.23, bf16[270,8,128]{2,1,0:T(8,128)(2,1)S(1)} %gather_fusion, pred[270]{0:T(512)(128)(4,1)S(1)} %copy-done.46), kind=kOutput, calls=%fused_computation.107 | convolution fusion | flops 71055360 | bytes 10506510 | tf_op jit(solution)/shard_map/btk,tkc->tbc/dot_general | solution.py:292
  187.4 2.0 fusion.28
  192.1 10.9 %all-to-all-start.3 = ((f32[32,136,128]{2,1,0:T(8,128)}), f32[32,136,128]{2,1,0:T(8,128)S(1)}, u32[]{:S(2)}, u32[]{:S(2)}) async-start(f32[32,136,128]{2,1,0:T(8,128)} %select_maximum_fusion), calls=%async_computation.3 | async-start | bytes 4456448 | tf_op jit(solution)/shard_map/all_to_all | solution.py:310
  203.1 52.1 %all-to-all-done.3 = f32[32,136,128]{2,1,0:T(8,128)S(1)} async-done(((f32[32,136,128]{2,1,0:T(8,128)}), f32[32,136,128]{2,1,0:T(8,128)S(1)}, u32[]{:S(2)}, u32[]{:S(2)}) %all-to-all-start.3) | async-done | bytes 2228256 | tf_op jit(solution)/shard_map/all_to_all | solution.py:310
  256.7 20.3 %all_to_all.30 = f32[8,8,32,128]{3,2,1,0:T(8,128)S(1)} all-to-all(f32[8,8,32,128]{3,2,1,0:T(8,128)S(1)} %broadcast_in_dim.43), channel_id=1, replica_groups=mesh['space'=32,'scen'=8] {'scen'}, dimensions={0} | all-to-all | bytes 2097152 | tf_op jit(solution)/shard_map/all_to_all | solution.py:324
  (344 shorter events, 101.1 us)
Async XLA Ops:
  24.7 15.0 %copy-start.44 = (s32[270]{0:T(512)S(1)}, s32[270]{0:T(512)}, u32[]{:S(2)}) copy-start(s32[270]{0:T(512)} %param.21) | copy-start | bytes 3244
  24.7 15.1 %copy-start.47 = (s32[270]{0:T(512)S(1)}, s32[270]{0:T(512)}, u32[]{:S(2)}) copy-start(s32[270]{0:T(512)} %param.22) | copy-start | bytes 3244
  24.7 30.2 %all-to-all-start = ((f32[32,1,2016]{2,1,0:T(1,128)}), f32[32,1,2016]{2,1,0:T(1,128)}, u32[]{:S(2)}, u32[]{:S(2)}) async-start(f32[32,1,2016]{2,1,0:T(1,128)} %all_to_all.24), calls=%async_computation | async-start | bytes 524288 | tf_op jit(solution)/shard_map/all_to_all | solution.py:87
  39.7 9.4 %copy-start.22 = (f32[8,6,1,384]{3,0,2,1:T(8,128)S(1)}, f32[8,6,1,384]{3,0,2,1:T(8,128)}, u32[]{:S(2)}) copy-start(f32[8,6,1,384]{3,0,2,1:T(8,128)} %get-tuple-element.145) | copy-start | bytes 221188
  39.7 10.1 %copy-start.18 = (f32[8,3,12,1]{3,0,2,1:T(8,128)S(1)}, f32[8,3,12,1]{3,0,2,1:T(8,128)}, u32[]{:S(2)}) copy-start(f32[8,3,12,1]{3,0,2,1:T(8,128)} %get-tuple-element.148) | copy-start | bytes 3460
  39.7 11.0 %copy-start.32 = (f32[8,1,12,1]{3,0,2,1:T(8,128)S(1)}, f32[8,1,12,1]{3,0,2,1:T(8,128)}, u32[]{:S(2)}) copy-start(f32[8,1,12,1]{3,0,2,1:T(8,128)} %get-tuple-element.130) | copy-start | bytes 1156
  39.7 11.1 %copy-start.31 = (f32[8,1,12,1]{3,0,2,1:T(8,128)S(1)}, f32[8,1,12,1]{3,0,2,1:T(8,128)}, u32[]{:S(2)}) copy-start(f32[8,1,12,1]{3,0,2,1:T(8,128)} %get-tuple-element.131) | copy-start | bytes 1156
  39.7 11.3 %copy-start.30 = (f32[8,1,12,1]{3,0,2,1:T(8,128)S(1)}, f32[8,1,12,1]{3,0,2,1:T(8,128)}, u32[]{:S(2)}) copy-start(f32[8,1,12,1]{3,0,2,1:T(8,128)} %get-tuple-element.132) | copy-start | bytes 1156
  39.8 11.4 %copy-start.29 = (f32[8,1,12,1]{3,0,2,1:T(8,128)S(1)}, f32[8,1,12,1]{3,0,2,1:T(8,128)}, u32[]{:S(2)}) copy-start(f32[8,1,12,1]{3,0,2,1:T(8,128)} %get-tuple-element.133) | copy-start | bytes 1156
  39.8 11.5 %copy-start.28 = (f32[8,1,12,1]{3,0,2,1:T(8,128)S(1)}, f32[8,1,12,1]{3,0,2,1:T(8,128)}, u32[]{:S(2)}) copy-start(f32[8,1,12,1]{3,0,2,1:T(8,128)} %get-tuple-element.134) | copy-start | bytes 1156
  39.8 11.6 %copy-start.27 = (f32[8,1,12,1]{3,0,2,1:T(8,128)S(1)}, f32[8,1,12,1]{3,0,2,1:T(8,128)}, u32[]{:S(2)}) copy-start(f32[8,1,12,1]{3,0,2,1:T(8,128)} %get-tuple-element.135) | copy-start | bytes 1156
  39.8 11.8 %copy-start.17 = (f32[8,3,12,1]{3,0,2,1:T(8,128)S(1)}, f32[8,3,12,1]{3,0,2,1:T(8,128)}, u32[]{:S(2)}) copy-start(f32[8,3,12,1]{3,0,2,1:T(8,128)} %get-tuple-element.149) | copy-start | bytes 3460
  41.1 13.2 %copy-start.45 = (s32[270]{0:T(512)S(1)}, s32[270]{0:T(512)}, u32[]{:S(2)}) copy-start(s32[270]{0:T(512)} %param.21) | copy-start | bytes 3244
  41.1 6.4 %copy-start.41 = (s32[270]{0:T(512)}, s32[270]{0:T(512)S(1)}, u32[]{:S(2)}) copy-start(s32[270]{0:T(512)S(1)} %add_select_fusion.2) | copy-start | bytes 3244
  61.6 11.1 %copy-start = (f32[1,8,6,12,1]{4,1,3,2,0:T(8,128)}, f32[1,8,6,12,1]{4,1,3,2,0:T(8,128)S(1)}, u32[]{:S(2)}) copy-start(f32[1,8,6,12,1]{4,1,3,2,0:T(8,128)S(1)} %copy.1193) | copy-start | bytes 6916
  63.5 9.2 %copy-start.2 = (f32[1,8,6,12,1]{4,1,3,2,0:T(8,128)}, f32[1,8,6,12,1]{4,1,3,2,0:T(8,128)S(1)}, u32[]{:S(2)}) copy-start(f32[1,8,6,12,1]{4,1,3,2,0:T(8,128)S(1)} %copy.1188) | copy-start | bytes 6916
  80.8 5.9 %copy-start.39 = (f32[12,24]{1,0:T(8,128)S(1)}, f32[12,24]{1,0:T(8,128)}, u32[]{:S(2)}) copy-start(f32[12,24]{1,0:T(8,128)} %copy.1213) | copy-start | bytes 3460
  84.3 19.6 %collective-permute-start.1 = (f32[192,384]{1,0:T(8,128)}, f32[192,384]{1,0:T(8,128)}, u32[]{:S(2)}, u32[]{:S(2)}) collective-permute-start(f32[192,384]{1,0:T(8,128)} %pad_maximum_fusion.6), channel_id=1, source_target_pairs={{8,0},{16,8},{24,16},{32,24},{40,32},{48,40},{56,48},{64,56},{72,6... | collective-permute-start | bytes 884744 | tf_op jit(solution)/shard_map/ppermute | solution.py:13
  86.2 22.0 %collective-permute-start = (f32[192,384]{1,0:T(8,128)}, f32[192,384]{1,0:T(8,128)}, u32[]{:S(2)}, u32[]{:S(2)}) collective-permute-start(f32[192,384]{1,0:T(8,128)} %pad_maximum_fusion.5), channel_id=1, source_target_pairs={{248,0},{0,8},{8,16},{16,24},{24,32},{32,40},{40,48},{48,56},{56,6... | collective-permute-start | bytes 884744 | tf_op jit(solution)/shard_map/ppermute | solution.py:13
  86.7 15.4 %copy-start.26 = (f32[12,96]{0,1:T(8,128)S(1)}, f32[12,96]{0,1:T(8,128)}, u32[]{:S(2)}) copy-start(f32[12,96]{0,1:T(8,128)} %copy-done.25) | copy-start | bytes 13828
  87.7 15.3 %copy-start.24 = (f32[12,96]{0,1:T(8,128)S(1)}, f32[12,96]{0,1:T(8,128)}, u32[]{:S(2)}) copy-start(f32[12,96]{0,1:T(8,128)} %copy-done.23) | copy-start | bytes 13828
  87.8 30.8 %all-to-all-start.1 = ((f32[32,12,240]{2,1,0:T(8,128)}), f32[32,12,240]{2,1,0:T(8,128)S(1)}, u32[]{:S(2)}, u32[]{:S(2)}) async-start(f32[32,12,240]{2,1,0:T(8,128)} %pad_maximum_fusion.4), calls=%async_computation.1 | async-start | bytes 1048576 | tf_op jit(solution)/shard_map/all_to_all | solution.py:183
  116.2 6.7 %copy-start.21 = (f32[1,8,1,3,384]{4,3,2,1,0:T(4,128)}, f32[1,8,1,3,384]{4,3,2,1,0:T(4,128)S(1)}, u32[]{:S(2)}) copy-start(f32[1,8,1,3,384]{4,3,2,1,0:T(4,128)S(1)} %get-tuple-element.179) | copy-start | bytes 110596
  128.1 9.3 %copy-start.7 = (f32[1,8,6,3,384]{4,1,3,2,0:T(8,128)S(1)}, f32[1,8,6,3,384]{4,1,3,2,0:T(8,128)}, u32[]{:S(2)}) copy-start(f32[1,8,6,3,384]{4,1,3,2,0:T(8,128)} %constant_dynamic-update-slice_fusion.29) | copy-start | bytes 663556
  128.1 12.7 %copy-start.20 = (f32[1,8,1,3,384]{4,3,2,1,0:T(4,128)S(1)}, f32[1,8,1,3,384]{4,3,2,1,0:T(4,128)}, u32[]{:S(2)}) copy-start(f32[1,8,1,3,384]{4,3,2,1,0:T(4,128)} %get-tuple-element.185) | copy-start | bytes 110596
  133.1 13.2 %copy-start.8 = (f32[8,6,384]{2,0,1:T(8,128)}, f32[8,6,384]{2,0,1:T(8,128)S(1)}, u32[]{:S(2)}) copy-start(f32[8,6,384]{2,0,1:T(8,128)S(1)} %copy.1404) | copy-start | bytes 221188
  137.4 8.8 %copy-start.10 = (f32[8,6,384]{2,0,1:T(8,128)}, f32[8,6,384]{2,0,1:T(8,128)S(1)}, u32[]{:S(2)}) copy-start(f32[8,6,384]{2,0,1:T(8,128)S(1)} %copy.1405) | copy-start | bytes 221188
  156.9 18.3 %all-to-all-start.2 = ((f32[32,1,864]{2,1,0:T(1,128)}), f32[32,1,864]{2,1,0:T(1,128)S(1)}, u32[]{:S(2)}, u32[]{:S(2)}) async-start(f32[32,1,864]{2,1,0:T(1,128)} %reshape.1088), calls=%async_computation.2 | async-start | bytes 229376 | tf_op jit(solution)/shard_map/all_to_all | solution.py:183
  165.9 11.2 %collective-permute-start.2 = (f32[144,384]{1,0:T(8,128)S(1)}, f32[144,384]{1,0:T(8,128)S(1)}, u32[]{:S(2)}, u32[]{:S(2)}) collective-permute-start(f32[144,384]{1,0:T(8,128)S(1)} %reshape.1043), channel_id=1, source_target_pairs={{248,0},{0,8},{8,16},{16,24},{24,32},{32,40},{40,48},{48,56},{56,6... | collective-permute-start | bytes 663560 | tf_op jit(solution)/shard_map/ppermute | solution.py:13
  166.6 10.7 %collective-permute-start.3 = (f32[144,384]{1,0:T(8,128)S(1)}, f32[144,384]{1,0:T(8,128)S(1)}, u32[]{:S(2)}, u32[]{:S(2)}) collective-permute-start(f32[144,384]{1,0:T(8,128)S(1)} %reshape.1049), channel_id=1, source_target_pairs={{8,0},{16,8},{24,16},{32,24},{40,32},{48,40},{56,48},{64,56},{72,6... | collective-permute-start | bytes 663560 | tf_op jit(solution)/shard_map/ppermute | solution.py:13
  192.1 63.0 %all-to-all-start.3 = ((f32[32,136,128]{2,1,0:T(8,128)}), f32[32,136,128]{2,1,0:T(8,128)S(1)}, u32[]{:S(2)}, u32[]{:S(2)}) async-start(f32[32,136,128]{2,1,0:T(8,128)} %select_maximum_fusion), calls=%async_computation.3 | async-start | bytes 4456448 | tf_op jit(solution)/shard_map/all_to_all | solution.py:310
  256.6 20.4 %copy-start.19 = (f32[8,128,32]{1,2,0:T(8,128)}, f32[8,128,32]{1,2,0:T(8,128)S(1)}, u32[]{:S(2)}) copy-start(f32[8,128,32]{1,2,0:T(8,128)S(1)} %fusion) | copy-start | bytes 393220
  (24 other events, 44.8 us)

commit v4 on v0

--- a/solution.py
+++ b/solution.py
@@ -140,8 +140,10 @@
     to_top = jnp.concatenate(to_top, 1)
     to_low = jnp.concatenate(to_low, 1)
     count = to_top.shape[1]
-    send = jnp.zeros((band_count, row_count, count), to_top.dtype)
-    send = send.at[band_count - 1].set(to_top).at[0].set(to_low)
+    destination = lax.broadcasted_iota(jnp.int32, (band_count, row_count, count), 0)
+    send = jnp.where(
+        destination == band_count - 1, to_top[None], jnp.where(destination == 0, to_low[None], 0.0)
+    ).astype(to_top.dtype)
     got = lax.all_to_all(send, "space", 0, 0, tiled=True)
     flipped = jnp.flip(got.reshape(-1, count), 0).T
     cells = scenarios * levels * 3 * 3

time: 247 us -> 245 us (level)
  local copies, waits for them, and re-layouts: 62.1 us -> 58.9 us
    scatter x4 -> x0, local copies, waits for them, and re-layouts: 3.8 us -> none  [edge_columns(): send = send.at[band_count - 1].set(to_top).at[0].set(to_low)]
    unnamed x104 -> x116, local copies, waits for them, and re-layouts: 13.3 us -> 11.7 us
where the time goes in v4:
time: 245 us; the launch traced here: 242 us
  waiting for transfers between devices  74.5 us (30%)
  local copies, waits for them, and re-layouts  58.9 us (24%)
  starting transfers between devices  52.6 us (21%)
  other arithmetic  24.9 us (10%)
  blocking collectives  21 us (9%)
  matrix products  8 us (3%)
    all_to_all x1, waiting for transfers between devices, regrid(): got = lax.all_to_all(send, 'space', 0, 0, tiled=True)  52.1 us
    all_to_all x2, starting transfers between devices, edge_rows(): got = lax.all_to_all(send, 'space', 0, 0, tiled=True)  24.2 us
    all_to_all x1, blocking collectives, moments_of(): everyone = lax.all_to_all(copies, 'scen', 0, 0, tiled=True)  21 us
    all_to_all x2, starting transfers between devices, edge_columns(): got = lax.all_to_all(send, 'space', 0, 0, tiled=True)  14.8 us
    all_to_all x2, waiting for transfers between devices, edge_columns(): got = lax.all_to_all(send, 'space', 0, 0, tiled=True)  13.8 us
    unnamed x116, local copies, waits for them, and re-layouts  11.7 us
    all_to_all x1, starting transfers between devices, regrid(): got = lax.all_to_all(send, 'space', 0, 0, tiled=True)  10.9 us
    all_to_all x2, waiting for transfers between devices, edge_rows(): got = lax.all_to_all(send, 'space', 0, 0, tiled=True)  8.65 us
  transfers between devices with their start and end apart: 9, of which 4 were waited for; matrix products, arithmetic and copies ran while one was open for 9% of the time, Pallas kernels for 0%

profile of v4, /device:TPU:2, one launch (start us, length us, event | category | flops | bytes accessed | tf_op | source)
XLA Modules:
  0.0 241.9 jit_solution(2149904175202514924)
XLA Ops:
  0.6 1.2 copy.1179
  2.0 1.1 scatter-add.4
  4.6 2.7 %fusion.81 = (f32[1,8,6,12,384]{4,1,3,2,0:T(8,128)S(1)}, f32[8,6,12,384]{3,0,2,1:T(8,128)}, f32[8,6,12,384]{3,0,2,1:T(8,128)S(1)}, f32[1,8,6,12,384]{4,1,3,2,0:T(8,128)S(1)}) fusion(f32[2,8,6,12,384]{4,1,3,2,0:T(8,128)} %param.12), kind=kLoop, calls=%fused_computation.255 | loop fusion | bytes 5308416 | tf_op jit(solution)/shard_map/slice | solution.py:286
  7.3 1.5 fusion.88
  9.4 1.4 reshape_squeeze.13
  10.8 1.4 copy.902
  12.2 1.4 reshape_squeeze.12
  13.7 1.7 fusion.68
  15.3 2.4 rev.14
  17.7 1.7 copy.905
  19.5 1.8 all_to_all.32
  21.3 11.7 %all-to-all-start = ((f32[32,1,1152]{2,1,0:T(1,128)}), f32[32,1,1152]{2,1,0:T(1,128)}, u32[]{:S(2)}, u32[]{:S(2)}) async-start(f32[32,1,1152]{2,1,0:T(1,128)} %all_to_all.32), calls=%async_computation | async-start | bytes 294912 | tf_op jit(solution)/shard_map/all_to_all | solution.py:81
  33.0 1.6 fusion.84
  51.6 1.1 copy.911
  58.5 1.4 fusion.18
  62.1 9.8 %all-to-all-start.1 = ((f32[32,12,96]{2,1,0:T(8,128)}), f32[32,12,96]{2,1,0:T(8,128)S(1)}, u32[]{:S(2)}, u32[]{:S(2)}) async-start(f32[32,12,96]{2,1,0:T(8,128)} %select_select_fusion.1), calls=%async_computation.1 | async-start | bytes 524288 | tf_op jit(solution)/shard_map/all_to_all | solution.py:147
  73.7 1.7 pad_maximum_fusion.5
  76.7 6.8 %all-to-all-done.1 = f32[32,12,96]{2,1,0:T(8,128)S(1)} async-done(((f32[32,12,96]{2,1,0:T(8,128)}), f32[32,12,96]{2,1,0:T(8,128)S(1)}, u32[]{:S(2)}, u32[]{:S(2)}) %all-to-all-start.1) | async-done | bytes 147488 | tf_op jit(solution)/shard_map/all_to_all | solution.py:147
  94.7 12.6 %all-to-all-start.2 = ((f32[32,1,864]{2,1,0:T(1,128)}), f32[32,1,864]{2,1,0:T(1,128)S(1)}, u32[]{:S(2)}, u32[]{:S(2)}) async-start(f32[32,1,864]{2,1,0:T(1,128)} %all_to_all.33), calls=%async_computation.2 | async-start | bytes 229376 | tf_op jit(solution)/shard_map/all_to_all | solution.py:81
  107.7 8.6 %all-to-all-done.2 = f32[32,1,864]{2,1,0:T(1,128)S(1)} async-done(((f32[32,1,864]{2,1,0:T(1,128)}), f32[32,1,864]{2,1,0:T(1,128)S(1)}, u32[]{:S(2)}, u32[]{:S(2)}) %all-to-all-start.2) | async-done | bytes 110624 | tf_op jit(solution)/shard_map/all_to_all | solution.py:81
  120.0 1.4 fusion.6
  123.6 5.0 %all-to-all-start.3 = ((f32[32,1,864]{2,1,0:T(1,128)}), f32[32,1,864]{2,1,0:T(1,128)S(1)}, u32[]{:S(2)}, u32[]{:S(2)}) async-start(f32[32,1,864]{2,1,0:T(1,128)} %reshape.935), calls=%async_computation.3 | async-start | bytes 229376 | tf_op jit(solution)/shard_map/all_to_all | solution.py:147
  129.3 1.9 collective-permute-start.3
  131.2 7.0 %all-to-all-done.3 = f32[32,1,864]{2,1,0:T(1,128)S(1)} async-done(((f32[32,1,864]{2,1,0:T(1,128)}), f32[32,1,864]{2,1,0:T(1,128)S(1)}, u32[]{:S(2)}, u32[]{:S(2)}) %all-to-all-start.3) | async-done | bytes 110624 | tf_op jit(solution)/shard_map/all_to_all | solution.py:147
  143.9 1.8 gather_fusion
  145.7 4.9 %fusion.62 = f32[270,8,128]{2,1,0:T(8,128)S(1)} fusion(bf16[270,128,128]{2,1,0:T(8,128)(2,1)} %param.15, bf16[270,8,128]{2,1,0:T(8,128)(2,1)S(1)} %gather_fusion, pred[270]{0:T(512)(128)(4,1)S(1)} %copy-done.38), kind=kOutput, calls=%fused_computation.107 | convolution fusion | flops 71055360 | bytes 10506510 | tf_op jit(solution)/shard_map/btk,tkc->tbc/dot_general | solution.py:244
  150.6 2.0 fusion.28
  152.7 1.2 copy.994
  153.9 1.5 select_maximum_fusion
  155.4 10.9 %all-to-all-start.4 = ((f32[32,136,128]{2,1,0:T(8,128)}), f32[32,136,128]{2,1,0:T(8,128)S(1)}, u32[]{:S(2)}, u32[]{:S(2)}) async-start(f32[32,136,128]{2,1,0:T(8,128)} %select_maximum_fusion), calls=%async_computation.4 | async-start | bytes 4456448 | tf_op jit(solution)/shard_map/all_to_all | solution.py:262
  166.4 52.1 %all-to-all-done.4 = f32[32,136,128]{2,1,0:T(8,128)S(1)} async-done(((f32[32,136,128]{2,1,0:T(8,128)}), f32[32,136,128]{2,1,0:T(8,128)S(1)}, u32[]{:S(2)}, u32[]{:S(2)}) %all-to-all-start.4) | async-done | bytes 2228256 | tf_op jit(solution)/shard_map/all_to_all | solution.py:262
  220.0 21.0 %all_to_all.40 = f32[8,8,32,128]{3,2,1,0:T(8,128)S(1)} all-to-all(f32[8,8,32,128]{3,2,1,0:T(8,128)S(1)} %broadcast_in_dim.127), channel_id=1, replica_groups=mesh['space'=32,'scen'=8] {'scen'}, dimensions={0} | all-to-all | bytes 2097152 | tf_op jit(solution)/shard_map/all_to_all | solution.py:276
  (308 shorter events, 55.4 us)
Async XLA Ops:
  7.3 85.0 %copy-start = (f32[1,8,6,12,384]{4,1,3,2,0:T(8,128)}, f32[1,8,6,12,384]{4,1,3,2,0:T(8,128)S(1)}, u32[]{:S(2)}) copy-start(f32[1,8,6,12,384]{4,1,3,2,0:T(8,128)S(1)} %get-tuple-element.53) | copy-start | bytes 2654212
  17.7 18.3 %copy-start.32 = (s32[270]{0:T(512)S(1)}, s32[270]{0:T(512)}, u32[]{:S(2)}) copy-start(s32[270]{0:T(512)} %param.13) | copy-start | bytes 3244
  17.7 19.0 %copy-start.39 = (s32[270]{0:T(512)S(1)}, s32[270]{0:T(512)}, u32[]{:S(2)}) copy-start(s32[270]{0:T(512)} %param.14) | copy-start | bytes 3244
  21.3 23.7 %all-to-all-start = ((f32[32,1,1152]{2,1,0:T(1,128)}), f32[32,1,1152]{2,1,0:T(1,128)}, u32[]{:S(2)}, u32[]{:S(2)}) async-start(f32[32,1,1152]{2,1,0:T(1,128)} %all_to_all.32), calls=%async_computation | async-start | bytes 294912 | tf_op jit(solution)/shard_map/all_to_all | solution.py:81
  36.1 5.7 %copy-start.12 = (f32[8,3,12,1]{3,0,2,1:T(8,128)S(1)}, f32[8,3,12,1]{3,0,2,1:T(8,128)}, u32[]{:S(2)}) copy-start(f32[8,3,12,1]{3,0,2,1:T(8,128)} %get-tuple-element.81) | copy-start | bytes 3460
  36.1 5.9 %copy-start.24 = (f32[8,1,12,1]{3,0,2,1:T(8,128)S(1)}, f32[8,1,12,1]{3,0,2,1:T(8,128)}, u32[]{:S(2)}) copy-start(f32[8,1,12,1]{3,0,2,1:T(8,128)} %get-tuple-element.83) | copy-start | bytes 1156
  36.1 6.1 %copy-start.23 = (f32[8,1,12,1]{3,0,2,1:T(8,128)S(1)}, f32[8,1,12,1]{3,0,2,1:T(8,128)}, u32[]{:S(2)}) copy-start(f32[8,1,12,1]{3,0,2,1:T(8,128)} %get-tuple-element.84) | copy-start | bytes 1156
  36.1 6.2 %copy-start.22 = (f32[8,1,12,1]{3,0,2,1:T(8,128)S(1)}, f32[8,1,12,1]{3,0,2,1:T(8,128)}, u32[]{:S(2)}) copy-start(f32[8,1,12,1]{3,0,2,1:T(8,128)} %get-tuple-element.85) | copy-start | bytes 1156
  36.1 6.3 %copy-start.21 = (f32[8,1,12,1]{3,0,2,1:T(8,128)S(1)}, f32[8,1,12,1]{3,0,2,1:T(8,128)}, u32[]{:S(2)}) copy-start(f32[8,1,12,1]{3,0,2,1:T(8,128)} %get-tuple-element.86) | copy-start | bytes 1156
  36.1 6.4 %copy-start.20 = (f32[8,1,12,1]{3,0,2,1:T(8,128)S(1)}, f32[8,1,12,1]{3,0,2,1:T(8,128)}, u32[]{:S(2)}) copy-start(f32[8,1,12,1]{3,0,2,1:T(8,128)} %get-tuple-element.87) | copy-start | bytes 1156
  36.1 6.6 %copy-start.19 = (f32[8,1,12,1]{3,0,2,1:T(8,128)S(1)}, f32[8,1,12,1]{3,0,2,1:T(8,128)}, u32[]{:S(2)}) copy-start(f32[8,1,12,1]{3,0,2,1:T(8,128)} %get-tuple-element.88) | copy-start | bytes 1156
  36.1 7.4 %copy-start.11 = (f32[8,3,12,1]{3,0,2,1:T(8,128)S(1)}, f32[8,3,12,1]{3,0,2,1:T(8,128)}, u32[]{:S(2)}) copy-start(f32[8,3,12,1]{3,0,2,1:T(8,128)} %get-tuple-element.82) | copy-start | bytes 3460
  50.9 7.6 %copy-start.2 = (f32[1,8,6,12,1]{4,1,3,2,0:T(8,128)}, f32[1,8,6,12,1]{4,1,3,2,0:T(8,128)S(1)}, u32[]{:S(2)}) copy-start(f32[1,8,6,12,1]{4,1,3,2,0:T(8,128)S(1)} %copy.916) | copy-start | bytes 6916
  52.7 5.8 %copy-start.4 = (f32[1,8,6,12,1]{4,1,3,2,0:T(8,128)}, f32[1,8,6,12,1]{4,1,3,2,0:T(8,128)S(1)}, u32[]{:S(2)}) copy-start(f32[1,8,6,12,1]{4,1,3,2,0:T(8,128)S(1)} %copy.911) | copy-start | bytes 6916
  62.1 21.4 %all-to-all-start.1 = ((f32[32,12,96]{2,1,0:T(8,128)}), f32[32,12,96]{2,1,0:T(8,128)S(1)}, u32[]{:S(2)}, u32[]{:S(2)}) async-start(f32[32,12,96]{2,1,0:T(8,128)} %select_select_fusion.1), calls=%async_computation.1 | async-start | bytes 524288 | tf_op jit(solution)/shard_map/all_to_all | solution.py:147
  72.0 3.5 %copy-start.16 = (f32[48,384]{1,0:T(8,128)S(1)}, f32[48,384]{1,0:T(8,128)}, u32[]{:S(2)}) copy-start(f32[48,384]{1,0:T(8,128)} %reshape.884) | copy-start | bytes 221188
  72.9 2.6 %copy-start.6 = (f32[144,384]{1,0:T(8,128)S(1)}, f32[144,384]{1,0:T(8,128)}, u32[]{:S(2)}) copy-start(f32[144,384]{1,0:T(8,128)} %reshape.883) | copy-start | bytes 663556
  75.5 9.3 %collective-permute-start.1 = (f32[192,384]{1,0:T(8,128)}, f32[192,384]{1,0:T(8,128)}, u32[]{:S(2)}, u32[]{:S(2)}) collective-permute-start(f32[192,384]{1,0:T(8,128)} %pad_maximum_fusion.5), channel_id=1, source_target_pairs={{8,0},{16,8},{24,16},{32,24},{40,32},{48,40},{56,48},{64,56},{72,6... | collective-permute-start | bytes 884744 | tf_op jit(solution)/shard_map/ppermute | solution.py:13
  76.3 11.4 %collective-permute-start = (f32[192,384]{1,0:T(8,128)}, f32[192,384]{1,0:T(8,128)}, u32[]{:S(2)}, u32[]{:S(2)}) collective-permute-start(f32[192,384]{1,0:T(8,128)} %pad_maximum_fusion.4), channel_id=1, source_target_pairs={{248,0},{0,8},{8,16},{16,24},{24,32},{32,40},{40,48},{48,56},{56,6... | collective-permute-start | bytes 884744 | tf_op jit(solution)/shard_map/ppermute | solution.py:13
  85.9 6.5 %copy-start.7 = (f32[8,6,384]{2,0,1:T(8,128)}, f32[8,6,384]{2,0,1:T(8,128)S(1)}, u32[]{:S(2)}) copy-start(f32[8,6,384]{2,0,1:T(8,128)S(1)} %copy.1125) | copy-start | bytes 221188
  88.9 3.5 %copy-start.9 = (f32[8,6,384]{2,0,1:T(8,128)}, f32[8,6,384]{2,0,1:T(8,128)S(1)}, u32[]{:S(2)}) copy-start(f32[8,6,384]{2,0,1:T(8,128)S(1)} %copy.1126) | copy-start | bytes 221188
  90.0 1.8 copy-start.14
  90.0 1.9 copy-start.17
  93.2 14.0 %copy-start.33 = (s32[270]{0:T(512)S(1)}, s32[270]{0:T(512)}, u32[]{:S(2)}) copy-start(s32[270]{0:T(512)} %param.13) | copy-start | bytes 3244
  94.7 21.7 %all-to-all-start.2 = ((f32[32,1,864]{2,1,0:T(1,128)}), f32[32,1,864]{2,1,0:T(1,128)S(1)}, u32[]{:S(2)}, u32[]{:S(2)}) async-start(f32[32,1,864]{2,1,0:T(1,128)} %all_to_all.33), calls=%async_computation.2 | async-start | bytes 229376 | tf_op jit(solution)/shard_map/all_to_all | solution.py:81
  123.6 14.6 %all-to-all-start.3 = ((f32[32,1,864]{2,1,0:T(1,128)}), f32[32,1,864]{2,1,0:T(1,128)S(1)}, u32[]{:S(2)}, u32[]{:S(2)}) async-start(f32[32,1,864]{2,1,0:T(1,128)} %reshape.935), calls=%async_computation.3 | async-start | bytes 229376 | tf_op jit(solution)/shard_map/all_to_all | solution.py:147
  128.9 11.3 %collective-permute-start.2 = (f32[144,384]{1,0:T(8,128)S(1)}, f32[144,384]{1,0:T(8,128)S(1)}, u32[]{:S(2)}, u32[]{:S(2)}) collective-permute-start(f32[144,384]{1,0:T(8,128)S(1)} %reshape.898), channel_id=1, source_target_pairs={{248,0},{0,8},{8,16},{16,24},{24,32},{32,40},{40,48},{48,56},{56,6... | collective-permute-start | bytes 663560 | tf_op jit(solution)/shard_map/ppermute | solution.py:13
  129.3 11.0 %collective-permute-start.3 = (f32[144,384]{1,0:T(8,128)S(1)}, f32[144,384]{1,0:T(8,128)S(1)}, u32[]{:S(2)}, u32[]{:S(2)}) collective-permute-start(f32[144,384]{1,0:T(8,128)S(1)} %reshape.902), channel_id=1, source_target_pairs={{8,0},{16,8},{24,16},{32,24},{40,32},{48,40},{56,48},{64,56},{72,6... | collective-permute-start | bytes 663560 | tf_op jit(solution)/shard_map/ppermute | solution.py:13
  142.8 2.9 %copy-start.38 = (pred[270]{0:T(512)(128)(4,1)S(1)}, pred[270]{0:T(512)(128)(4,1)}, u32[]{:S(2)}) copy-start(pred[270]{0:T(512)(128)(4,1)} %compare_and_fusion) | copy-start | bytes 814
  145.7 4.9 %copy-start.30 = (s32[270]{0:T(512)S(1)}, s32[270]{0:T(512)}, u32[]{:S(2)}) copy-start(s32[270]{0:T(512)} %copy-done.29) | copy-start | bytes 3244
  155.4 63.0 %all-to-all-start.4 = ((f32[32,136,128]{2,1,0:T(8,128)}), f32[32,136,128]{2,1,0:T(8,128)S(1)}, u32[]{:S(2)}, u32[]{:S(2)}) async-start(f32[32,136,128]{2,1,0:T(8,128)} %select_maximum_fusion), calls=%async_computation.4 | async-start | bytes 4456448 | tf_op jit(solution)/shard_map/all_to_all | solution.py:262
  219.9 21.1 %copy-start.13 = (f32[8,128,32]{1,2,0:T(8,128)}, f32[8,128,32]{1,2,0:T(8,128)S(1)}, u32[]{:S(2)}) copy-start(f32[8,128,32]{1,2,0:T(8,128)S(1)} %fusion) | copy-start | bytes 393220
  (17 other events, 18.3 us)

commit v5 on v4

--- a/solution.py
+++ b/solution.py
@@ -77,10 +77,13 @@
     top = jnp.concatenate(top, 0)
     low = jnp.concatenate(low, 0)
     send = jnp.where(position == band_count - 1, top, jnp.where(position == 0, low, 0.0))
-    send = jnp.flip(send.T, 0).reshape(band_count, -1)
+    count = top.shape[0]
+    send = jnp.flip(send.T.reshape(band_count, -1, count), 0).reshape(band_count, -1)
     got = lax.all_to_all(send, "space", 0, 0, tiled=True)
-    count = top.shape[0]
-    return got[band_count - 1].reshape(-1, count), got[0].reshape(-1, count)
+    return (
+        jnp.flip(got[band_count - 1].reshape(-1, count), 0),
+        jnp.flip(got[0].reshape(-1, count), 0),
+    )
 
 
 def column_halos(tracer, east_wind, north_wind, position, band_count, edge_wind, faces_known):
@@ -137,15 +140,15 @@
         to_low.append(
             jnp.moveaxis(east_wind[:, 1::2, :, width_cells - 1], 2, 0).reshape(row_count, -1)
         )
-    to_top = jnp.concatenate(to_top, 1)
-    to_low = jnp.concatenate(to_low, 1)
+    to_top = jnp.flip(jnp.concatenate(to_top, 1), 0)
+    to_low = jnp.flip(jnp.concatenate(to_low, 1), 0)
     count = to_top.shape[1]
     destination = lax.broadcasted_iota(jnp.int32, (band_count, row_count, count), 0)
     send = jnp.where(
         destination == band_count - 1, to_top[None], jnp.where(destination == 0, to_low[None], 0.0)
     ).astype(to_top.dtype)
     got = lax.all_to_all(send, "space", 0, 0, tiled=True)
-    flipped = jnp.flip(got.reshape(-1, count), 0).T
+    flipped = jnp.flip(got, 0).reshape(-1, count).T
     cells = scenarios * levels * 3 * 3
     layers = flipped[:cells].reshape(scenarios, levels, 3, 3, band_count * row_count)
     wind = None

time: 245 us -> 249 us (1.016)
    rev x6 -> x12, local copies, waits for them, and re-layouts: 4.73 us -> 2.21 us  [the longest x2 1.69 us: edge_rows(): jnp.flip(send.T.reshape(band_count, -1, count), 0).reshape(band_count, -1)]
    unnamed x116 -> x110, local copies, waits for them, and re-layouts: 11.7 us -> 13.5 us
  transfers between devices with their start and end apart: 9 -> 9, of which waited for: 4 -> 4; matrix products, arithmetic and copies ran while one was open for 9% -> 10% of each run, Pallas kernels for 0% -> 0%
where the time goes in v5:
time: 249 us; the launch traced here: 246 us
  waiting for transfers between devices  72.9 us (29%)
  local copies, waits for them, and re-layouts  61.3 us (25%)
  starting transfers between devices  54.7 us (22%)
  other arithmetic  25.9 us (10%)
  blocking collectives  21.1 us (8%)
  matrix products  7.99 us (3%)
    all_to_all x1, waiting for transfers between devices, regrid(): got = lax.all_to_all(send, 'space', 0, 0, tiled=True)  52 us
    all_to_all x2, starting transfers between devices, edge_rows(): got = lax.all_to_all(send, 'space', 0, 0, tiled=True)  26.2 us
    all_to_all x1, blocking collectives, moments_of(): everyone = lax.all_to_all(copies, 'scen', 0, 0, tiled=True)  21.1 us
    all_to_all x2, starting transfers between devices, edge_columns(): got = lax.all_to_all(send, 'space', 0, 0, tiled=True)  14.8 us
    unnamed x110, local copies, waits for them, and re-layouts  13.5 us
    all_to_all x2, waiting for transfers between devices, edge_columns(): got = lax.all_to_all(send, 'space', 0, 0, tiled=True)  11.3 us
    all_to_all x1, starting transfers between devices, regrid(): got = lax.all_to_all(send, 'space', 0, 0, tiled=True)  11 us
    all_to_all x2, waiting for transfers between devices, edge_rows(): got = lax.all_to_all(send, 'space', 0, 0, tiled=True)  9.51 us
  transfers between devices with their start and end apart: 9, of which 4 were waited for; matrix products, arithmetic and copies ran while one was open for 10% of the time, Pallas kernels for 0%

profile of v5, /device:TPU:2, one launch (start us, length us, event | category | flops | bytes accessed | tf_op | source)
XLA Modules:
  0.0 245.8 jit_solution(12278291766906719667)
XLA Ops:
  0.6 1.2 copy.1197
  4.6 1.8 fusion.81
  8.6 1.4 reshape_squeeze.19
  10.0 1.4 copy.918
  11.4 1.4 reshape_squeeze.18
  12.8 1.7 fusion.68
  14.5 1.7 copy.921
  16.2 1.6 reshape.897
  17.8 1.7 rev.36
  19.5 1.9 all_to_all.32
  21.4 11.7 %all-to-all-start = ((f32[32,1,1152]{2,1,0:T(1,128)}), f32[32,1,1152]{2,1,0:T(1,128)}, u32[]{:S(2)}, u32[]{:S(2)}) async-start(f32[32,1,1152]{2,1,0:T(1,128)} %all_to_all.32), calls=%async_computation | async-start | bytes 294912 | tf_op jit(solution)/shard_map/all_to_all | solution.py:82
  33.1 1.6 fusion.84
  52.1 1.1 copy.927
  59.0 1.4 fusion.18
  63.3 9.8 %all-to-all-start.1 = ((f32[32,12,96]{2,1,0:T(8,128)}), f32[32,12,96]{2,1,0:T(8,128)S(1)}, u32[]{:S(2)}, u32[]{:S(2)}) async-start(f32[32,12,96]{2,1,0:T(8,128)} %select_select_fusion.1), calls=%async_computation.1 | async-start | bytes 524288 | tf_op jit(solution)/shard_map/all_to_all | solution.py:150
  76.5 1.7 pad_maximum_fusion.5
  78.3 1.7 pad_maximum_fusion.4
  80.4 4.3 %all-to-all-done.1 = f32[32,12,96]{2,1,0:T(8,128)S(1)} async-done(((f32[32,12,96]{2,1,0:T(8,128)}), f32[32,12,96]{2,1,0:T(8,128)S(1)}, u32[]{:S(2)}, u32[]{:S(2)}) %all-to-all-start.1) | async-done | bytes 147488 | tf_op jit(solution)/shard_map/all_to_all | solution.py:150
  95.4 14.5 %all-to-all-start.2 = ((f32[32,1,864]{2,1,0:T(1,128)}), f32[32,1,864]{2,1,0:T(1,128)S(1)}, u32[]{:S(2)}, u32[]{:S(2)}) async-start(f32[32,1,864]{2,1,0:T(1,128)} %all_to_all.33), calls=%async_computation.2 | async-start | bytes 229376 | tf_op jit(solution)/shard_map/all_to_all | solution.py:82
  110.0 9.5 %all-to-all-done.2 = f32[32,1,864]{2,1,0:T(1,128)S(1)} async-done(((f32[32,1,864]{2,1,0:T(1,128)}), f32[32,1,864]{2,1,0:T(1,128)S(1)}, u32[]{:S(2)}, u32[]{:S(2)}) %all-to-all-start.2) | async-done | bytes 110624 | tf_op jit(solution)/shard_map/all_to_all | solution.py:82
  123.8 1.4 fusion.6
  127.5 5.0 %all-to-all-start.3 = ((f32[32,1,864]{2,1,0:T(1,128)}), f32[32,1,864]{2,1,0:T(1,128)S(1)}, u32[]{:S(2)}, u32[]{:S(2)}) async-start(f32[32,1,864]{2,1,0:T(1,128)} %reshape.959), calls=%async_computation.3 | async-start | bytes 229376 | tf_op jit(solution)/shard_map/all_to_all | solution.py:150
  133.2 1.9 collective-permute-start.3
  135.1 7.0 %all-to-all-done.3 = f32[32,1,864]{2,1,0:T(1,128)S(1)} async-done(((f32[32,1,864]{2,1,0:T(1,128)}), f32[32,1,864]{2,1,0:T(1,128)S(1)}, u32[]{:S(2)}, u32[]{:S(2)}) %all-to-all-start.3) | async-done | bytes 110624 | tf_op jit(solution)/shard_map/all_to_all | solution.py:150
  147.7 1.8 gather_fusion
  149.5 4.9 %fusion.62 = f32[270,8,128]{2,1,0:T(8,128)S(1)} fusion(bf16[270,128,128]{2,1,0:T(8,128)(2,1)} %param.15, bf16[270,8,128]{2,1,0:T(8,128)(2,1)S(1)} %gather_fusion, pred[270]{0:T(512)(128)(4,1)S(1)} %compare_and_fusion), kind=kOutput, calls=%fused_computation.107 | convolution fusion | flops 71055360 | bytes 10506510 | tf_op jit(solution)/shard_map/btk,tkc->tbc/dot_general | solution.py:247
  154.4 2.0 fusion.28
  156.5 1.2 copy.1012
  157.7 1.6 select_maximum_fusion
  159.3 11.0 %all-to-all-start.4 = ((f32[32,136,128]{2,1,0:T(8,128)}), f32[32,136,128]{2,1,0:T(8,128)S(1)}, u32[]{:S(2)}, u32[]{:S(2)}) async-start(f32[32,136,128]{2,1,0:T(8,128)} %select_maximum_fusion), calls=%async_computation.4 | async-start | bytes 4456448 | tf_op jit(solution)/shard_map/all_to_all | solution.py:265
  170.3 52.0 %all-to-all-done.4 = f32[32,136,128]{2,1,0:T(8,128)S(1)} async-done(((f32[32,136,128]{2,1,0:T(8,128)}), f32[32,136,128]{2,1,0:T(8,128)S(1)}, u32[]{:S(2)}, u32[]{:S(2)}) %all-to-all-start.4) | async-done | bytes 2228256 | tf_op jit(solution)/shard_map/all_to_all | solution.py:265
  223.9 21.1 %all_to_all.40 = f32[8,8,32,128]{3,2,1,0:T(8,128)S(1)} all-to-all(f32[8,8,32,128]{3,2,1,0:T(8,128)S(1)} %broadcast_in_dim.81), channel_id=1, replica_groups=mesh['space'=32,'scen'=8] {'scen'}, dimensions={0} | all-to-all | bytes 2097152 | tf_op jit(solution)/shard_map/all_to_all | solution.py:279
  (318 shorter events, 59.8 us)
Async XLA Ops:
  6.4 87.0 %copy-start = (f32[1,8,6,12,384]{4,1,3,2,0:T(8,128)}, f32[1,8,6,12,384]{4,1,3,2,0:T(8,128)S(1)}, u32[]{:S(2)}) copy-start(f32[1,8,6,12,384]{4,1,3,2,0:T(8,128)S(1)} %get-tuple-element.53) | copy-start | bytes 2654212
  19.5 16.7 %copy-start.28 = (s32[270]{0:T(512)S(1)}, s32[270]{0:T(512)}, u32[]{:S(2)}) copy-start(s32[270]{0:T(512)} %param.13) | copy-start | bytes 3244
  19.5 17.4 %copy-start.33 = (s32[270]{0:T(512)S(1)}, s32[270]{0:T(512)}, u32[]{:S(2)}) copy-start(s32[270]{0:T(512)} %param.14) | copy-start | bytes 3244
  21.4 23.7 %all-to-all-start = ((f32[32,1,1152]{2,1,0:T(1,128)}), f32[32,1,1152]{2,1,0:T(1,128)}, u32[]{:S(2)}, u32[]{:S(2)}) async-start(f32[32,1,1152]{2,1,0:T(1,128)} %all_to_all.32), calls=%async_computation | async-start | bytes 294912 | tf_op jit(solution)/shard_map/all_to_all | solution.py:82
  36.2 5.7 %copy-start.8 = (f32[8,3,12,1]{3,0,2,1:T(8,128)S(1)}, f32[8,3,12,1]{3,0,2,1:T(8,128)}, u32[]{:S(2)}) copy-start(f32[8,3,12,1]{3,0,2,1:T(8,128)} %get-tuple-element.81) | copy-start | bytes 3460
  36.2 5.9 %copy-start.21 = (f32[8,1,12,1]{3,0,2,1:T(8,128)S(1)}, f32[8,1,12,1]{3,0,2,1:T(8,128)}, u32[]{:S(2)}) copy-start(f32[8,1,12,1]{3,0,2,1:T(8,128)} %get-tuple-element.83) | copy-start | bytes 1156
  36.2 6.0 %copy-start.20 = (f32[8,1,12,1]{3,0,2,1:T(8,128)S(1)}, f32[8,1,12,1]{3,0,2,1:T(8,128)}, u32[]{:S(2)}) copy-start(f32[8,1,12,1]{3,0,2,1:T(8,128)} %get-tuple-element.84) | copy-start | bytes 1156
  36.2 6.2 %copy-start.19 = (f32[8,1,12,1]{3,0,2,1:T(8,128)S(1)}, f32[8,1,12,1]{3,0,2,1:T(8,128)}, u32[]{:S(2)}) copy-start(f32[8,1,12,1]{3,0,2,1:T(8,128)} %get-tuple-element.85) | copy-start | bytes 1156
  36.2 6.3 %copy-start.18 = (f32[8,1,12,1]{3,0,2,1:T(8,128)S(1)}, f32[8,1,12,1]{3,0,2,1:T(8,128)}, u32[]{:S(2)}) copy-start(f32[8,1,12,1]{3,0,2,1:T(8,128)} %get-tuple-element.86) | copy-start | bytes 1156
  36.3 6.4 %copy-start.17 = (f32[8,1,12,1]{3,0,2,1:T(8,128)S(1)}, f32[8,1,12,1]{3,0,2,1:T(8,128)}, u32[]{:S(2)}) copy-start(f32[8,1,12,1]{3,0,2,1:T(8,128)} %get-tuple-element.87) | copy-start | bytes 1156
  36.3 6.6 %copy-start.16 = (f32[8,1,12,1]{3,0,2,1:T(8,128)S(1)}, f32[8,1,12,1]{3,0,2,1:T(8,128)}, u32[]{:S(2)}) copy-start(f32[8,1,12,1]{3,0,2,1:T(8,128)} %get-tuple-element.88) | copy-start | bytes 1156
  36.3 7.4 %copy-start.7 = (f32[8,3,12,1]{3,0,2,1:T(8,128)S(1)}, f32[8,3,12,1]{3,0,2,1:T(8,128)}, u32[]{:S(2)}) copy-start(f32[8,3,12,1]{3,0,2,1:T(8,128)} %get-tuple-element.82) | copy-start | bytes 3460
  51.3 7.6 %copy-start.2 = (f32[1,8,6,12,1]{4,1,3,2,0:T(8,128)}, f32[1,8,6,12,1]{4,1,3,2,0:T(8,128)S(1)}, u32[]{:S(2)}) copy-start(f32[1,8,6,12,1]{4,1,3,2,0:T(8,128)S(1)} %copy.932) | copy-start | bytes 6916
  53.2 5.8 %copy-start.4 = (f32[1,8,6,12,1]{4,1,3,2,0:T(8,128)}, f32[1,8,6,12,1]{4,1,3,2,0:T(8,128)S(1)}, u32[]{:S(2)}) copy-start(f32[1,8,6,12,1]{4,1,3,2,0:T(8,128)S(1)} %copy.927) | copy-start | bytes 6916
  60.7 1.8 copy-start.30
  63.3 21.4 %all-to-all-start.1 = ((f32[32,12,96]{2,1,0:T(8,128)}), f32[32,12,96]{2,1,0:T(8,128)S(1)}, u32[]{:S(2)}, u32[]{:S(2)}) async-start(f32[32,12,96]{2,1,0:T(8,128)} %select_select_fusion.1), calls=%async_computation.1 | async-start | bytes 524288 | tf_op jit(solution)/shard_map/all_to_all | solution.py:150
  73.8 2.7 %copy-start.13 = (f32[48,384]{1,0:T(8,128)S(1)}, f32[48,384]{1,0:T(8,128)}, u32[]{:S(2)}) copy-start(f32[48,384]{1,0:T(8,128)} %reshape.912) | copy-start | bytes 221188
  73.9 4.4 %copy-start.12 = (f32[48,384]{1,0:T(8,128)S(1)}, f32[48,384]{1,0:T(8,128)}, u32[]{:S(2)}) copy-start(f32[48,384]{1,0:T(8,128)} %reshape.903) | copy-start | bytes 221188
  78.2 7.7 %collective-permute-start.1 = (f32[192,384]{1,0:T(8,128)}, f32[192,384]{1,0:T(8,128)}, u32[]{:S(2)}, u32[]{:S(2)}) collective-permute-start(f32[192,384]{1,0:T(8,128)} %pad_maximum_fusion.5), channel_id=1, source_target_pairs={{8,0},{16,8},{24,16},{32,24},{40,32},{48,40},{56,48},{64,56},{72,6... | collective-permute-start | bytes 884744 | tf_op jit(solution)/shard_map/ppermute | solution.py:13
  80.0 8.8 %collective-permute-start = (f32[192,384]{1,0:T(8,128)}, f32[192,384]{1,0:T(8,128)}, u32[]{:S(2)}, u32[]{:S(2)}) collective-permute-start(f32[192,384]{1,0:T(8,128)} %pad_maximum_fusion.4), channel_id=1, source_target_pairs={{248,0},{0,8},{8,16},{16,24},{24,32},{32,40},{40,48},{48,56},{56,6... | collective-permute-start | bytes 884744 | tf_op jit(solution)/shard_map/ppermute | solution.py:13
  90.9 1.8 copy-start.11
  91.0 1.8 copy-start.10
  91.0 1.8 copy-start.15
  91.0 1.9 copy-start.14
  94.2 15.7 %copy-start.29 = (s32[270]{0:T(512)S(1)}, s32[270]{0:T(512)}, u32[]{:S(2)}) copy-start(s32[270]{0:T(512)} %param.13) | copy-start | bytes 3244
  95.4 24.1 %all-to-all-start.2 = ((f32[32,1,864]{2,1,0:T(1,128)}), f32[32,1,864]{2,1,0:T(1,128)S(1)}, u32[]{:S(2)}, u32[]{:S(2)}) async-start(f32[32,1,864]{2,1,0:T(1,128)} %all_to_all.33), calls=%async_computation.2 | async-start | bytes 229376 | tf_op jit(solution)/shard_map/all_to_all | solution.py:82
  127.5 14.6 %all-to-all-start.3 = ((f32[32,1,864]{2,1,0:T(1,128)}), f32[32,1,864]{2,1,0:T(1,128)S(1)}, u32[]{:S(2)}, u32[]{:S(2)}) async-start(f32[32,1,864]{2,1,0:T(1,128)} %reshape.959), calls=%async_computation.3 | async-start | bytes 229376 | tf_op jit(solution)/shard_map/all_to_all | solution.py:150
  132.8 11.2 %collective-permute-start.2 = (f32[144,384]{1,0:T(8,128)S(1)}, f32[144,384]{1,0:T(8,128)S(1)}, u32[]{:S(2)}, u32[]{:S(2)}) collective-permute-start(f32[144,384]{1,0:T(8,128)S(1)} %reshape.920), channel_id=1, source_target_pairs={{248,0},{0,8},{8,16},{16,24},{24,32},{32,40},{40,48},{48,56},{56,6... | collective-permute-start | bytes 663560 | tf_op jit(solution)/shard_map/ppermute | solution.py:13
  133.2 10.9 %collective-permute-start.3 = (f32[144,384]{1,0:T(8,128)S(1)}, f32[144,384]{1,0:T(8,128)S(1)}, u32[]{:S(2)}, u32[]{:S(2)}) collective-permute-start(f32[144,384]{1,0:T(8,128)S(1)} %reshape.926), channel_id=1, source_target_pairs={{8,0},{16,8},{24,16},{32,24},{40,32},{48,40},{56,48},{64,56},{72,6... | collective-permute-start | bytes 663560 | tf_op jit(solution)/shard_map/ppermute | solution.py:13
  149.5 4.9 %copy-start.26 = (s32[270]{0:T(512)S(1)}, s32[270]{0:T(512)}, u32[]{:S(2)}) copy-start(s32[270]{0:T(512)} %copy-done.25) | copy-start | bytes 3244
  159.3 63.1 %all-to-all-start.4 = ((f32[32,136,128]{2,1,0:T(8,128)}), f32[32,136,128]{2,1,0:T(8,128)S(1)}, u32[]{:S(2)}, u32[]{:S(2)}) async-start(f32[32,136,128]{2,1,0:T(8,128)} %select_maximum_fusion), calls=%async_computation.4 | async-start | bytes 4456448 | tf_op jit(solution)/shard_map/all_to_all | solution.py:265
  223.8 21.2 %copy-start.9 = (f32[8,128,32]{1,2,0:T(8,128)}, f32[8,128,32]{1,2,0:T(8,128)S(1)}, u32[]{:S(2)}) copy-start(f32[8,128,32]{1,2,0:T(8,128)S(1)} %fusion) | copy-start | bytes 393220
  (11 other events, 12.1 us)

commit v6 on v4

--- a/solution.py
+++ b/solution.py
@@ -66,7 +66,7 @@
     return jnp.concatenate(parts, 0)
 
 
-def edge_rows(tracer, north_wind, position, band_count, with_wind):
+def edge_rows(tracer, north_wind, position, band_count, with_wind, rider=None):
     row_count = tracer.shape[3]
     width_cells = tracer.shape[4]
     top = [tracer[:, :, 0::2, row_count - 3 :, :].reshape(-1, width_cells)]
@@ -78,14 +78,21 @@
     low = jnp.concatenate(low, 0)
     send = jnp.where(position == band_count - 1, top, jnp.where(position == 0, low, 0.0))
     send = jnp.flip(send.T, 0).reshape(band_count, -1)
+    width = send.shape[1]
+    if rider is not None:
+        send = jnp.concatenate([send, rider.astype(send.dtype)], 1)
     got = lax.all_to_all(send, "space", 0, 0, tiled=True)
     count = top.shape[0]
-    return got[band_count - 1].reshape(-1, count), got[0].reshape(-1, count)
-
-
-def column_halos(tracer, east_wind, north_wind, position, band_count, edge_wind, faces_known):
+    rode = got[:, width:]
+    got = got[:, :width]
+    return got[band_count - 1].reshape(-1, count), got[0].reshape(-1, count), rode
+
+
+def column_halos(
+    tracer, east_wind, north_wind, position, band_count, edge_wind, faces_known, rider=None
+):
     scenarios, levels, _, row_count, width_cells = tracer.shape
-    top, low = edge_rows(tracer, north_wind, position, band_count, edge_wind is None)
+    top, low, rode = edge_rows(tracer, north_wind, position, band_count, edge_wind is None, rider)
     cells = scenarios * levels * 3 * 3
     top_layers = top[:, :cells].reshape(row_count, scenarios, levels, 3, 3)
     low_layers = low[:, :cells].reshape(row_count, scenarios, levels, 3, 3)
@@ -125,7 +132,7 @@
             -1,
         )
         faces_known = 0.5 * (speeds[..., :-1] + speeds[..., 1:])
-    return (padded, faces_known, edge_wind)
+    return (padded, faces_known, edge_wind, rode)
 
 
 def edge_columns(tracer, east_wind, position, band_count, with_wind):
@@ -234,7 +241,18 @@
     return (padded, faces_known, row_wind)
 
 
-def regrid(tracer, tile_source, tile_target, intersection, band_count):
+def slot_plan(tile_target, band_count):
+    target_band = tile_target // TGT_DEV
+    target_block = tile_target % TGT_DEV
+    band_hot = (target_band[:, None] == jnp.arange(band_count)[None, :]).astype(jnp.int32)
+    rank = jnp.sum((jnp.cumsum(band_hot, 0) - band_hot) * band_hot, 1)
+    slot = jnp.where(rank < SLOTS, target_band * SLOTS + rank, -1)
+    slot_hot = (slot[None, :] == jnp.arange(band_count * SLOTS)[:, None]).astype(jnp.float32)
+    slot_block = jnp.sum(slot_hot * target_block[None, :].astype(jnp.float32), 1)
+    return slot_hot, slot_block.reshape(band_count, SLOTS)
+
+
+def regrid(tracer, tile_source, slot_hot, got_block, intersection, band_count):
     scenarios = tracer.shape[0]
     levels = tracer.shape[1]
     batch_rows = scenarios * levels
@@ -244,27 +262,15 @@
     partial_value = jnp.einsum(
         "btk,tkc->tbc", chosen, intersection, preferred_element_type=jnp.float32
     )
-    target_band = tile_target // TGT_DEV
-    target_block = tile_target % TGT_DEV
-    band_hot = (target_band[:, None] == jnp.arange(band_count)[None, :]).astype(jnp.int32)
-    rank = jnp.sum((jnp.cumsum(band_hot, 0) - band_hot) * band_hot, 1)
-    slot = jnp.where(rank < SLOTS, target_band * SLOTS + rank, -1)
-    slot_hot = (slot[None, :] == jnp.arange(band_count * SLOTS)[:, None]).astype(jnp.float32)
     slotted = jnp.einsum(
         "st,tbc->sbc", slot_hot, partial_value, precision=lax.Precision.HIGHEST
     )
-    slot_block = jnp.sum(slot_hot * target_block[None, :].astype(jnp.float32), 1)
-    index_rows = jnp.zeros((band_count, 8, block_cells), jnp.float32)
-    index_rows = index_rows.at[:, 0, :SLOTS].set(slot_block.reshape(band_count, SLOTS))
-    send = jnp.concatenate(
-        [slotted.reshape(band_count, SLOTS * batch_rows, block_cells), index_rows], 1
-    )
+    send = slotted.reshape(band_count, SLOTS * batch_rows, block_cells)
     got = lax.all_to_all(send, "space", 0, 0, tiled=True)
-    values = got[:, : SLOTS * batch_rows].reshape(band_count * SLOTS, batch_rows, block_cells)
-    got_block = got[:, SLOTS * batch_rows, :SLOTS].reshape(-1)
-    block_hot = (got_block[None, :] == jnp.arange(TGT_DEV)[:, None].astype(jnp.float32)).astype(
-        jnp.float32
-    )
+    values = got.reshape(band_count * SLOTS, batch_rows, block_cells)
+    block_hot = (
+        got_block.reshape(-1)[None, :] == jnp.arange(TGT_DEV)[:, None].astype(jnp.float32)
+    ).astype(jnp.float32)
     summed = jnp.einsum("ks,sbc->bkc", block_hot, values, precision=lax.Precision.HIGHEST)
     return summed.reshape(scenarios, levels, TGT_DEV, block_cells)
 
@@ -288,16 +294,27 @@
     row_wind = None
     cx = None
     cy = None
+    slot_hot, slot_block = slot_plan(tile_target, band_count)
+    got_block = None
     for step_number in range(2):
-        padded, cx, edge_wind = column_halos(
-            tracer, east_wind, north_wind, position, band_count, edge_wind, cx
-        )
+        padded, cx, edge_wind, rode = column_halos(
+            tracer,
+            east_wind,
+            north_wind,
+            position,
+            band_count,
+            edge_wind,
+            cx,
+            slot_block if step_number == 0 else None,
+        )
+        if step_number == 0:
+            got_block = rode
         tracer = parabola_sweep(padded, cx, 4)
         padded, cy, row_wind = row_halos(
             tracer, east_wind, north_wind, position, band_count, row_wind, cy
         )
         tracer = parabola_sweep(padded, cy, 3)
-    regridded = regrid(tracer, tile_source, tile_target, intersection, band_count)
+    regridded = regrid(tracer, tile_source, slot_hot, got_block, intersection, band_count)
     ensemble_moments = moments_of(regridded)
     return (tracer, regridded, ensemble_moments)
 

time: 245 us -> 247 us (level)
  local copies, waits for them, and re-layouts: 58.9 us -> 65.2 us
  waiting for transfers between devices: 74.5 us -> 71.6 us
    all_to_all x1, waiting for transfers between devices: 52.1 us -> 48.6 us  [regrid(): got = lax.all_to_all(send, 'space', 0, 0, tiled=True)]
    unnamed x116 -> x99, local copies, waits for them, and re-layouts: 11.7 us -> 12.7 us
  transfers between devices with their start and end apart: 9 -> 9, of which waited for: 4 -> 4; matrix products, arithmetic and copies ran while one was open for 9% -> 10% of each run, Pallas kernels for 0% -> 0%
where the time goes in v6:
time: 247 us; the launch traced here: 243 us
  waiting for transfers between devices  71.6 us (29%)
  local copies, waits for them, and re-layouts  65.2 us (26%)
  starting transfers between devices  52.6 us (21%)
  other arithmetic  23.8 us (10%)
  blocking collectives  20.4 us (8%)
  matrix products  7.98 us (3%)
    all_to_all x1, waiting for transfers between devices, regrid(): got = lax.all_to_all(send, 'space', 0, 0, tiled=True)  48.6 us
    all_to_all x2, starting transfers between devices, edge_rows(): got = lax.all_to_all(send, 'space', 0, 0, tiled=True)  24.2 us
    all_to_all x1, blocking collectives, moments_of(): everyone = lax.all_to_all(copies, 'scen', 0, 0, tiled=True)  20.4 us
    all_to_all x2, starting transfers between devices, edge_columns(): got = lax.all_to_all(send, 'space', 0, 0, tiled=True)  14.8 us
    all_to_all x2, waiting for transfers between devices, edge_columns(): got = lax.all_to_all(send, 'space', 0, 0, tiled=True)  13.8 us
    unnamed x99, local copies, waits for them, and re-layouts  12.7 us
    all_to_all x1, starting transfers between devices, regrid(): got = lax.all_to_all(send, 'space', 0, 0, tiled=True)  10.9 us
    all_to_all x2, waiting for transfers between devices, edge_rows(): got = lax.all_to_all(send, 'space', 0, 0, tiled=True)  9.14 us
  transfers between devices with their start and end apart: 9, of which 4 were waited for; matrix products, arithmetic and copies ran while one was open for 10% of the time, Pallas kernels for 0%

profile of v6, /device:TPU:2, one launch (start us, length us, event | category | flops | bytes accessed | tf_op | source)
XLA Modules:
  0.0 243.5 jit_solution(1133789448838435103)
XLA Ops:
  0.7 1.2 copy.1173
  4.0 1.1 scatter-add.4
  6.6 2.7 %fusion.81 = (f32[1,8,6,12,384]{4,1,3,2,0:T(8,128)S(1)}, f32[8,6,12,384]{3,0,2,1:T(8,128)}, f32[8,6,12,384]{3,0,2,1:T(8,128)S(1)}, f32[1,8,6,12,384]{4,1,3,2,0:T(8,128)S(1)}) fusion(f32[2,8,6,12,384]{4,1,3,2,0:T(8,128)} %param.10), kind=kLoop, calls=%fused_computation.254 | loop fusion | bytes 5308416 | tf_op jit(solution)/shard_map/slice | solution.py:292
  9.4 1.5 fusion.88
  11.4 1.4 reshape_squeeze.13
  12.9 1.4 copy.894
  14.3 1.4 reshape_squeeze.12
  15.7 1.7 fusion.68
  17.4 2.4 rev.14
  19.8 1.7 copy.897
  21.5 1.7 reshape.839
  25.0 11.7 %all-to-all-start = ((f32[32,1,1168]{2,1,0:T(1,128)}), f32[32,1,1168]{2,1,0:T(1,128)}, u32[]{:S(2)}, u32[]{:S(2)}) async-start(f32[32,1,1168]{2,1,0:T(1,128)} %copy.900), calls=%async_computation | async-start | bytes 327680 | tf_op jit(solution)/shard_map/all_to_all | solution.py:84
  36.6 1.6 fusion.84
  42.6 1.1 copy.922
  57.2 1.1 copy.905
  64.1 1.4 fusion.18
  67.7 9.8 %all-to-all-start.1 = ((f32[32,12,96]{2,1,0:T(8,128)}), f32[32,12,96]{2,1,0:T(8,128)S(1)}, u32[]{:S(2)}, u32[]{:S(2)}) async-start(f32[32,12,96]{2,1,0:T(8,128)} %select_select_fusion.1), calls=%async_computation.1 | async-start | bytes 524288 | tf_op jit(solution)/shard_map/all_to_all | solution.py:154
  79.3 1.7 pad_maximum_fusion.5
  82.2 6.8 %all-to-all-done.1 = f32[32,12,96]{2,1,0:T(8,128)S(1)} async-done(((f32[32,12,96]{2,1,0:T(8,128)}), f32[32,12,96]{2,1,0:T(8,128)S(1)}, u32[]{:S(2)}, u32[]{:S(2)}) %all-to-all-start.1) | async-done | bytes 147488 | tf_op jit(solution)/shard_map/all_to_all | solution.py:154
  100.2 12.6 %all-to-all-start.2 = ((f32[32,1,864]{2,1,0:T(1,128)}), f32[32,1,864]{2,1,0:T(1,128)S(1)}, u32[]{:S(2)}, u32[]{:S(2)}) async-start(f32[32,1,864]{2,1,0:T(1,128)} %all_to_all.35), calls=%async_computation.2 | async-start | bytes 229376 | tf_op jit(solution)/shard_map/all_to_all | solution.py:84
  112.8 9.1 %all-to-all-done.2 = f32[32,1,864]{2,1,0:T(1,128)S(1)} async-done(((f32[32,1,864]{2,1,0:T(1,128)}), f32[32,1,864]{2,1,0:T(1,128)S(1)}, u32[]{:S(2)}, u32[]{:S(2)}) %all-to-all-start.2) | async-done | bytes 110624 | tf_op jit(solution)/shard_map/all_to_all | solution.py:84
  125.5 1.4 fusion.6
  129.1 5.0 %all-to-all-start.3 = ((f32[32,1,864]{2,1,0:T(1,128)}), f32[32,1,864]{2,1,0:T(1,128)S(1)}, u32[]{:S(2)}, u32[]{:S(2)}) async-start(f32[32,1,864]{2,1,0:T(1,128)} %reshape.889), calls=%async_computation.3 | async-start | bytes 229376 | tf_op jit(solution)/shard_map/all_to_all | solution.py:154
  134.8 1.9 collective-permute-start.3
  136.7 7.0 %all-to-all-done.3 = f32[32,1,864]{2,1,0:T(1,128)S(1)} async-done(((f32[32,1,864]{2,1,0:T(1,128)}), f32[32,1,864]{2,1,0:T(1,128)S(1)}, u32[]{:S(2)}, u32[]{:S(2)}) %all-to-all-start.3) | async-done | bytes 110624 | tf_op jit(solution)/shard_map/all_to_all | solution.py:154
  149.4 1.8 gather_fusion
  151.2 4.9 %fusion.62 = f32[270,8,128]{2,1,0:T(8,128)S(1)} fusion(bf16[270,128,128]{2,1,0:T(8,128)(2,1)} %param.13, bf16[270,8,128]{2,1,0:T(8,128)(2,1)S(1)} %gather_fusion, pred[270]{0:T(512)(128)(4,1)S(1)} %compare_and_fusion), kind=kOutput, calls=%fused_computation.105 | convolution fusion | flops 71055360 | bytes 10506510 | tf_op jit(solution)/shard_map/btk,tkc->tbc/dot_general | solution.py:262
  156.1 2.0 fusion.28
  158.1 2.6 %copy.986 = f32[512,8,128]{2,1,0:T(8,128)} copy(f32[512,8,128]{2,0,1:T(8,128)S(1)} %fusion.28) | data formatting | bytes 4194304 | tf_op jit(solution)/shard_map/st,tbc->sbc/dot_general | solution.py:265
  160.7 10.9 %all-to-all-start.4 = ((f32[32,128,128]{2,1,0:T(8,128)}), f32[32,128,128]{2,1,0:T(8,128)S(1)}, u32[]{:S(2)}, u32[]{:S(2)}) async-start(f32[32,128,128]{2,1,0:T(8,128)} %bitcast.221), calls=%async_computation.4 | async-start | bytes 4194304 | tf_op jit(solution)/shard_map/all_to_all | solution.py:269
  172.4 48.6 %all-to-all-done.4 = f32[32,128,128]{2,1,0:T(8,128)S(1)} async-done(((f32[32,128,128]{2,1,0:T(8,128)}), f32[32,128,128]{2,1,0:T(8,128)S(1)}, u32[]{:S(2)}, u32[]{:S(2)}) %all-to-all-start.4) | async-done | bytes 2097184 | tf_op jit(solution)/shard_map/all_to_all | solution.py:269
  222.2 20.4 %all_to_all.42 = f32[8,8,32,128]{3,2,1,0:T(8,128)S(1)} all-to-all(f32[8,8,32,128]{3,2,1,0:T(8,128)S(1)} %broadcast_in_dim.126), channel_id=1, replica_groups=mesh['space'=32,'scen'=8] {'scen'}, dimensions={0} | all-to-all | bytes 2097152 | tf_op jit(solution)/shard_map/all_to_all | solution.py:282
  (291 shorter events, 59.8 us)
Async XLA Ops:
  0.6 3.2 %copy-start.19 = (f32[1,6,12,384]{3,0,2,1:T(1,128)S(1)}, f32[1,6,12,384]{3,0,2,1:T(1,128)}, u32[]{:S(2)}) copy-start(f32[1,6,12,384]{3,0,2,1:T(1,128)} %param.9) | copy-start | bytes 331780
  0.6 1.2 copy-start.30
  9.4 88.5 %copy-start = (f32[1,8,6,12,384]{4,1,3,2,0:T(8,128)}, f32[1,8,6,12,384]{4,1,3,2,0:T(8,128)S(1)}, u32[]{:S(2)}) copy-start(f32[1,8,6,12,384]{4,1,3,2,0:T(8,128)S(1)} %get-tuple-element.41) | copy-start | bytes 2654212
  24.1 15.6 %copy-start.24 = (s32[270]{0:T(512)S(1)}, s32[270]{0:T(512)}, u32[]{:S(2)}) copy-start(s32[270]{0:T(512)} %param.11) | copy-start | bytes 3244
  25.0 25.3 %all-to-all-start = ((f32[32,1,1168]{2,1,0:T(1,128)}), f32[32,1,1168]{2,1,0:T(1,128)}, u32[]{:S(2)}, u32[]{:S(2)}) async-start(f32[32,1,1168]{2,1,0:T(1,128)} %copy.900), calls=%async_computation | async-start | bytes 327680 | tf_op jit(solution)/shard_map/all_to_all | solution.py:84
  39.8 9.6 %copy-start.11 = (f32[8,3,12,1]{3,0,2,1:T(8,128)S(1)}, f32[8,3,12,1]{3,0,2,1:T(8,128)}, u32[]{:S(2)}) copy-start(f32[8,3,12,1]{3,0,2,1:T(8,128)} %get-tuple-element.70) | copy-start | bytes 3460
  51.2 4.8 %copy-start.16 = (f32[32,1,1168]{2,0,1:T(8,128)}, f32[32,1,1168]{2,0,1:T(8,128)S(1)}, u32[]{:S(2)}) copy-start(f32[32,1,1168]{2,0,1:T(8,128)S(1)} %copy.1118) | copy-start | bytes 448516
  56.4 7.6 %copy-start.2 = (f32[1,8,6,12,1]{4,1,3,2,0:T(8,128)}, f32[1,8,6,12,1]{4,1,3,2,0:T(8,128)S(1)}, u32[]{:S(2)}) copy-start(f32[1,8,6,12,1]{4,1,3,2,0:T(8,128)S(1)} %copy.910) | copy-start | bytes 6916
  58.3 5.8 %copy-start.4 = (f32[1,8,6,12,1]{4,1,3,2,0:T(8,128)}, f32[1,8,6,12,1]{4,1,3,2,0:T(8,128)S(1)}, u32[]{:S(2)}) copy-start(f32[1,8,6,12,1]{4,1,3,2,0:T(8,128)S(1)} %copy.905) | copy-start | bytes 6916
  67.7 21.4 %all-to-all-start.1 = ((f32[32,12,96]{2,1,0:T(8,128)}), f32[32,12,96]{2,1,0:T(8,128)S(1)}, u32[]{:S(2)}, u32[]{:S(2)}) async-start(f32[32,12,96]{2,1,0:T(8,128)} %select_select_fusion.1), calls=%async_computation.1 | async-start | bytes 524288 | tf_op jit(solution)/shard_map/all_to_all | solution.py:154
  77.6 3.5 %copy-start.15 = (f32[48,384]{1,0:T(8,128)S(1)}, f32[48,384]{1,0:T(8,128)}, u32[]{:S(2)}) copy-start(f32[48,384]{1,0:T(8,128)} %reshape.848) | copy-start | bytes 221188
  78.5 2.6 %copy-start.6 = (f32[144,384]{1,0:T(8,128)S(1)}, f32[144,384]{1,0:T(8,128)}, u32[]{:S(2)}) copy-start(f32[144,384]{1,0:T(8,128)} %reshape.847) | copy-start | bytes 663556
  81.0 9.3 %collective-permute-start.1 = (f32[192,384]{1,0:T(8,128)}, f32[192,384]{1,0:T(8,128)}, u32[]{:S(2)}, u32[]{:S(2)}) collective-permute-start(f32[192,384]{1,0:T(8,128)} %pad_maximum_fusion.5), channel_id=1, source_target_pairs={{8,0},{16,8},{24,16},{32,24},{40,32},{48,40},{56,48},{64,56},{72,6... | collective-permute-start | bytes 884744 | tf_op jit(solution)/shard_map/ppermute | solution.py:13
  81.8 11.4 %collective-permute-start = (f32[192,384]{1,0:T(8,128)}, f32[192,384]{1,0:T(8,128)}, u32[]{:S(2)}, u32[]{:S(2)}) collective-permute-start(f32[192,384]{1,0:T(8,128)} %pad_maximum_fusion.4), channel_id=1, source_target_pairs={{248,0},{0,8},{8,16},{16,24},{24,32},{32,40},{40,48},{48,56},{56,6... | collective-permute-start | bytes 884744 | tf_op jit(solution)/shard_map/ppermute | solution.py:13
  91.4 6.5 %copy-start.7 = (f32[8,6,384]{2,0,1:T(8,128)}, f32[8,6,384]{2,0,1:T(8,128)S(1)}, u32[]{:S(2)}) copy-start(f32[8,6,384]{2,0,1:T(8,128)S(1)} %copy.1119) | copy-start | bytes 221188
  94.4 3.5 %copy-start.9 = (f32[8,6,384]{2,0,1:T(8,128)}, f32[8,6,384]{2,0,1:T(8,128)S(1)}, u32[]{:S(2)}) copy-start(f32[8,6,384]{2,0,1:T(8,128)S(1)} %copy.1120) | copy-start | bytes 221188
  95.5 1.8 copy-start.14
  95.5 1.8 copy-start.13
  95.5 1.8 copy-start.18
  95.5 1.9 copy-start.17
  98.7 14.0 %copy-start.25 = (s32[270]{0:T(512)S(1)}, s32[270]{0:T(512)}, u32[]{:S(2)}) copy-start(s32[270]{0:T(512)} %param.11) | copy-start | bytes 3244
  100.2 21.7 %all-to-all-start.2 = ((f32[32,1,864]{2,1,0:T(1,128)}), f32[32,1,864]{2,1,0:T(1,128)S(1)}, u32[]{:S(2)}, u32[]{:S(2)}) async-start(f32[32,1,864]{2,1,0:T(1,128)} %all_to_all.35), calls=%async_computation.2 | async-start | bytes 229376 | tf_op jit(solution)/shard_map/all_to_all | solution.py:84
  129.1 14.6 %all-to-all-start.3 = ((f32[32,1,864]{2,1,0:T(1,128)}), f32[32,1,864]{2,1,0:T(1,128)S(1)}, u32[]{:S(2)}, u32[]{:S(2)}) async-start(f32[32,1,864]{2,1,0:T(1,128)} %reshape.889), calls=%async_computation.3 | async-start | bytes 229376 | tf_op jit(solution)/shard_map/all_to_all | solution.py:154
  134.4 11.3 %collective-permute-start.2 = (f32[144,384]{1,0:T(8,128)S(1)}, f32[144,384]{1,0:T(8,128)S(1)}, u32[]{:S(2)}, u32[]{:S(2)}) collective-permute-start(f32[144,384]{1,0:T(8,128)S(1)} %reshape.862), channel_id=1, source_target_pairs={{248,0},{0,8},{8,16},{16,24},{24,32},{32,40},{40,48},{48,56},{56,6... | collective-permute-start | bytes 663560 | tf_op jit(solution)/shard_map/ppermute | solution.py:13
  134.8 11.0 %collective-permute-start.3 = (f32[144,384]{1,0:T(8,128)S(1)}, f32[144,384]{1,0:T(8,128)S(1)}, u32[]{:S(2)}, u32[]{:S(2)}) collective-permute-start(f32[144,384]{1,0:T(8,128)S(1)} %reshape.866), channel_id=1, source_target_pairs={{8,0},{16,8},{24,16},{32,24},{40,32},{48,40},{56,48},{64,56},{72,6... | collective-permute-start | bytes 663560 | tf_op jit(solution)/shard_map/ppermute | solution.py:13
  146.4 1.2 copy-start.1
  146.5 1.2 copy-start.8
  146.5 1.2 copy-start.10
  148.3 1.1 copy-start.23
  151.2 4.9 %copy-start.22 = (s32[270]{0:T(512)S(1)}, s32[270]{0:T(512)}, u32[]{:S(2)}) copy-start(s32[270]{0:T(512)} %copy-done.21) | copy-start | bytes 3244
  160.7 60.4 %all-to-all-start.4 = ((f32[32,128,128]{2,1,0:T(8,128)}), f32[32,128,128]{2,1,0:T(8,128)S(1)}, u32[]{:S(2)}, u32[]{:S(2)}) async-start(f32[32,128,128]{2,1,0:T(8,128)} %bitcast.221), calls=%async_computation.4 | async-start | bytes 4194304 | tf_op jit(solution)/shard_map/all_to_all | solution.py:269
  222.1 20.5 %copy-start.12 = (f32[8,128,32]{1,2,0:T(8,128)}, f32[8,128,32]{1,2,0:T(8,128)S(1)}, u32[]{:S(2)}) copy-start(f32[8,128,32]{1,2,0:T(8,128)S(1)} %fusion) | copy-start | bytes 393220
  (8 other events, 7.0 us)

commit v7 on v6

--- a/solution.py
+++ b/solution.py
@@ -135,7 +135,7 @@
     return (padded, faces_known, edge_wind, rode)
 
 
-def edge_columns(tracer, east_wind, position, band_count, with_wind):
+def edge_columns(tracer, east_wind, position, band_count, with_wind, rider=None):
     scenarios, levels, _, row_count, width_cells = tracer.shape
     to_top = [jnp.moveaxis(tracer[:, :, 0::2, :, 0:3], 3, 0).reshape(row_count, -1)]
     to_low = [jnp.moveaxis(tracer[:, :, 1::2, :, width_cells - 3 :], 3, 0).reshape(row_count, -1)]
@@ -151,23 +151,33 @@
     send = jnp.where(
         destination == band_count - 1, to_top[None], jnp.where(destination == 0, to_low[None], 0.0)
     ).astype(to_top.dtype)
+    rode = None
+    if rider is not None:
+        send = jnp.concatenate([send.reshape(band_count, -1), rider.astype(send.dtype)], 1)
     got = lax.all_to_all(send, "space", 0, 0, tiled=True)
+    if rider is not None:
+        rode = got[:, row_count * count :]
+        got = got[:, : row_count * count].reshape(band_count, row_count, count)
     flipped = jnp.flip(got.reshape(-1, count), 0).T
     cells = scenarios * levels * 3 * 3
     layers = flipped[:cells].reshape(scenarios, levels, 3, 3, band_count * row_count)
     wind = None
     if with_wind:
         wind = flipped[cells:].reshape(levels, 3, band_count * row_count)
-    return layers, wind
-
-
-def row_halos(tracer, east_wind, north_wind, position, band_count, row_wind, faces_known):
+    return layers, wind, rode
+
+
+def row_halos(
+    tracer, east_wind, north_wind, position, band_count, row_wind, faces_known, rider=None
+):
     first_step = row_wind is None
     shifted = []
     for step_by, lowest in ((-1, True), (1, False)):
         packed = pack_rows(tracer, north_wind if first_step else None, lowest)
         shifted.append(from_behind(packed, "space", step_by))
-    edge_layers, edge_speed = edge_columns(tracer, east_wind, position, band_count, first_step)
+    edge_layers, edge_speed, rode = edge_columns(
+        tracer, east_wind, position, band_count, first_step, rider
+    )
     layer_rows = tracer.shape[0] * tracer.shape[1] * 18
     width_cells = tracer.shape[4]
     if first_step:
@@ -238,7 +248,7 @@
             -2,
         )
         faces_known = 0.5 * (speeds[:, :, :-1, :] + speeds[:, :, 1:, :])
-    return (padded, faces_known, row_wind)
+    return (padded, faces_known, row_wind, rode)
 
 
 def slot_plan(tile_target, band_count):
@@ -305,14 +315,20 @@
             band_count,
             edge_wind,
             cx,
-            slot_block if step_number == 0 else None,
-        )
-        if step_number == 0:
+        )
+        tracer = parabola_sweep(padded, cx, 4)
+        padded, cy, row_wind, rode = row_halos(
+            tracer,
+            east_wind,
+            north_wind,
+            position,
+            band_count,
+            row_wind,
+            cy,
+            slot_block if step_number == 1 else None,
+        )
+        if step_number == 1:
             got_block = rode
-        tracer = parabola_sweep(padded, cx, 4)
-        padded, cy, row_wind = row_halos(
-            tracer, east_wind, north_wind, position, band_count, row_wind, cy
-        )
         tracer = parabola_sweep(padded, cy, 3)
     regridded = regrid(tracer, tile_source, slot_hot, got_block, intersection, band_count)
     ensemble_moments = moments_of(regridded)

time: 247 us -> 242 us (0.980)
  local copies, waits for them, and re-layouts: 65.2 us -> 59.2 us
    unnamed x99 -> x115, local copies, waits for them, and re-layouts: 12.7 us -> 10.7 us
  transfers between devices with their start and end apart: 9 -> 9, of which waited for: 4 -> 4; matrix products, arithmetic and copies ran while one was open for 10% -> 9% of each run, Pallas kernels for 0% -> 0%
where the time goes in v7:
time: 242 us; the launch traced here: 238 us
  waiting for transfers between devices  71.7 us (30%)
  local copies, waits for them, and re-layouts  59.2 us (24%)
  starting transfers between devices  54.1 us (22%)
  other arithmetic  22.5 us (9%)
  blocking collectives  20.3 us (8%)
  matrix products  7.99 us (3%)
    all_to_all x1, waiting for transfers between devices, regrid(): got = lax.all_to_all(send, 'space', 0, 0, tiled=True)  49.3 us
    all_to_all x2, starting transfers between devices, edge_rows(): got = lax.all_to_all(send, 'space', 0, 0, tiled=True)  24.2 us
    all_to_all x1, blocking collectives, moments_of(): everyone = lax.all_to_all(copies, 'scen', 0, 0, tiled=True)  20.3 us
    all_to_all x2, starting transfers between devices, edge_columns(): got = lax.all_to_all(send, 'space', 0, 0, tiled=True)  14.8 us
    all_to_all x2, waiting for transfers between devices, edge_columns(): got = lax.all_to_all(send, 'space', 0, 0, tiled=True)  13.8 us
    all_to_all x1, starting transfers between devices, regrid(): got = lax.all_to_all(send, 'space', 0, 0, tiled=True)  12.4 us
    unnamed x115, local copies, waits for them, and re-layouts  10.7 us
    all_to_all x2, waiting for transfers between devices, edge_rows(): got = lax.all_to_all(send, 'space', 0, 0, tiled=True)  8.61 us
  transfers between devices with their start and end apart: 9, of which 4 were waited for; matrix products, arithmetic and copies ran while one was open for 9% of the time, Pallas kernels for 0%

profile of v7, /device:TPU:2, one launch (start us, length us, event | category | flops | bytes accessed | tf_op | source)
XLA Modules:
  0.0 237.8 jit_solution(14428548655589555420)
XLA Ops:
  0.6 1.2 copy.1155
  2.0 1.1 scatter-add.4
  4.6 2.7 %fusion.81 = (f32[1,8,6,12,384]{4,1,3,2,0:T(8,128)S(1)}, f32[8,6,12,384]{3,0,2,1:T(8,128)}, f32[8,6,12,384]{3,0,2,1:T(8,128)S(1)}, f32[1,8,6,12,384]{4,1,3,2,0:T(8,128)S(1)}) fusion(f32[2,8,6,12,384]{4,1,3,2,0:T(8,128)} %param.10), kind=kLoop, calls=%fused_computation.254 | loop fusion | bytes 5308416 | tf_op jit(solution)/shard_map/slice | solution.py:302
  7.3 1.5 fusion.88
  9.4 1.4 reshape_squeeze.13
  10.9 1.4 copy.878
  12.3 1.4 reshape_squeeze.12
  13.7 1.7 fusion.68
  15.4 2.4 %rev.14 = f32[384,96]{0,1:T(8,128)} reverse(f32[384,96]{0,1:T(8,128)} %fusion.68), dimensions={0} | reverse | bytes 294912 | tf_op jit(solution)/shard_map/jit(_flip)/rev | solution.py:80
  17.7 1.7 copy.881
  19.5 1.8 all_to_all.39
  21.3 11.7 %all-to-all-start = ((f32[32,1,1152]{2,1,0:T(1,128)}), f32[32,1,1152]{2,1,0:T(1,128)}, u32[]{:S(2)}, u32[]{:S(2)}) async-start(f32[32,1,1152]{2,1,0:T(1,128)} %all_to_all.39), calls=%async_computation | async-start | bytes 294912 | tf_op jit(solution)/shard_map/all_to_all | solution.py:84
  33.0 1.6 fusion.84
  51.7 1.1 copy.887
  58.6 1.4 fusion.18
  62.2 9.8 %all-to-all-start.1 = ((f32[32,12,96]{2,1,0:T(8,128)}), f32[32,12,96]{2,1,0:T(8,128)S(1)}, u32[]{:S(2)}, u32[]{:S(2)}) async-start(f32[32,12,96]{2,1,0:T(8,128)} %select_select_fusion), calls=%async_computation.1 | async-start | bytes 524288 | tf_op jit(solution)/shard_map/all_to_all | solution.py:157
  73.8 1.7 pad_maximum_fusion.5
  76.8 6.8 %all-to-all-done.1 = f32[32,12,96]{2,1,0:T(8,128)S(1)} async-done(((f32[32,12,96]{2,1,0:T(8,128)}), f32[32,12,96]{2,1,0:T(8,128)S(1)}, u32[]{:S(2)}, u32[]{:S(2)}) %all-to-all-start.1) | async-done | bytes 147488 | tf_op jit(solution)/shard_map/all_to_all | solution.py:157
  94.8 12.6 %all-to-all-start.2 = ((f32[32,1,864]{2,1,0:T(1,128)}), f32[32,1,864]{2,1,0:T(1,128)S(1)}, u32[]{:S(2)}, u32[]{:S(2)}) async-start(f32[32,1,864]{2,1,0:T(1,128)} %all_to_all.40), calls=%async_computation.2 | async-start | bytes 229376 | tf_op jit(solution)/shard_map/all_to_all | solution.py:84
  107.9 8.6 %all-to-all-done.2 = f32[32,1,864]{2,1,0:T(1,128)S(1)} async-done(((f32[32,1,864]{2,1,0:T(1,128)}), f32[32,1,864]{2,1,0:T(1,128)S(1)}, u32[]{:S(2)}, u32[]{:S(2)}) %all-to-all-start.2) | async-done | bytes 110624 | tf_op jit(solution)/shard_map/all_to_all | solution.py:84
  120.1 1.4 fusion.6
  123.5 5.0 %all-to-all-start.3 = ((f32[32,1,880]{2,1,0:T(1,128)}), f32[32,1,880]{2,1,0:T(1,128)S(1)}, u32[]{:S(2)}, u32[]{:S(2)}) async-start(f32[32,1,880]{2,1,0:T(1,128)} %all_to_all.34), calls=%async_computation.3 | async-start | bytes 229376 | tf_op jit(solution)/shard_map/all_to_all | solution.py:157
  129.2 1.9 collective-permute-start.3
  131.1 7.0 %all-to-all-done.3 = f32[32,1,880]{2,1,0:T(1,128)S(1)} async-done(((f32[32,1,880]{2,1,0:T(1,128)}), f32[32,1,880]{2,1,0:T(1,128)S(1)}, u32[]{:S(2)}, u32[]{:S(2)}) %all-to-all-start.3) | async-done | bytes 112672 | tf_op jit(solution)/shard_map/all_to_all | solution.py:157
  141.2 1.1 fusion.79
  142.3 1.8 gather_fusion
  144.1 4.9 %fusion.62 = f32[270,8,128]{2,1,0:T(8,128)S(1)} fusion(bf16[270,128,128]{2,1,0:T(8,128)(2,1)} %param.13, bf16[270,8,128]{2,1,0:T(8,128)(2,1)S(1)} %gather_fusion, pred[270]{0:T(512)(128)(4,1)S(1)} %copy-done.38), kind=kOutput, calls=%fused_computation.105 | convolution fusion | flops 71055360 | bytes 10506510 | tf_op jit(solution)/shard_map/btk,tkc->tbc/dot_general | solution.py:272
  149.0 2.0 fusion.28
  151.0 2.6 %copy.968 = f32[512,8,128]{2,1,0:T(8,128)} copy(f32[512,8,128]{2,0,1:T(8,128)S(1)} %fusion.28) | data formatting | bytes 4194304 | tf_op jit(solution)/shard_map/st,tbc->sbc/dot_general | solution.py:275
  153.6 12.4 %all-to-all-start.4 = ((f32[32,128,128]{2,1,0:T(8,128)}), f32[32,128,128]{2,1,0:T(8,128)S(1)}, u32[]{:S(2)}, u32[]{:S(2)}) async-start(f32[32,128,128]{2,1,0:T(8,128)} %bitcast.220), calls=%async_computation.4 | async-start | bytes 4194304 | tf_op jit(solution)/shard_map/all_to_all | solution.py:279
  166.2 49.3 %all-to-all-done.4 = f32[32,128,128]{2,1,0:T(8,128)S(1)} async-done(((f32[32,128,128]{2,1,0:T(8,128)}), f32[32,128,128]{2,1,0:T(8,128)S(1)}, u32[]{:S(2)}, u32[]{:S(2)}) %all-to-all-start.4) | async-done | bytes 2097184 | tf_op jit(solution)/shard_map/all_to_all | solution.py:279
  216.7 20.3 %all_to_all.47 = f32[8,8,32,128]{3,2,1,0:T(8,128)S(1)} all-to-all(f32[8,8,32,128]{3,2,1,0:T(8,128)S(1)} %broadcast_in_dim.126), channel_id=1, replica_groups=mesh['space'=32,'scen'=8] {'scen'}, dimensions={0} | all-to-all | bytes 2097152 | tf_op jit(solution)/shard_map/all_to_all | solution.py:292
  (303 shorter events, 52.5 us)
Async XLA Ops:
  7.3 85.1 %copy-start = (f32[1,8,6,12,384]{4,1,3,2,0:T(8,128)}, f32[1,8,6,12,384]{4,1,3,2,0:T(8,128)S(1)}, u32[]{:S(2)}) copy-start(f32[1,8,6,12,384]{4,1,3,2,0:T(8,128)S(1)} %get-tuple-element.41) | copy-start | bytes 2654212
  17.7 18.4 %copy-start.32 = (s32[270]{0:T(512)S(1)}, s32[270]{0:T(512)}, u32[]{:S(2)}) copy-start(s32[270]{0:T(512)} %param.11) | copy-start | bytes 3244
  17.7 19.0 %copy-start.39 = (s32[270]{0:T(512)S(1)}, s32[270]{0:T(512)}, u32[]{:S(2)}) copy-start(s32[270]{0:T(512)} %param.12) | copy-start | bytes 3244
  21.3 23.8 %all-to-all-start = ((f32[32,1,1152]{2,1,0:T(1,128)}), f32[32,1,1152]{2,1,0:T(1,128)}, u32[]{:S(2)}, u32[]{:S(2)}) async-start(f32[32,1,1152]{2,1,0:T(1,128)} %all_to_all.39), calls=%async_computation | async-start | bytes 294912 | tf_op jit(solution)/shard_map/all_to_all | solution.py:84
  36.1 5.7 %copy-start.12 = (f32[8,3,12,1]{3,0,2,1:T(8,128)S(1)}, f32[8,3,12,1]{3,0,2,1:T(8,128)}, u32[]{:S(2)}) copy-start(f32[8,3,12,1]{3,0,2,1:T(8,128)} %get-tuple-element.69) | copy-start | bytes 3460
  36.1 5.9 %copy-start.24 = (f32[8,1,12,1]{3,0,2,1:T(8,128)S(1)}, f32[8,1,12,1]{3,0,2,1:T(8,128)}, u32[]{:S(2)}) copy-start(f32[8,1,12,1]{3,0,2,1:T(8,128)} %get-tuple-element.71) | copy-start | bytes 1156
  36.1 6.1 %copy-start.23 = (f32[8,1,12,1]{3,0,2,1:T(8,128)S(1)}, f32[8,1,12,1]{3,0,2,1:T(8,128)}, u32[]{:S(2)}) copy-start(f32[8,1,12,1]{3,0,2,1:T(8,128)} %get-tuple-element.72) | copy-start | bytes 1156
  36.1 6.2 %copy-start.22 = (f32[8,1,12,1]{3,0,2,1:T(8,128)S(1)}, f32[8,1,12,1]{3,0,2,1:T(8,128)}, u32[]{:S(2)}) copy-start(f32[8,1,12,1]{3,0,2,1:T(8,128)} %get-tuple-element.73) | copy-start | bytes 1156
  36.1 6.3 %copy-start.21 = (f32[8,1,12,1]{3,0,2,1:T(8,128)S(1)}, f32[8,1,12,1]{3,0,2,1:T(8,128)}, u32[]{:S(2)}) copy-start(f32[8,1,12,1]{3,0,2,1:T(8,128)} %get-tuple-element.74) | copy-start | bytes 1156
  36.1 6.5 %copy-start.20 = (f32[8,1,12,1]{3,0,2,1:T(8,128)S(1)}, f32[8,1,12,1]{3,0,2,1:T(8,128)}, u32[]{:S(2)}) copy-start(f32[8,1,12,1]{3,0,2,1:T(8,128)} %get-tuple-element.75) | copy-start | bytes 1156
  36.2 6.6 %copy-start.19 = (f32[8,1,12,1]{3,0,2,1:T(8,128)S(1)}, f32[8,1,12,1]{3,0,2,1:T(8,128)}, u32[]{:S(2)}) copy-start(f32[8,1,12,1]{3,0,2,1:T(8,128)} %get-tuple-element.76) | copy-start | bytes 1156
  36.2 7.4 %copy-start.11 = (f32[8,3,12,1]{3,0,2,1:T(8,128)S(1)}, f32[8,3,12,1]{3,0,2,1:T(8,128)}, u32[]{:S(2)}) copy-start(f32[8,3,12,1]{3,0,2,1:T(8,128)} %get-tuple-element.70) | copy-start | bytes 3460
  51.0 7.6 %copy-start.2 = (f32[1,8,6,12,1]{4,1,3,2,0:T(8,128)}, f32[1,8,6,12,1]{4,1,3,2,0:T(8,128)S(1)}, u32[]{:S(2)}) copy-start(f32[1,8,6,12,1]{4,1,3,2,0:T(8,128)S(1)} %copy.892) | copy-start | bytes 6916
  52.8 5.8 %copy-start.4 = (f32[1,8,6,12,1]{4,1,3,2,0:T(8,128)}, f32[1,8,6,12,1]{4,1,3,2,0:T(8,128)S(1)}, u32[]{:S(2)}) copy-start(f32[1,8,6,12,1]{4,1,3,2,0:T(8,128)S(1)} %copy.887) | copy-start | bytes 6916
  62.2 21.4 %all-to-all-start.1 = ((f32[32,12,96]{2,1,0:T(8,128)}), f32[32,12,96]{2,1,0:T(8,128)S(1)}, u32[]{:S(2)}, u32[]{:S(2)}) async-start(f32[32,12,96]{2,1,0:T(8,128)} %select_select_fusion), calls=%async_computation.1 | async-start | bytes 524288 | tf_op jit(solution)/shard_map/all_to_all | solution.py:157
  72.1 3.5 %copy-start.16 = (f32[48,384]{1,0:T(8,128)S(1)}, f32[48,384]{1,0:T(8,128)}, u32[]{:S(2)}) copy-start(f32[48,384]{1,0:T(8,128)} %reshape.851) | copy-start | bytes 221188
  73.0 2.6 %copy-start.6 = (f32[144,384]{1,0:T(8,128)S(1)}, f32[144,384]{1,0:T(8,128)}, u32[]{:S(2)}) copy-start(f32[144,384]{1,0:T(8,128)} %reshape.850) | copy-start | bytes 663556
  75.5 9.3 %collective-permute-start.1 = (f32[192,384]{1,0:T(8,128)}, f32[192,384]{1,0:T(8,128)}, u32[]{:S(2)}, u32[]{:S(2)}) collective-permute-start(f32[192,384]{1,0:T(8,128)} %pad_maximum_fusion.5), channel_id=1, source_target_pairs={{8,0},{16,8},{24,16},{32,24},{40,32},{48,40},{56,48},{64,56},{72,6... | collective-permute-start | bytes 884744 | tf_op jit(solution)/shard_map/ppermute | solution.py:13
  76.4 11.4 %collective-permute-start = (f32[192,384]{1,0:T(8,128)}, f32[192,384]{1,0:T(8,128)}, u32[]{:S(2)}, u32[]{:S(2)}) collective-permute-start(f32[192,384]{1,0:T(8,128)} %pad_maximum_fusion.4), channel_id=1, source_target_pairs={{248,0},{0,8},{8,16},{16,24},{24,32},{32,40},{40,48},{48,56},{56,6... | collective-permute-start | bytes 884744 | tf_op jit(solution)/shard_map/ppermute | solution.py:13
  86.0 6.5 %copy-start.7 = (f32[8,6,384]{2,0,1:T(8,128)}, f32[8,6,384]{2,0,1:T(8,128)S(1)}, u32[]{:S(2)}) copy-start(f32[8,6,384]{2,0,1:T(8,128)S(1)} %copy.1101) | copy-start | bytes 221188
  89.0 3.5 %copy-start.9 = (f32[8,6,384]{2,0,1:T(8,128)}, f32[8,6,384]{2,0,1:T(8,128)S(1)}, u32[]{:S(2)}) copy-start(f32[8,6,384]{2,0,1:T(8,128)S(1)} %copy.1102) | copy-start | bytes 221188
  90.1 1.8 copy-start.14
  90.1 1.9 copy-start.17
  93.3 14.0 %copy-start.33 = (s32[270]{0:T(512)S(1)}, s32[270]{0:T(512)}, u32[]{:S(2)}) copy-start(s32[270]{0:T(512)} %param.11) | copy-start | bytes 3244
  94.8 21.8 %all-to-all-start.2 = ((f32[32,1,864]{2,1,0:T(1,128)}), f32[32,1,864]{2,1,0:T(1,128)S(1)}, u32[]{:S(2)}, u32[]{:S(2)}) async-start(f32[32,1,864]{2,1,0:T(1,128)} %all_to_all.40), calls=%async_computation.2 | async-start | bytes 229376 | tf_op jit(solution)/shard_map/all_to_all | solution.py:84
  123.5 14.6 %all-to-all-start.3 = ((f32[32,1,880]{2,1,0:T(1,128)}), f32[32,1,880]{2,1,0:T(1,128)S(1)}, u32[]{:S(2)}, u32[]{:S(2)}) async-start(f32[32,1,880]{2,1,0:T(1,128)} %all_to_all.34), calls=%async_computation.3 | async-start | bytes 229376 | tf_op jit(solution)/shard_map/all_to_all | solution.py:157
  128.8 9.8 %collective-permute-start.2 = (f32[144,384]{1,0:T(8,128)S(1)}, f32[144,384]{1,0:T(8,128)S(1)}, u32[]{:S(2)}, u32[]{:S(2)}) collective-permute-start(f32[144,384]{1,0:T(8,128)S(1)} %reshape.865), channel_id=1, source_target_pairs={{248,0},{0,8},{8,16},{16,24},{24,32},{32,40},{40,48},{48,56},{56,6... | collective-permute-start | bytes 663560 | tf_op jit(solution)/shard_map/ppermute | solution.py:13
  129.2 9.5 %collective-permute-start.3 = (f32[144,384]{1,0:T(8,128)S(1)}, f32[144,384]{1,0:T(8,128)S(1)}, u32[]{:S(2)}, u32[]{:S(2)}) collective-permute-start(f32[144,384]{1,0:T(8,128)S(1)} %reshape.871), channel_id=1, source_target_pairs={{8,0},{16,8},{24,16},{32,24},{40,32},{48,40},{56,48},{64,56},{72,6... | collective-permute-start | bytes 663560 | tf_op jit(solution)/shard_map/ppermute | solution.py:13
  141.2 2.9 %copy-start.38 = (pred[270]{0:T(512)(128)(4,1)S(1)}, pred[270]{0:T(512)(128)(4,1)}, u32[]{:S(2)}) copy-start(pred[270]{0:T(512)(128)(4,1)} %compare_and_fusion) | copy-start | bytes 814
  144.1 4.9 %copy-start.30 = (s32[270]{0:T(512)S(1)}, s32[270]{0:T(512)}, u32[]{:S(2)}) copy-start(s32[270]{0:T(512)} %copy-done.29) | copy-start | bytes 3244
  153.6 61.9 %all-to-all-start.4 = ((f32[32,128,128]{2,1,0:T(8,128)}), f32[32,128,128]{2,1,0:T(8,128)S(1)}, u32[]{:S(2)}, u32[]{:S(2)}) async-start(f32[32,128,128]{2,1,0:T(8,128)} %bitcast.220), calls=%async_computation.4 | async-start | bytes 4194304 | tf_op jit(solution)/shard_map/all_to_all | solution.py:279
  216.5 20.4 %copy-start.13 = (f32[8,128,32]{1,2,0:T(8,128)}, f32[8,128,32]{1,2,0:T(8,128)S(1)}, u32[]{:S(2)}) copy-start(f32[8,128,32]{1,2,0:T(8,128)S(1)} %fusion) | copy-start | bytes 393220
  (17 other events, 18.1 us)

commit v8 on v7

--- a/solution.py
+++ b/solution.py
@@ -297,7 +297,7 @@
 def local(concentration, emissions, courant, tile_source, tile_target, intersection):
     band_count = lax.axis_size("space")
     position = lax.axis_index("space")
-    tracer = concentration.at[:, 0].add(emissions)
+    tracer = jnp.concatenate([concentration[:, :1] + emissions[:, None], concentration[:, 1:]], 1)
     east_wind = courant[0]
     north_wind = courant[1]
     edge_wind = None

time: 242 us -> 223 us (0.921)
  local copies, waits for them, and re-layouts: 59.2 us -> 37.8 us
  other arithmetic: 22.5 us -> 25.8 us
    rev x4, local copies, waits for them, and re-layouts: 4.52 us -> 0.78 us  [edge_rows(): send = jnp.flip(send.T, 0).reshape(band_count, -1)]
    slice x16 -> x2, local copies, waits for them, and re-layouts: 4.42 us -> 1.5 us  [the longest x1 1.28 us: local(): concentration[:, 1:]]
    slice x2, local copies, waits for them, and re-layouts: 2.49 us -> 0.03 us  [pack_rows(): north_wind[:, :, row_count - 1:, :]]
  transfers between devices with their start and end apart: 9 -> 9, of which waited for: 4 -> 4; matrix products, arithmetic and copies ran while one was open for 9% -> 8% of each run, Pallas kernels for 0% -> 0%
where the time goes in v8:
time: 223 us; the launch traced here: 220 us
  waiting for transfers between devices  73.8 us (33%)
  starting transfers between devices  53 us (24%)
  local copies, waits for them, and re-layouts  37.8 us (17%)
  other arithmetic  25.8 us (12%)
  blocking collectives  19.9 us (9%)
  matrix products  7.98 us (4%)
    all_to_all x1, waiting for transfers between devices, regrid(): got = lax.all_to_all(send, 'space', 0, 0, tiled=True)  49.6 us
    all_to_all x2, starting transfers between devices, edge_rows(): got = lax.all_to_all(send, 'space', 0, 0, tiled=True)  23.7 us
    all_to_all x1, blocking collectives, moments_of(): everyone = lax.all_to_all(copies, 'scen', 0, 0, tiled=True)  19.9 us
    all_to_all x2, waiting for transfers between devices, edge_columns(): got = lax.all_to_all(send, 'space', 0, 0, tiled=True)  15.8 us
    all_to_all x2, starting transfers between devices, edge_columns(): got = lax.all_to_all(send, 'space', 0, 0, tiled=True)  15.3 us
    unnamed x115, local copies, waits for them, and re-layouts  11.5 us
    all_to_all x1, starting transfers between devices, regrid(): got = lax.all_to_all(send, 'space', 0, 0, tiled=True)  11.4 us
    all_to_all x2, waiting for transfers between devices, edge_rows(): got = lax.all_to_all(send, 'space', 0, 0, tiled=True)  8.4 us
  transfers between devices with their start and end apart: 9, of which 4 were waited for; matrix products, arithmetic and copies ran while one was open for 8% of the time, Pallas kernels for 0%

profile of v8, /device:TPU:2, one launch (start us, length us, event | category | flops | bytes accessed | tf_op | source)
XLA Modules:
  0.0 220.2 jit_solution(11950638758043747732)
XLA Ops:
  0.6 1.3 slice.578
  1.9 1.3 bitcast_add_fusion
  3.7 2.6 %fusion.87 = (f32[1,8,6,12,384]{4,1,3,2,0:T(8,128)}, f32[8,6,12,384]{3,0,2,1:T(8,128)S(1)}, f32[1,8,6,12,384]{4,1,3,2,0:T(8,128)S(1)}) fusion(f32[2,8,6,12,384]{4,1,3,2,0:T(8,128)} %param.8), kind=kLoop, calls=%fused_computation.298 | loop fusion | bytes 4423680 | tf_op jit(solution)/shard_map/slice | solution.py:302
  6.8 0.9 all_to_all.39
  7.7 11.6 %all-to-all-start = ((f32[32,1,1152]{2,1,0:T(1,128)}), f32[32,1,1152]{2,1,0:T(1,128)S(1)}, u32[]{:S(2)}, u32[]{:S(2)}) async-start(f32[32,1,1152]{2,1,0:T(1,128)} %all_to_all.39), calls=%async_computation | async-start | bytes 294912 | tf_op jit(solution)/shard_map/all_to_all | solution.py:84
  20.1 0.9 reduce-window.6
  22.3 5.7 %copy.485 = f32[1,8,6,12,384]{3,1,4,2,0:T(8,128)} copy(f32[1,8,6,12,384]{4,1,3,2,0:T(8,128)S(1)} %get-tuple-element.30) | data formatting | bytes 1769472
  35.2 2.3 %fusion.25 = f32[1,8,6,12,387]{4,1,3,2,0:T(8,128)S(1)} fusion(f32[1,8,6,12,390]{4,1,3,2,0:T(8,128)S(1)} %pad_maximum_fusion.3, f32[1,7,6,12,384]{4,1,3,2,0:T(8,128)S(1)} %slice.578, f32[1,1,6,12,384]{4,1,3,2,0:T(1,128)S(1)} %bitcast_add_fusion, f32[1,8,6,12,3]{4,1,3,2,0:T(8,128)S(1)} %copy.419, f32[1,8,6,12,3]{4,1,3,2,0:T(8,128)} %copy-done.4), kind=kLoop, calls=%fused_computation.43 | loop fusion | flops 2006208 | bytes 3573504 | tf_op jit(solution)/shard_map/sub | solution.py:22
  37.5 2.1 slice_subtract_fusion.1
  42.1 1.1 copy.402
  43.3 3.7 %fusion.18 = f32[1,8,6,12,385]{4,1,3,2,0:T(8,128)S(1)} fusion(f32[1,8,6,12,386]{4,1,3,2,0:T(8,128)} %get-tuple-element.34, f32[1,8,6,12,386]{4,1,3,2,0:T(8,128)} %get-tuple-element.33, f32[1,8,6,12,387]{4,1,3,2,0:T(8,128)S(1)} %fusion.25, f32[1,8,6,12,1]{4,1,3,2,0:T(8,128)S(1)} %copy.406, f32[1,8,6,12,384]{4,1,3,2,0:T(8,128)S(1)} %get-tuple-element.30, ...), kind=kLoop, calls=%fused_computation.33 | loop fusion | flops 5100480 | bytes 6211584 | tf_op jit(solution)/shard_map/jit(_where)/select_n | solution.py:49
  49.3 9.8 %all-to-all-start.1 = ((f32[32,12,96]{2,1,0:T(8,128)}), f32[32,12,96]{2,1,0:T(8,128)S(1)}, u32[]{:S(2)}, u32[]{:S(2)}) async-start(f32[32,12,96]{2,1,0:T(8,128)} %select_select_fusion), calls=%async_computation.1 | async-start | bytes 524288 | tf_op jit(solution)/shard_map/all_to_all | solution.py:157
  62.1 8.7 %all-to-all-done.1 = f32[32,12,96]{2,1,0:T(8,128)S(1)} async-done(((f32[32,12,96]{2,1,0:T(8,128)}), f32[32,12,96]{2,1,0:T(8,128)S(1)}, u32[]{:S(2)}, u32[]{:S(2)}) %all-to-all-start.1) | async-done | bytes 147488 | tf_op jit(solution)/shard_map/all_to_all | solution.py:157
  74.2 1.0 copy-done
  76.5 0.9 all_to_all.40
  77.4 12.1 %all-to-all-start.2 = ((f32[32,1,864]{2,1,0:T(1,128)}), f32[32,1,864]{2,1,0:T(1,128)S(1)}, u32[]{:S(2)}, u32[]{:S(2)}) async-start(f32[32,1,864]{2,1,0:T(1,128)} %all_to_all.40), calls=%async_computation.2 | async-start | bytes 229376 | tf_op jit(solution)/shard_map/all_to_all | solution.py:84
  90.4 8.4 %all-to-all-done.2 = f32[32,1,864]{2,1,0:T(1,128)S(1)} async-done(((f32[32,1,864]{2,1,0:T(1,128)}), f32[32,1,864]{2,1,0:T(1,128)S(1)}, u32[]{:S(2)}, u32[]{:S(2)}) %all-to-all-start.2) | async-done | bytes 110624 | tf_op jit(solution)/shard_map/all_to_all | solution.py:84
  100.3 1.0 fusion.13
  102.3 1.4 fusion.6
  105.8 5.5 %all-to-all-start.3 = ((f32[32,1,880]{2,1,0:T(1,128)}), f32[32,1,880]{2,1,0:T(1,128)S(1)}, u32[]{:S(2)}, u32[]{:S(2)}) async-start(f32[32,1,880]{2,1,0:T(1,128)} %all_to_all.34), calls=%async_computation.3 | async-start | bytes 229376 | tf_op jit(solution)/shard_map/all_to_all | solution.py:157
  111.9 1.9 collective-permute-start.3
  113.8 7.1 %all-to-all-done.3 = f32[32,1,880]{2,1,0:T(1,128)S(1)} async-done(((f32[32,1,880]{2,1,0:T(1,128)}), f32[32,1,880]{2,1,0:T(1,128)S(1)}, u32[]{:S(2)}, u32[]{:S(2)}) %all-to-all-start.3) | async-done | bytes 112672 | tf_op jit(solution)/shard_map/all_to_all | solution.py:157
  121.4 1.0 reshape.822
  124.8 1.0 fusion.85
  125.8 1.8 gather_fusion
  127.6 4.9 %fusion.62 = f32[270,8,128]{2,1,0:T(8,128)S(1)} fusion(bf16[270,128,128]{2,1,0:T(8,128)(2,1)} %param.11, bf16[270,8,128]{2,1,0:T(8,128)(2,1)S(1)} %gather_fusion, pred[270]{0:T(512)(128)(4,1)S(1)} %compare_and_fusion), kind=kOutput, calls=%fused_computation.118 | convolution fusion | flops 71055360 | bytes 10506510 | tf_op jit(solution)/shard_map/btk,tkc->tbc/dot_general | solution.py:272
  132.5 2.0 fusion.28
  134.6 2.6 %copy.481 = f32[512,8,128]{2,1,0:T(8,128)} copy(f32[512,8,128]{2,0,1:T(8,128)S(1)} %fusion.28) | data formatting | bytes 4194304 | tf_op jit(solution)/shard_map/st,tbc->sbc/dot_general | solution.py:275
  137.1 11.4 %all-to-all-start.4 = ((f32[32,128,128]{2,1,0:T(8,128)}), f32[32,128,128]{2,1,0:T(8,128)S(1)}, u32[]{:S(2)}, u32[]{:S(2)}) async-start(f32[32,128,128]{2,1,0:T(8,128)} %bitcast.255), calls=%async_computation.4 | async-start | bytes 4194304 | tf_op jit(solution)/shard_map/all_to_all | solution.py:279
  148.6 49.6 %all-to-all-done.4 = f32[32,128,128]{2,1,0:T(8,128)S(1)} async-done(((f32[32,128,128]{2,1,0:T(8,128)}), f32[32,128,128]{2,1,0:T(8,128)S(1)}, u32[]{:S(2)}, u32[]{:S(2)}) %all-to-all-start.4) | async-done | bytes 2097184 | tf_op jit(solution)/shard_map/all_to_all | solution.py:279
  198.3 1.0 fusion
  199.5 19.9 %all_to_all.47 = f32[8,8,32,128]{3,2,1,0:T(8,128)S(1)} all-to-all(f32[8,8,32,128]{3,2,1,0:T(8,128)S(1)} %broadcast_in_dim.130), channel_id=1, replica_groups=mesh['space'=32,'scen'=8] {'scen'}, dimensions={0} | all-to-all | bytes 2097152 | tf_op jit(solution)/shard_map/all_to_all | solution.py:292
  (276 shorter events, 31.8 us)
Async XLA Ops:
  0.6 1.3 copy-start.10
  6.8 12.7 %copy-start.29 = (s32[270]{0:T(512)S(1)}, s32[270]{0:T(512)}, u32[]{:S(2)}) copy-start(s32[270]{0:T(512)} %param.10) | copy-start | bytes 3244
  7.7 23.0 %all-to-all-start = ((f32[32,1,1152]{2,1,0:T(1,128)}), f32[32,1,1152]{2,1,0:T(1,128)S(1)}, u32[]{:S(2)}, u32[]{:S(2)}) async-start(f32[32,1,1152]{2,1,0:T(1,128)} %all_to_all.39), calls=%async_computation | async-start | bytes 294912 | tf_op jit(solution)/shard_map/all_to_all | solution.py:84
  30.7 58.8 %copy-start.13 = (s32[270]{0:T(512)}, s32[270]{0:T(512)S(1)}, u32[]{:S(2)}) copy-start(s32[270]{0:T(512)S(1)} %add_select_fusion.2) | copy-start | bytes 3244
  37.5 2.9 %copy-start.18 = (f32[12,8,1]{0,2,1:T(1,128)S(1)}, f32[12,8,1]{0,2,1:T(1,128)}, u32[]{:S(2)}) copy-start(f32[12,8,1]{0,2,1:T(1,128)} %get-tuple-element.121) | copy-start | bytes 1156
  37.5 2.9 %copy-start.19 = (f32[12,8,1]{0,2,1:T(1,128)S(1)}, f32[12,8,1]{0,2,1:T(1,128)}, u32[]{:S(2)}) copy-start(f32[12,8,1]{0,2,1:T(1,128)} %get-tuple-element.117) | copy-start | bytes 1156
  37.5 3.5 %copy-start.17 = (f32[12,8,1]{0,2,1:T(1,128)S(1)}, f32[12,8,1]{0,2,1:T(1,128)}, u32[]{:S(2)}) copy-start(f32[12,8,1]{0,2,1:T(1,128)} %get-tuple-element.116) | copy-start | bytes 1156
  37.5 3.5 %copy-start.16 = (f32[12,8,1]{0,2,1:T(1,128)S(1)}, f32[12,8,1]{0,2,1:T(1,128)}, u32[]{:S(2)}) copy-start(f32[12,8,1]{0,2,1:T(1,128)} %get-tuple-element.120) | copy-start | bytes 1156
  37.5 4.2 %copy-start.15 = (f32[12,8,1]{0,2,1:T(1,128)S(1)}, f32[12,8,1]{0,2,1:T(1,128)}, u32[]{:S(2)}) copy-start(f32[12,8,1]{0,2,1:T(1,128)} %get-tuple-element.119) | copy-start | bytes 1156
  42.1 4.8 %copy-start.1 = (f32[1,8,6,12,1]{4,1,3,2,0:T(8,128)}, f32[1,8,6,12,1]{4,1,3,2,0:T(8,128)S(1)}, u32[]{:S(2)}) copy-start(f32[1,8,6,12,1]{4,1,3,2,0:T(8,128)S(1)} %copy.406) | copy-start | bytes 6916
  47.4 1.0 copy-start.12
  47.4 1.1 copy-start.25
  47.4 1.1 copy-start.27
  48.5 11.7 %copy-start.23 = (s32[270]{0:T(512)S(1)}, s32[270]{0:T(512)}, u32[]{:S(2)}) copy-start(s32[270]{0:T(512)} %param.9) | copy-start | bytes 3244
  49.3 21.4 %all-to-all-start.1 = ((f32[32,12,96]{2,1,0:T(8,128)}), f32[32,12,96]{2,1,0:T(8,128)S(1)}, u32[]{:S(2)}, u32[]{:S(2)}) async-start(f32[32,12,96]{2,1,0:T(8,128)} %select_select_fusion), calls=%async_computation.1 | async-start | bytes 524288 | tf_op jit(solution)/shard_map/all_to_all | solution.py:157
  60.1 11.2 %collective-permute-start.1 = (f32[192,384]{1,0:T(8,128)}, f32[192,384]{1,0:T(8,128)S(1)}, u32[]{:S(2)}, u32[]{:S(2)}) collective-permute-start(f32[192,384]{1,0:T(8,128)} %pad_maximum_fusion.6), channel_id=1, source_target_pairs={{8,0},{16,8},{24,16},{32,24},{40,32},{48,40},{56,48},{64,56},{72,6... | collective-permute-start | bytes 884744 | tf_op jit(solution)/shard_map/ppermute | solution.py:13
  61.7 10.7 %collective-permute-start = (f32[192,384]{1,0:T(8,128)}, f32[192,384]{1,0:T(8,128)S(1)}, u32[]{:S(2)}, u32[]{:S(2)}) collective-permute-start(f32[192,384]{1,0:T(8,128)} %pad_maximum_fusion.5), channel_id=1, source_target_pairs={{248,0},{0,8},{8,16},{16,24},{24,32},{32,40},{40,48},{48,56},{56,6... | collective-permute-start | bytes 884744 | tf_op jit(solution)/shard_map/ppermute | solution.py:13
  73.9 1.2 copy-start
  74.0 1.2 copy-start.5
  74.0 1.2 copy-start.7
  75.9 13.6 %copy-start.21 = (f32[270]{0:T(512)S(1)}, f32[270]{0:T(512)}, u32[]{:S(2)}) copy-start(f32[270]{0:T(512)} %get-tuple-element.123) | copy-start | bytes 3244
  76.0 13.8 %copy-start.22 = (s32[270]{0:T(512)S(1)}, s32[270]{0:T(512)}, u32[]{:S(2)}) copy-start(s32[270]{0:T(512)} %compare_select_fusion) | copy-start | bytes 3244
  77.4 21.4 %all-to-all-start.2 = ((f32[32,1,864]{2,1,0:T(1,128)}), f32[32,1,864]{2,1,0:T(1,128)S(1)}, u32[]{:S(2)}, u32[]{:S(2)}) async-start(f32[32,1,864]{2,1,0:T(1,128)} %all_to_all.40), calls=%async_computation.2 | async-start | bytes 229376 | tf_op jit(solution)/shard_map/all_to_all | solution.py:84
  101.3 1.0 copy-start.3
  104.6 7.1 %copy-start.24 = (s32[270]{0:T(512)S(1)}, s32[270]{0:T(512)}, u32[]{:S(2)}) copy-start(s32[270]{0:T(512)} %param.9) | copy-start | bytes 3244
  105.8 15.1 %all-to-all-start.3 = ((f32[32,1,880]{2,1,0:T(1,128)}), f32[32,1,880]{2,1,0:T(1,128)S(1)}, u32[]{:S(2)}, u32[]{:S(2)}) async-start(f32[32,1,880]{2,1,0:T(1,128)} %all_to_all.34), calls=%async_computation.3 | async-start | bytes 229376 | tf_op jit(solution)/shard_map/all_to_all | solution.py:157
  111.5 9.9 %collective-permute-start.2 = (f32[144,384]{1,0:T(8,128)S(1)}, f32[144,384]{1,0:T(8,128)}, u32[]{:S(2)}, u32[]{:S(2)}) collective-permute-start(f32[144,384]{1,0:T(8,128)S(1)} %reshape.821), channel_id=1, source_target_pairs={{248,0},{0,8},{8,16},{16,24},{24,32},{32,40},{40,48},{48,56},{56,6... | collective-permute-start | bytes 663560 | tf_op jit(solution)/shard_map/ppermute | solution.py:13
  111.9 10.6 %collective-permute-start.3 = (f32[144,384]{1,0:T(8,128)S(1)}, f32[144,384]{1,0:T(8,128)S(1)}, u32[]{:S(2)}, u32[]{:S(2)}) collective-permute-start(f32[144,384]{1,0:T(8,128)S(1)} %reshape.827), channel_id=1, source_target_pairs={{8,0},{16,8},{24,16},{32,24},{40,32},{48,40},{56,48},{64,56},{72,6... | collective-permute-start | bytes 663560 | tf_op jit(solution)/shard_map/ppermute | solution.py:13
  124.8 1.1 copy-start.20
  127.6 4.9 %copy-start.14 = (s32[270]{0:T(512)S(1)}, s32[270]{0:T(512)}, u32[]{:S(2)}) copy-start(s32[270]{0:T(512)} %copy-done.13) | copy-start | bytes 3244
  137.1 61.2 %all-to-all-start.4 = ((f32[32,128,128]{2,1,0:T(8,128)}), f32[32,128,128]{2,1,0:T(8,128)S(1)}, u32[]{:S(2)}, u32[]{:S(2)}) async-start(f32[32,128,128]{2,1,0:T(8,128)} %bitcast.255), calls=%async_computation.4 | async-start | bytes 4194304 | tf_op jit(solution)/shard_map/all_to_all | solution.py:279
  199.3 20.0 %copy-start.9 = (f32[8,128,32]{1,2,0:T(8,128)}, f32[8,128,32]{1,2,0:T(8,128)S(1)}, u32[]{:S(2)}) copy-start(f32[8,128,32]{1,2,0:T(8,128)S(1)} %fusion) | copy-start | bytes 393220
  (7 other events, 6.0 us)
